TPU v7x, 256 devices: a whole 4x4x8 slice. The times are simulated.
256 devices in a mesh: rep: 16 (over z, core), wide: 4 (over x), narrow: 4 (over y).
Axes of the slice: x: 4, y: 4, z: 8, core: 2. Of those that a mesh axis runs over, the one named last changes fastest.
Arguments:
- tokens: bfloat16 [16384, 1536], P(('rep', 'wide'), 'narrow'), parts along dimension 0, may hold values from -6 to 6
- attn_gain: float32 [1536], replicated, may hold values from 0.1 to 1.9
- w_qkv: bfloat16 [1536, 2048], P(None, ('wide', 'narrow')), may hold values from -0.15625 to 0.15625
- w_out: bfloat16 [1536, 1536], P(None, 'narrow'), may hold values from -0.15625 to 0.15625
- prefix_cache: bfloat16 [2, 32, 8192, 2, 128], P(None, 'rep', ('wide', 'narrow')), parts along dimension 1, may hold values from -1500 to 1500
- decode_cache: bfloat16 [2, 64, 8192, 2, 128], P(None, 'rep', ('wide', 'narrow')), parts along dimension 1, may hold values from -1500 to 1500
- offsets: int32 [32], P('rep'), parts along dimension 0, may hold values from 1 to 8192, as said below
- lengths: int32 [64], P('rep'), parts along dimension 0, may hold values from 1 to 8192, as said below
Outputs:
- mixed: bfloat16 [16384, 1536], P(('rep', 'wide'), 'narrow'), parts along dimension 0
There are 16 independent parts, one for each index of `rep`. A program takes and returns all parts, laid end to end along the dimension named above; an argument that names none is the same for every part. Nothing has to cross between parts.
Inputs may be any that keep to these rules, and one draw needn't show every extreme that they name: `offsets`: exactly one prefill block has 8192 cached positions. `lengths`: exactly one decode has 8192 cached positions.
All inputs are finite; a program needn't handle non-finite values.
Results may differ from a plain program's by a relative error of at most 0.008.
Values may be sent and summed in bfloat16 or wider, within the bound.
No kernel may reach another device: no remote copies, remote signals or barrier semaphores. Data moves between devices by JAX's collectives and lax.ppermute only.
A program may use at most 320 MiB of HBM per device.

v0:
```python
import jax
import jax.numpy as jnp
from jax import lax
from jax.sharding import PartitionSpec as P

EPS = 1e-06
NEG = -1e30


def merged(part, axis, combine):
    gathered = jax.tree.map(lambda a: lax.all_gather(a, axis), part)

    def take(source):
        return jax.tree.map(lambda a: lax.dynamic_index_in_dim(a, source, 0, False), gathered)

    return lax.fori_loop(
        1, lax.axis_size(axis), lambda source, state: combine(state, take(source)), take(0)
    )


def normalize(rows, gain):
    full = rows.astype(jnp.float32)
    meansq = jnp.mean(full * full, -1, keepdims=True)
    return (full * lax.rsqrt(meansq + EPS) * gain).astype(jnp.bfloat16)


def partial_softmax(grouped_queries, keys, values, allowed, form_s, form_o):
    scores = jnp.einsum(
        form_s, grouped_queries, keys, preferred_element_type=jnp.float32
    ) * grouped_queries.shape[-1] ** (-0.5)
    masked = jnp.where(allowed, scores, NEG)
    peak = jnp.max(masked, -1)
    weights = jnp.where(allowed, jnp.exp(masked - peak[..., None]), 0.0)
    total = jnp.sum(weights, -1)
    weighted = jnp.einsum(
        form_o, weights.astype(jnp.bfloat16), values, preferred_element_type=jnp.float32
    )
    return (peak, total, weighted)


def join_parts(first, second):
    peak = jnp.maximum(first[0], second[0])
    scale_a = jnp.exp(first[0] - peak)
    scale_b = jnp.exp(second[0] - peak)
    total = first[1] * scale_a + second[1] * scale_b
    weighted = first[2] * scale_a[..., None] + second[2] * scale_b[..., None]
    return (peak, total, weighted)


def per_device(tokens, attn_gain, w_qkv, w_out, prefix_cache, decode_cache, offsets, lengths):
    n_wide = lax.axis_size("wide")
    n_narrow = lax.axis_size("narrow")
    devices = n_wide * n_narrow
    joined = lax.axis_index("wide") * n_narrow + lax.axis_index("narrow")
    block_rows = tokens.shape[0]
    every_rows = block_rows * n_wide
    own = every_rows // devices
    head_dim = prefix_cache.shape[-1]
    kv_heads = prefix_cache.shape[-2]
    n_prefix = prefix_cache.shape[1]
    n_decode = decode_cache.shape[1]
    span = (every_rows - n_decode) // n_prefix
    q_width = w_out.shape[0]
    heads = q_width // head_dim
    group = heads // kv_heads
    starts = (offsets[:, None] + jnp.arange(span, dtype=jnp.int32)[None, :]).reshape(-1)
    positions = jnp.concatenate([starts, lengths])
    row_ids = jnp.arange(every_rows, dtype=jnp.int32)
    sequence = jnp.where(
        row_ids < n_prefix * span, row_ids // span, row_ids - n_prefix * span + n_prefix
    )
    own_start = joined * own
    own_pos = lax.dynamic_slice_in_dim(positions, own_start, own)
    own_seq = lax.dynamic_slice_in_dim(sequence, own_start, own)
    features = lax.all_gather(tokens, "narrow", axis=1, tiled=True)
    everyone = lax.all_gather(features, "wide", axis=0, tiled=True)
    normed_rows = normalize(everyone, attn_gain)
    columns = jnp.dot(normed_rows, w_qkv, preferred_element_type=jnp.float32).astype(jnp.bfloat16)
    qkv_all = lax.all_gather(columns, ("wide", "narrow"), axis=1, tiled=True)
    query_matrix = qkv_all[:, :q_width].reshape(every_rows, heads, head_dim)
    own_qkv = lax.dynamic_slice_in_dim(qkv_all, own_start, own, 0)
    kv_width = kv_heads * head_dim
    own_keys = own_qkv[:, q_width : q_width + kv_width].reshape(own, kv_heads, head_dim)
    own_values = own_qkv[:, q_width + kv_width :].reshape(own, kv_heads, head_dim)
    grouped_queries = query_matrix.reshape(every_rows, kv_heads, group, head_dim)
    shard = prefix_cache.shape[2]
    cache_pos = joined * shard + jnp.arange(shard, dtype=jnp.int32)
    pieces = []
    for index in range(n_prefix):
        block = grouped_queries[index * span : (index + 1) * span]
        allowed = (cache_pos < offsets[index])[None, None, None, :]
        pieces.append(
            partial_softmax(
                block,
                prefix_cache[0, index],
                prefix_cache[1, index],
                allowed,
                "qhgd,khd->qhgk",
                "qhgk,khd->qhgd",
            )
        )
    allowed = (cache_pos[None, :] < lengths[:, None])[:, None, None, :]
    pieces.append(
        partial_softmax(
            grouped_queries[n_prefix * span :],
            decode_cache[0],
            decode_cache[1],
            allowed,
            "nhgd,nkhd->nhgk",
            "nhgk,nkhd->nhgd",
        )
    )
    cached = tuple((jnp.concatenate([piece[slot] for piece in pieces], 0) for slot in range(3)))
    allowed = ((sequence[:, None] == own_seq[None, :]) & (own_pos[None, :] <= positions[:, None]))[
        :, None, None, :
    ]
    fresh = partial_softmax(
        grouped_queries, own_keys, own_values, allowed, "rhgd,khd->rhgk", "rhgk,khd->rhgd"
    )
    local = join_parts(cached, fresh)
    peak, total, weighted = merged(local, ("wide", "narrow"), join_parts)
    attended = (weighted / total[..., None]).astype(jnp.bfloat16).reshape(every_rows, q_width)
    mine_rows = lax.dynamic_slice_in_dim(
        attended, lax.axis_index("wide") * block_rows, block_rows, 0
    )
    mixed = tokens.astype(jnp.float32) + jnp.dot(
        mine_rows, w_out, preferred_element_type=jnp.float32
    )
    return mixed.astype(jnp.bfloat16)


def solution(mesh):
    return jax.shard_map(
        per_device,
        mesh=mesh,
        in_specs=(
            P(("rep", "wide"), "narrow"),
            P(),
            P(None, ("wide", "narrow")),
            P(None, "narrow"),
            P(None, "rep", ("wide", "narrow"), None, None),
            P(None, "rep", ("wide", "narrow"), None, None),
            P("rep"),
            P("rep"),
        ),
        out_specs=P(("rep", "wide"), "narrow"),
        check_vma=False,
    )
```

profile of v0, /device:TPU:32, one launch (start us, length us, event | category | flops | bytes accessed | tf_op | source)
XLA Modules:
  0.0 1092.4 jit_solution(1917597206381465944)
XLA Ops:
  6.5 17.1 %all_gather.23 = bf16[256,1536]{1,0:T(8,128)(2,1)} all-gather(bf16[256,384]{1,0:T(8,128)(2,1)} %param.10), channel_id=1, replica_groups=mesh['rep'=16,'wide'=4,'narrow'=4] {'narrow'}, dimensions={1}, use_global_device_ids=true | all-gather | bytes 983040 | tf_op jit(solution)/shard_map/all_gather | solution.py:75
  23.7 42.9 %all-gather.5.cloned.1.call-done = bf16[1024,1536]{1,0:T(8,128)(2,1)} async-done(((bf16[256,1536]{1,0:T(8,128)(2,1)}), bf16[1024,1536]{1,0:T(8,128)(2,1)}) %all-gather.5.cloned.1.call-update) | async-done | bytes 3145744 | tf_op jit(solution)/shard_map/all_gather | solution.py:76
  69.2 3.8 fusion.43
  80.6 54.6 %all-gather.7.cloned.1.call-done = bf16[1024,2048]{1,0:T(8,128)(2,1)} async-done(((bf16[1024,128]{1,0:T(8,128)(2,1)}), bf16[1024,2048]{1,0:T(8,128)(2,1)}) %all-gather.7.cloned.1.call-update) | async-done | bytes 4194320 | tf_op jit(solution)/shard_map/all_gather | solution.py:79
  138.9 3.9 fusion.84
  144.6 3.8 slice.78
  148.3 4.7 copy.77
  173.5 7.6 fusion.15
  185.1 7.1 fusion.11
  194.0 3.6 fusion.9
  197.8 28.0 %all_gather.26 = f32[16,1024,2,6]{1,2,3,0:T(2,128)} all-gather(f32[1,1024,2,6]{1,2,3,0:T(2,128)S(1)} %copy.80), channel_id=1, replica_groups=mesh['rep'=16,'wide'=4,'narrow'=4] {'wide','narrow'}, dimensions={0}, use_global_device_ids=true | all-gather | bytes 835584 | tf_op jit(solution)/shard_map/all_gather | solution.py:11
  225.8 26.7 %all_gather.27 = f32[16,1024,2,6]{1,2,3,0:T(2,128)} all-gather(f32[1,1024,2,6]{1,2,3,0:T(2,128)S(1)} %copy.82), channel_id=1, replica_groups=mesh['rep'=16,'wide'=4,'narrow'=4] {'wide','narrow'}, dimensions={0}, use_global_device_ids=true | all-gather | bytes 835584 | tf_op jit(solution)/shard_map/all_gather | solution.py:11
  254.1 478.2 %all-gather.9.cloned.1.call-done = f32[16384,2,6,128]{3,0,2,1:T(8,128)} async-done(((f32[1024,2,6,128]{3,0,2,1:T(8,128)}), f32[16384,2,6,128]{3,0,2,1:T(8,128)}) %all-gather.9.cloned.1.call-update) | async-done | bytes 100663312 | tf_op jit(solution)/shard_map/all_gather | solution.py:11
  735.5 7.1 copy.90
  742.6 330.1 %while.19 = (s32[]{:T(128)}, f32[1024,2,6]{0,1,2:T(2,128)S(1)}, f32[1024,2,6]{0,1,2:T(2,128)S(1)}, f32[1024,2,6,128]{3,2,1,0:T(8,128)}, f32[16,1024,2,6]{1,2,3,0...) while((s32[]{:T(128)}, f32[1024,2,6]{0,1,2:T(2,128)S(1)}, ...), condition=%wide.region_10.11_spmd, body=%wide.region_9.10_spmd.sunk | while | flops 4792325 | bytes 82477248 | solution.py:16
  749.9 11.4 %fusion.98 = f32[1024,2,6,128]{3,2,1,0:T(8,128)S(1)} fusion(f32[1,1024,2,6,128]{4,1,0,3,2:T(8,128)S(1)} %constant_dynamic-slice_fusion.2, f32[1024,2,6,128]{3,2,1,0:T(8,128)S(1)} %copy-done.1, f32[1024,2,6]{2,1,0:T(2,128)S(1)} %copy.148, f32[1024,2,6]{2,1,0:T(2,128)S(1)} %copy.149), kind=kLoop, calls=%fused_computation.2.clone.1 | loop fusion | flops 4718592 | bytes 18972672 | tf_op jit(solution)/shard_map/while/body/eval_jaxpr/add | solution.py:46
  771.9 11.4 %fusion.98 = f32[1024,2,6,128]{3,2,1,0:T(8,128)S(1)} fusion(f32[1,1024,2,6,128]{4,1,0,3,2:T(8,128)S(1)} %constant_dynamic-slice_fusion.2, f32[1024,2,6,128]{3,2,1,0:T(8,128)S(1)} %copy-done.1, f32[1024,2,6]{2,1,0:T(2,128)S(1)} %copy.148, f32[1024,2,6]{2,1,0:T(2,128)S(1)} %copy.149), kind=kLoop, calls=%fused_computation.2.clone.1 | loop fusion | flops 4718592 | bytes 18972672 | tf_op jit(solution)/shard_map/while/body/eval_jaxpr/add | solution.py:46
  793.9 11.4 %fusion.98 = f32[1024,2,6,128]{3,2,1,0:T(8,128)S(1)} fusion(f32[1,1024,2,6,128]{4,1,0,3,2:T(8,128)S(1)} %constant_dynamic-slice_fusion.2, f32[1024,2,6,128]{3,2,1,0:T(8,128)S(1)} %copy-done.1, f32[1024,2,6]{2,1,0:T(2,128)S(1)} %copy.148, f32[1024,2,6]{2,1,0:T(2,128)S(1)} %copy.149), kind=kLoop, calls=%fused_computation.2.clone.1 | loop fusion | flops 4718592 | bytes 18972672 | tf_op jit(solution)/shard_map/while/body/eval_jaxpr/add | solution.py:46
  815.9 11.4 %fusion.98 = f32[1024,2,6,128]{3,2,1,0:T(8,128)S(1)} fusion(f32[1,1024,2,6,128]{4,1,0,3,2:T(8,128)S(1)} %constant_dynamic-slice_fusion.2, f32[1024,2,6,128]{3,2,1,0:T(8,128)S(1)} %copy-done.1, f32[1024,2,6]{2,1,0:T(2,128)S(1)} %copy.148, f32[1024,2,6]{2,1,0:T(2,128)S(1)} %copy.149), kind=kLoop, calls=%fused_computation.2.clone.1 | loop fusion | flops 4718592 | bytes 18972672 | tf_op jit(solution)/shard_map/while/body/eval_jaxpr/add | solution.py:46
  837.9 11.4 %fusion.98 = f32[1024,2,6,128]{3,2,1,0:T(8,128)S(1)} fusion(f32[1,1024,2,6,128]{4,1,0,3,2:T(8,128)S(1)} %constant_dynamic-slice_fusion.2, f32[1024,2,6,128]{3,2,1,0:T(8,128)S(1)} %copy-done.1, f32[1024,2,6]{2,1,0:T(2,128)S(1)} %copy.148, f32[1024,2,6]{2,1,0:T(2,128)S(1)} %copy.149), kind=kLoop, calls=%fused_computation.2.clone.1 | loop fusion | flops 4718592 | bytes 18972672 | tf_op jit(solution)/shard_map/while/body/eval_jaxpr/add | solution.py:46
  859.9 11.4 %fusion.98 = f32[1024,2,6,128]{3,2,1,0:T(8,128)S(1)} fusion(f32[1,1024,2,6,128]{4,1,0,3,2:T(8,128)S(1)} %constant_dynamic-slice_fusion.2, f32[1024,2,6,128]{3,2,1,0:T(8,128)S(1)} %copy-done.1, f32[1024,2,6]{2,1,0:T(2,128)S(1)} %copy.148, f32[1024,2,6]{2,1,0:T(2,128)S(1)} %copy.149), kind=kLoop, calls=%fused_computation.2.clone.1 | loop fusion | flops 4718592 | bytes 18972672 | tf_op jit(solution)/shard_map/while/body/eval_jaxpr/add | solution.py:46
  881.9 11.4 %fusion.98 = f32[1024,2,6,128]{3,2,1,0:T(8,128)S(1)} fusion(f32[1,1024,2,6,128]{4,1,0,3,2:T(8,128)S(1)} %constant_dynamic-slice_fusion.2, f32[1024,2,6,128]{3,2,1,0:T(8,128)S(1)} %copy-done.1, f32[1024,2,6]{2,1,0:T(2,128)S(1)} %copy.148, f32[1024,2,6]{2,1,0:T(2,128)S(1)} %copy.149), kind=kLoop, calls=%fused_computation.2.clone.1 | loop fusion | flops 4718592 | bytes 18972672 | tf_op jit(solution)/shard_map/while/body/eval_jaxpr/add | solution.py:46
  903.9 11.4 %fusion.98 = f32[1024,2,6,128]{3,2,1,0:T(8,128)S(1)} fusion(f32[1,1024,2,6,128]{4,1,0,3,2:T(8,128)S(1)} %constant_dynamic-slice_fusion.2, f32[1024,2,6,128]{3,2,1,0:T(8,128)S(1)} %copy-done.1, f32[1024,2,6]{2,1,0:T(2,128)S(1)} %copy.148, f32[1024,2,6]{2,1,0:T(2,128)S(1)} %copy.149), kind=kLoop, calls=%fused_computation.2.clone.1 | loop fusion | flops 4718592 | bytes 18972672 | tf_op jit(solution)/shard_map/while/body/eval_jaxpr/add | solution.py:46
  925.9 11.4 %fusion.98 = f32[1024,2,6,128]{3,2,1,0:T(8,128)S(1)} fusion(f32[1,1024,2,6,128]{4,1,0,3,2:T(8,128)S(1)} %constant_dynamic-slice_fusion.2, f32[1024,2,6,128]{3,2,1,0:T(8,128)S(1)} %copy-done.1, f32[1024,2,6]{2,1,0:T(2,128)S(1)} %copy.148, f32[1024,2,6]{2,1,0:T(2,128)S(1)} %copy.149), kind=kLoop, calls=%fused_computation.2.clone.1 | loop fusion | flops 4718592 | bytes 18972672 | tf_op jit(solution)/shard_map/while/body/eval_jaxpr/add | solution.py:46
  947.9 11.4 %fusion.98 = f32[1024,2,6,128]{3,2,1,0:T(8,128)S(1)} fusion(f32[1,1024,2,6,128]{4,1,0,3,2:T(8,128)S(1)} %constant_dynamic-slice_fusion.2, f32[1024,2,6,128]{3,2,1,0:T(8,128)S(1)} %copy-done.1, f32[1024,2,6]{2,1,0:T(2,128)S(1)} %copy.148, f32[1024,2,6]{2,1,0:T(2,128)S(1)} %copy.149), kind=kLoop, calls=%fused_computation.2.clone.1 | loop fusion | flops 4718592 | bytes 18972672 | tf_op jit(solution)/shard_map/while/body/eval_jaxpr/add | solution.py:46
  969.9 11.4 %fusion.98 = f32[1024,2,6,128]{3,2,1,0:T(8,128)S(1)} fusion(f32[1,1024,2,6,128]{4,1,0,3,2:T(8,128)S(1)} %constant_dynamic-slice_fusion.2, f32[1024,2,6,128]{3,2,1,0:T(8,128)S(1)} %copy-done.1, f32[1024,2,6]{2,1,0:T(2,128)S(1)} %copy.148, f32[1024,2,6]{2,1,0:T(2,128)S(1)} %copy.149), kind=kLoop, calls=%fused_computation.2.clone.1 | loop fusion | flops 4718592 | bytes 18972672 | tf_op jit(solution)/shard_map/while/body/eval_jaxpr/add | solution.py:46
  991.9 11.4 %fusion.98 = f32[1024,2,6,128]{3,2,1,0:T(8,128)S(1)} fusion(f32[1,1024,2,6,128]{4,1,0,3,2:T(8,128)S(1)} %constant_dynamic-slice_fusion.2, f32[1024,2,6,128]{3,2,1,0:T(8,128)S(1)} %copy-done.1, f32[1024,2,6]{2,1,0:T(2,128)S(1)} %copy.148, f32[1024,2,6]{2,1,0:T(2,128)S(1)} %copy.149), kind=kLoop, calls=%fused_computation.2.clone.1 | loop fusion | flops 4718592 | bytes 18972672 | tf_op jit(solution)/shard_map/while/body/eval_jaxpr/add | solution.py:46
  1014.0 11.4 %fusion.98 = f32[1024,2,6,128]{3,2,1,0:T(8,128)S(1)} fusion(f32[1,1024,2,6,128]{4,1,0,3,2:T(8,128)S(1)} %constant_dynamic-slice_fusion.2, f32[1024,2,6,128]{3,2,1,0:T(8,128)S(1)} %copy-done.1, f32[1024,2,6]{2,1,0:T(2,128)S(1)} %copy.148, f32[1024,2,6]{2,1,0:T(2,128)S(1)} %copy.149), kind=kLoop, calls=%fused_computation.2.clone.1 | loop fusion | flops 4718592 | bytes 18972672 | tf_op jit(solution)/shard_map/while/body/eval_jaxpr/add | solution.py:46
  1036.0 11.4 %fusion.98 = f32[1024,2,6,128]{3,2,1,0:T(8,128)S(1)} fusion(f32[1,1024,2,6,128]{4,1,0,3,2:T(8,128)S(1)} %constant_dynamic-slice_fusion.2, f32[1024,2,6,128]{3,2,1,0:T(8,128)S(1)} %copy-done.1, f32[1024,2,6]{2,1,0:T(2,128)S(1)} %copy.148, f32[1024,2,6]{2,1,0:T(2,128)S(1)} %copy.149), kind=kLoop, calls=%fused_computation.2.clone.1 | loop fusion | flops 4718592 | bytes 18972672 | tf_op jit(solution)/shard_map/while/body/eval_jaxpr/add | solution.py:46
  1058.0 11.4 %fusion.98 = f32[1024,2,6,128]{3,2,1,0:T(8,128)S(1)} fusion(f32[1,1024,2,6,128]{4,1,0,3,2:T(8,128)S(1)} %constant_dynamic-slice_fusion.2, f32[1024,2,6,128]{3,2,1,0:T(8,128)S(1)} %copy-done.1, f32[1024,2,6]{2,1,0:T(2,128)S(1)} %copy.148, f32[1024,2,6]{2,1,0:T(2,128)S(1)} %copy.149), kind=kLoop, calls=%fused_computation.2.clone.1 | loop fusion | flops 4718592 | bytes 18972672 | tf_op jit(solution)/shard_map/while/body/eval_jaxpr/add | solution.py:46
  1072.7 8.0 copy.93
  1080.7 3.8 divide_convert_fusion
  (197 shorter events, 206.3 us)
Async XLA Ops:
  6.5 1078.0 %copy-start = (bf16[1536,384]{1,0:T(8,128)(2,1)S(1)}, bf16[1536,384]{1,0:T(8,128)(2,1)}, u32[]{:S(2)}) copy-start(bf16[1536,384]{1,0:T(8,128)(2,1)} %param.13) | copy-start | bytes 3538948
  6.5 60.0 %all-gather.5.cloned.1.call-start = ((), (), s32[]{:S(2)}) async-start(), calls=%async_computation | async-start | bytes 3932160 | tf_op jit(solution)/shard_map/all_gather | solution.py:76
  23.6 111.6 %all-gather.7.cloned.1.call-start = ((), (), s32[]{:S(2)}) async-start(), calls=%async_computation.1 | async-start | bytes 4456448 | tf_op jit(solution)/shard_map/all_gather | solution.py:79
  69.1 3.9 copy-start.14
  69.1 4.1 copy-start.15
  69.1 6.5 copy-start.8
  73.0 659.3 %all-gather.9.cloned.1.call-start = ((), (), s32[]{:S(2)}) async-start(), calls=%async_computation.2 | async-start | bytes 106954752 | tf_op jit(solution)/shard_map/all_gather | solution.py:11
  137.2 5.6 copy-start.10
  158.6 14.8 %copy-start.6 = (f32[2,64,1024,6]{2,1,3,0:T(8,128)}, f32[2,64,1024,6]{2,1,3,0:T(8,128)S(1)}, u32[]{:S(2)}) copy-start(f32[2,64,1024,6]{2,1,3,0:T(8,128)S(1)} %get-tuple-element.246) | copy-start | bytes 9437188
  161.5 4.5 copy-start.3
  168.8 4.5 copy-start.4
  185.1 8.9 copy-start.5
  744.7 5.2 copy-start.1
  766.7 5.2 copy-start.1
  788.7 5.2 copy-start.1
  805.3 3.3 copy-start.2
  810.7 5.2 copy-start.1
  827.3 3.3 copy-start.2
  832.7 5.2 copy-start.1
  854.7 5.2 copy-start.1
  876.7 5.2 copy-start.1
  893.3 3.3 copy-start.2
  898.7 5.2 copy-start.1
  920.7 5.2 copy-start.1
  942.7 5.2 copy-start.1
  964.7 5.2 copy-start.1
  981.4 3.3 copy-start.2
  986.7 5.2 copy-start.1
  1008.8 5.2 copy-start.1
  1030.8 5.2 copy-start.1
  1052.8 5.2 copy-start.1
  1080.7 3.8 copy-start.9
  (15 other events, 46.0 us)
Sparse Core Ops, SparseCore 0:
  23.7 42.7 all-gather.4
  73.1 62.0 all-gather.6
  181.2 551.0 all-gather.8
where the time goes:
time: 1100 us; the launch traced here: 1090 us
  waiting for transfers between devices  576 us (52%)
  other arithmetic  207 us (19%)
  local copies, waits for them, and re-layouts  194 us (18%)
  blocking collectives  71.8 us (7%)
  matrix products  30.2 us (3%)
  between operations  13.4 us (1%)
    all_gather x1, waiting for transfers between devices, merged(): gathered = jax.tree.map(lambda a: lax.all_gather(a, axis), part)  478 us
    add x15, other arithmetic, join_parts(): weighted = first[2] * scale_a[..., None] + second[2] * scale_b[..., None]  171 us
    while x60, local copies, waits for them, and re-layouts  76.9 us
    all_gather x2, blocking collectives, merged(): gathered = jax.tree.map(lambda a: lax.all_gather(a, axis), part)  54.8 us
    all_gather x1, waiting for transfers between devices, per_device(): qkv_all = lax.all_gather(columns, ('wide', 'narrow'), axis=1, tiled=True)  54.6 us
    dynamic_slice x16, local copies, waits for them, and re-layouts, take(): lax.dynamic_index_in_dim(a, source, 0, False)  53.5 us
    all_gather x1, waiting for transfers between devices, per_device(): everyone = lax.all_gather(features, 'wide', axis=0, tiled=True)  42.9 us
  transfers between devices with their start and end apart: 3, of which 3 were waited for; matrix products, arithmetic and copies ran while one was open for 2% of the time, Pallas kernels for 0%

commit v1 on v0

--- a/solution.py
+++ b/solution.py
@@ -5,17 +5,6 @@
 
 EPS = 1e-06
 NEG = -1e30
-
-
-def merged(part, axis, combine):
-    gathered = jax.tree.map(lambda a: lax.all_gather(a, axis), part)
-
-    def take(source):
-        return jax.tree.map(lambda a: lax.dynamic_index_in_dim(a, source, 0, False), gathered)
-
-    return lax.fori_loop(
-        1, lax.axis_size(axis), lambda source, state: combine(state, take(source)), take(0)
-    )
 
 
 def normalize(rows, gain):
@@ -117,12 +106,16 @@
     fresh = partial_softmax(
         grouped_queries, own_keys, own_values, allowed, "rhgd,khd->rhgk", "rhgk,khd->rhgd"
     )
-    local = join_parts(cached, fresh)
-    peak, total, weighted = merged(local, ("wide", "narrow"), join_parts)
-    attended = (weighted / total[..., None]).astype(jnp.bfloat16).reshape(every_rows, q_width)
-    mine_rows = lax.dynamic_slice_in_dim(
-        attended, lax.axis_index("wide") * block_rows, block_rows, 0
+    peak, total, weighted = join_parts(cached, fresh)
+    axes = ("wide", "narrow")
+    top = lax.pmax(peak, axes)
+    scale = jnp.exp(peak - top)
+    total = lax.psum_scatter(total * scale, axes, scatter_dimension=0, tiled=True)
+    weighted = lax.psum_scatter(
+        weighted * scale[..., None], axes, scatter_dimension=0, tiled=True
     )
+    attended = (weighted / total[..., None]).astype(jnp.bfloat16).reshape(own, q_width)
+    mine_rows = lax.all_gather(attended, "narrow", axis=0, tiled=True)
     mixed = tokens.astype(jnp.float32) + jnp.dot(
         mine_rows, w_out, preferred_element_type=jnp.float32
     )

time: 1100 us -> 445 us (0.40)
  waiting for transfers between devices: 576 us -> 251 us
  other arithmetic: 207 us -> 13.7 us
  local copies, waits for them, and re-layouts: 194 us -> 28.4 us
  blocking collectives: 71.8 us -> 104 us
    all_gather x1 -> x0, waiting for transfers between devices: 478 us -> none  [merged(): gathered = jax.tree.map(lambda a: lax.all_gather(a, axis), part)]
    add x31 -> x0, other arithmetic: 185 us -> none  [the longest x15 171 us: join_parts(): weighted = first[2] * scale_a[..., None] + second[2] * scale_b[..., None]]
    while x63 -> x0, local copies, waits for them, and re-layouts: 92 us -> none
    reduce_scatter x0 -> x1, waiting for transfers between devices: none -> 88.8 us  [per_device(): lax.psum_scatter(weighted * scale[..., None], axes, scatter_dimension=0,...]
    pmax x0 -> x1, blocking collectives: none -> 72.1 us  [per_device(): top = lax.pmax(peak, axes)]
    unnamed x3 -> x5, waiting for transfers between devices: 0.05 us -> 64.7 us
    dynamic_slice x16 -> x0, local copies, waits for them, and re-layouts: 53.5 us -> none  [take(): lax.dynamic_index_in_dim(a, source, 0, False)]
    all_gather x2 -> x1, blocking collectives: 54.8 us -> 14.3 us  [per_device(): mine_rows = lax.all_gather(attended, 'narrow', axis=0, tiled=True)]
  transfers between devices with their start and end apart: 3 -> 4, of which waited for: 3 -> 4; matrix products, arithmetic and copies ran while one was open for 2% -> 4% of each run, Pallas kernels for 0% -> 0%
where the time goes in v1:
time: 445 us; the launch traced here: 444 us
  waiting for transfers between devices  251 us (56%)
  blocking collectives  104 us (23%)
  matrix products  34.3 us (8%)
  local copies, waits for them, and re-layouts  28.4 us (6%)
  other arithmetic  13.7 us (3%)
  between operations  13.4 us (3%)
    reduce_scatter x1, waiting for transfers between devices, per_device(): lax.psum_scatter(weighted * scale[..., None], axes, scatter_dimension=0,...  88.8 us
    pmax x1, blocking collectives, per_device(): top = lax.pmax(peak, axes)  72.1 us
    unnamed x5, waiting for transfers between devices  64.7 us
    all_gather x1, waiting for transfers between devices, per_device(): qkv_all = lax.all_gather(columns, ('wide', 'narrow'), axis=1, tiled=True)  54.6 us
    all_gather x1, waiting for transfers between devices, per_device(): everyone = lax.all_gather(features, 'wide', axis=0, tiled=True)  42.9 us
    dot_general x4, matrix products, partial_softmax(): jnp.einsum(form_o, weights.astype(jnp.bfloat16), values, preferred_elemen...  20.7 us
    all_gather x1, blocking collectives, per_device(): features = lax.all_gather(tokens, 'narrow', axis=1, tiled=True)  17.1 us
    all_gather x1, blocking collectives, per_device(): mine_rows = lax.all_gather(attended, 'narrow', axis=0, tiled=True)  14.3 us
  transfers between devices with their start and end apart: 4, of which 4 were waited for; matrix products, arithmetic and copies ran while one was open for 4% of the time, Pallas kernels for 0%

profile of v1, /device:TPU:32, one launch (start us, length us, event | category | flops | bytes accessed | tf_op | source)
XLA Modules:
  0.0 444.4 jit_solution(4805044523268731337)
XLA Ops:
  6.5 17.1 %all_gather.12 = bf16[256,1536]{1,0:T(8,128)(2,1)} all-gather(bf16[256,384]{1,0:T(8,128)(2,1)} %param.8), channel_id=1, replica_groups=mesh['rep'=16,'wide'=4,'narrow'=4] {'narrow'}, dimensions={1}, use_global_device_ids=true | all-gather | bytes 983040 | tf_op jit(solution)/shard_map/all_gather | solution.py:64
  23.7 42.9 %all-gather.3.cloned.1.call-done = bf16[1024,1536]{1,0:T(8,128)(2,1)} async-done(((bf16[256,1536]{1,0:T(8,128)(2,1)}), bf16[1024,1536]{1,0:T(8,128)(2,1)}) %all-gather.3.cloned.1.call-update) | async-done | bytes 3145744 | tf_op jit(solution)/shard_map/all_gather | solution.py:65
  66.6 2.6 fusion.8
  69.2 3.8 fusion.40
  74.1 1.3 fusion.64
  75.6 1.5 fusion.79
  77.1 3.5 fusion.78
  80.6 54.6 %all-gather.5.cloned.1.call-done = bf16[1024,2048]{1,0:T(8,128)(2,1)} async-done(((bf16[1024,128]{1,0:T(8,128)(2,1)}), bf16[1024,2048]{1,0:T(8,128)(2,1)}) %all-gather.5.cloned.1.call-update) | async-done | bytes 4194320 | tf_op jit(solution)/shard_map/all_gather | solution.py:68
  137.6 1.5 fusion.45
  139.2 4.0 fusion.77
  143.2 1.7 copy.41
  144.9 3.8 slice.74
  148.7 4.6 %copy.53 = bf16[1024,1536]{0,1:T(8,128)(2,1)} copy(bf16[1024,1536]{1,0:T(8,128)(2,1)} %slice.74) | data formatting | bytes 6291456 | tf_op jit(solution)/shard_map/slice | solution.py:69
  153.3 2.6 copy.45
  155.9 4.2 bitcast_reduce_fusion
  160.1 3.6 fusion.6
  163.7 4.3 fusion.31
  168.0 2.8 bitcast_reduce_fusion.1
  170.8 3.6 fusion.4
  174.4 4.5 %fusion.28 = f32[510,2,6,128]{3,0,2,1:T(8,128)} fusion(f32[2,510,6,512]{3,1,2,0:T(8,128)S(1)} %get-tuple-element.26, f32[510,2,6]{0,2,1:T(8,128)S(1)} %get-tuple-element.25, pred[512]{0:T(512)(128)(4,1)S(1)} %get-tuple-element.30, bf16[1,1,512,2,128]{4,3,2,1,0:T(2,128)(2,1)S(1)} %copy-done.4), kind=kOutput, calls=%fused_computation.37 | convolution fusion | flops 817827840 | bytes 15954336 | tf_op jit(solution)/shard_map/qhgk,khd->qhgd/dot_general | solution.py:24
  178.9 1.1 fusion.25
  180.0 1.7 copy-done.1
  181.6 0.8 fusion.26
  182.6 72.1 %pmax.7 = f32[1024,2,6]{0,2,1:T(8,128)S(1)} all-reduce(f32[1024,2,6]{0,2,1:T(8,128)S(1)} %fusion.56), channel_id=1, replica_groups=mesh['rep'=16,'wide'=4,'narrow'=4] {'wide','narrow'}, use_global_device_ids=true, to_apply=%region_5.6 | all-reduce | flops 12288 | bytes 98304 | tf_op jit(solution)/shard_map/pmax | solution.py:111
  254.8 1.0 copy.76
  255.9 10.4 %fusion.12 = f32[1024,2,6,128]{3,0,2,1:T(8,128)} fusion(f32[4,2,6,128]{3,0,2,1:T(4,128)S(1)} %copy.51, f32[510,2,6,128]{3,0,2,1:T(8,128)} %fusion.31, f32[510,2,6,128]{3,0,2,1:T(8,128)} %fusion.28, f32[1024,2,6]{0,2,1:T(8,128)S(1)} %get-tuple-element.8, f32[1024,2,6]{0,2,1:T(8,128)S(1)} %get-tuple-element.7, f32[1024,2,6]{0,2,1:T(8,128)S(1)} %get-tuple-element.6, ...), kind=kOutput, calls=%fused_computation.21 | convolution fusion | flops 214695936 | bytes 16023552 | tf_op jit(solution)/shard_map/rhgk,khd->rhgd/dot_general | solution.py:24
  266.4 64.6 %reduce-scatter.7.cloned.1.call-done = f32[64,12]{1,0:T(8,128)} async-done(((f32[1024,12]{1,0:T(8,128)}), f32[64,12]{1,0:T(8,128)}) %reduce-scatter.7.cloned.1.call-update) | async-done | bytes 3088
  331.0 0.9 reshape.202
  331.9 88.8 %reduce-scatter.5.cloned.1.call-done = f32[64,2,6,128]{3,0,2,1:T(8,128)} async-done(((f32[1024,2,6,128]{3,0,2,1:T(8,128)}), f32[64,2,6,128]{3,0,2,1:T(8,128)}) %reduce-scatter.5.cloned.1.call-update) | async-done | bytes 393232 | tf_op jit(solution)/shard_map/reduce_scatter | solution.py:114
  420.7 1.2 divide_convert_fusion
  422.3 14.3 %all_gather.15 = bf16[256,1536]{1,0:T(8,128)(2,1)S(1)} all-gather(bf16[64,1536]{1,0:T(8,128)(2,1)S(1)} %reshape.194), channel_id=1, replica_groups=mesh['rep'=16,'wide'=4,'narrow'=4] {'narrow'}, dimensions={0}, use_global_device_ids=true | all-gather | bytes 983040 | tf_op jit(solution)/shard_map/all_gather | solution.py:118
  436.6 1.3 fusion.43
  (51 shorter events, 4.5 us)
Async XLA Ops:
  6.5 430.1 %copy-start = (bf16[1536,384]{1,0:T(8,128)(2,1)S(1)}, bf16[1536,384]{1,0:T(8,128)(2,1)}, u32[]{:S(2)}) copy-start(bf16[1536,384]{1,0:T(8,128)(2,1)} %param.11) | copy-start | bytes 3538948
  6.5 60.0 %all-gather.3.cloned.1.call-start = ((), (), s32[]{:S(2)}) async-start(), calls=%async_computation.2 | async-start | bytes 3932160 | tf_op jit(solution)/shard_map/all_gather | solution.py:65
  23.6 111.6 %all-gather.5.cloned.1.call-start = ((), (), s32[]{:S(2)}) async-start(), calls=%async_computation.3 | async-start | bytes 4456448 | tf_op jit(solution)/shard_map/all_gather | solution.py:68
  69.2 3.9 copy-start.7
  69.2 4.1 copy-start.8
  69.2 6.4 %copy-start.3 = (bf16[2,2,512,2,128]{4,3,2,1,0:T(2,128)(2,1)S(1)}, bf16[2,2,512,2,128]{4,3,2,1,0:T(2,128)(2,1)}, u32[]{:S(2)}) copy-start(bf16[2,2,512,2,128]{4,3,2,1,0:T(2,128)(2,1)} %param.12) | copy-start | bytes 3145732
  73.0 258.0 %reduce-scatter.7.cloned.1.call-start = ((), (), s32[]{:S(2)}) async-start(), calls=%async_computation.5 | async-start | bytes 557056
  160.1 3.6 copy-start.5
  170.8 3.6 copy-start.4
  174.4 4.5 %copy-start.2 = (bf16[1024,1536]{0,1:T(8,128)(2,1)S(1)}, bf16[1024,1536]{0,1:T(8,128)(2,1)}, u32[]{:S(2)}) copy-start(bf16[1024,1536]{0,1:T(8,128)(2,1)} %copy.53) | copy-start | bytes 9437188
  180.0 1.7 copy-start.1
  255.9 164.8 %reduce-scatter.5.cloned.1.call-start = ((), (), s32[]{:S(2)}) async-start(), calls=%async_computation.4 | async-start | bytes 6684672 | tf_op jit(solution)/shard_map/reduce_scatter | solution.py:114
  266.4 170.2 %copy-start.6 = (bf16[256,384]{1,0:T(8,128)(2,1)S(1)}, bf16[256,384]{1,0:T(8,128)(2,1)}, u32[]{:S(2)}) copy-start(bf16[256,384]{1,0:T(8,128)(2,1)} %param.8) | copy-start | bytes 589828
Sparse Core Ops, SparseCore 0:
  23.8 42.7 all-gather.2
  73.1 62.0 all-gather.4
  256.0 74.9 reduce-scatter.6
  334.6 86.1 reduce-scatter.4

commit v2 on v1

--- a/solution.py
+++ b/solution.py
@@ -107,14 +107,30 @@
         grouped_queries, own_keys, own_values, allowed, "rhgd,khd->rhgk", "rhgk,khd->rhgd"
     )
     peak, total, weighted = join_parts(cached, fresh)
-    axes = ("wide", "narrow")
-    top = lax.pmax(peak, axes)
+    top = lax.pmax(lax.pmax(peak, "narrow"), "wide")
     scale = jnp.exp(peak - top)
-    total = lax.psum_scatter(total * scale, axes, scatter_dimension=0, tiled=True)
-    weighted = lax.psum_scatter(
-        weighted * scale[..., None], axes, scatter_dimension=0, tiled=True
+    lanes = 128
+    packed = jnp.concatenate(
+        [
+            (weighted * scale[..., None]).reshape(every_rows, q_width),
+            (total * scale).reshape(every_rows, heads),
+            jnp.zeros((every_rows, lanes - heads), jnp.float32),
+        ],
+        1,
     )
-    attended = (weighted / total[..., None]).astype(jnp.bfloat16).reshape(own, q_width)
+    width = packed.shape[1]
+    packed = (
+        packed.astype(jnp.bfloat16)
+        .reshape(n_wide, n_narrow, own, width)
+        .transpose(1, 0, 2, 3)
+        .reshape(every_rows, width)
+    )
+    packed = lax.psum_scatter(packed, "narrow", scatter_dimension=0, tiled=True)
+    packed = lax.psum_scatter(packed, "wide", scatter_dimension=0, tiled=True)
+    packed = packed.astype(jnp.float32)
+    total = packed[:, q_width : q_width + heads].reshape(own, heads, 1)
+    weighted = packed[:, :q_width].reshape(own, heads, head_dim)
+    attended = (weighted / total).astype(jnp.bfloat16).reshape(own, q_width)
     mine_rows = lax.all_gather(attended, "narrow", axis=0, tiled=True)
     mixed = tokens.astype(jnp.float32) + jnp.dot(
         mine_rows, w_out, preferred_element_type=jnp.float32

time: 445 us -> 341 us (0.77)
  waiting for transfers between devices: 251 us -> 166 us
  blocking collectives: 104 us -> 64.2 us
  local copies, waits for them, and re-layouts: 28.4 us -> 49.4 us
    unnamed x5 -> x4, waiting for transfers between devices: 64.7 us -> 0.07 us
    pmax x1 -> x2, blocking collectives: 72.1 us -> 32.8 us  [per_device(): top = lax.pmax(lax.pmax(peak, 'narrow'), 'wide')]
    reduce_scatter x1 -> x2, waiting for transfers between devices: 88.8 us -> 68.8 us  [the longest x1 41.3 us: per_device(): packed = lax.psum_scatter(packed, 'narrow', scatter_dimension=0, tiled=True)]
    concatenate x0 -> x4, local copies, waits for them, and re-layouts: none -> 14.2 us  [per_device(): jnp.concatenate([(weighted * scale[..., None]).reshape(every_rows, q_widt...]
  transfers between devices with their start and end apart: 4 -> 4, of which waited for: 4 -> 4; matrix products, arithmetic and copies ran while one was open for 4% -> 2% of each run, Pallas kernels for 0% -> 0%
where the time goes in v2:
time: 341 us; the launch traced here: 339 us
  waiting for transfers between devices  166 us (49%)
  blocking collectives  64.2 us (19%)
  local copies, waits for them, and re-layouts  49.4 us (14%)
  matrix products  32.4 us (10%)
  other arithmetic  13.6 us (4%)
  between operations  13.4 us (4%)
    all_gather x1, waiting for transfers between devices, per_device(): qkv_all = lax.all_gather(columns, ('wide', 'narrow'), axis=1, tiled=True)  54.6 us
    all_gather x1, waiting for transfers between devices, per_device(): everyone = lax.all_gather(features, 'wide', axis=0, tiled=True)  42.9 us
    reduce_scatter x1, waiting for transfers between devices, per_device(): packed = lax.psum_scatter(packed, 'narrow', scatter_dimension=0, tiled=True)  41.3 us
    pmax x2, blocking collectives, per_device(): top = lax.pmax(lax.pmax(peak, 'narrow'), 'wide')  32.8 us
    reduce_scatter x1, waiting for transfers between devices, per_device(): packed = lax.psum_scatter(packed, 'wide', scatter_dimension=0, tiled=True)  27.5 us
    dot_general x4, matrix products, partial_softmax(): jnp.einsum(form_o, weights.astype(jnp.bfloat16), values, preferred_elemen...  18.8 us
    all_gather x1, blocking collectives, per_device(): features = lax.all_gather(tokens, 'narrow', axis=1, tiled=True)  17.1 us
    all_gather x1, blocking collectives, per_device(): mine_rows = lax.all_gather(attended, 'narrow', axis=0, tiled=True)  14.3 us
  transfers between devices with their start and end apart: 4, of which 4 were waited for; matrix products, arithmetic and copies ran while one was open for 2% of the time, Pallas kernels for 0%

profile of v2, /device:TPU:32, one launch (start us, length us, event | category | flops | bytes accessed | tf_op | source)
XLA Modules:
  0.0 339.5 jit_solution(13739886081821220119)
XLA Ops:
  6.5 17.1 %all_gather.12 = bf16[256,1536]{1,0:T(8,128)(2,1)} all-gather(bf16[256,384]{1,0:T(8,128)(2,1)} %param.8), channel_id=1, replica_groups=mesh['rep'=16,'wide'=4,'narrow'=4] {'narrow'}, dimensions={1}, use_global_device_ids=true | all-gather | bytes 983040 | tf_op jit(solution)/shard_map/all_gather | solution.py:64
  23.7 42.9 %all-gather.3.cloned.1.call-done = bf16[1024,1536]{1,0:T(8,128)(2,1)} async-done(((bf16[256,1536]{1,0:T(8,128)(2,1)}), bf16[1024,1536]{1,0:T(8,128)(2,1)}) %all-gather.3.cloned.1.call-update) | async-done | bytes 3145744 | tf_op jit(solution)/shard_map/all_gather | solution.py:65
  66.6 2.6 fusion.8
  69.2 3.7 %fusion.41 = bf16[1024,128]{1,0:T(8,128)(2,1)} fusion(bf16[1536,128]{1,0:T(8,128)(2,1)S(1)} %copy-done.9, bf16[1024,1536]{1,0:T(8,128)(2,1)} %all-gather.3.cloned.1.call-done, f32[1536]{0:T(1024)S(1)} %copy-done.10, f32[1024]{0:T(1024)S(1)} %add_rsqrt_fusion), kind=kOutput, calls=%fused_computation.46 | convolution fusion | flops 409075712 | bytes 3811328 | tf_op jit(solution)/shard_map/dot_general | solution.py:67
  74.0 1.3 fusion.67
  75.5 1.6 fusion.82
  77.1 3.5 %fusion.81 = (bf16[1,4,512,2,128]{4,3,2,1,0:T(2,128)(2,1)S(1)}, bf16[1,4,512,2,128]{4,3,2,1,0:T(2,128)(2,1)}) fusion(bf16[2,4,512,2,128]{4,3,2,1,0:T(2,128)(2,1)} %param.13), kind=kLoop, calls=%fused_computation.109 | loop fusion | bytes 4194304 | tf_op jit(solution)/shard_map/slice | solution.py:95
  80.6 54.6 %all-gather.5.cloned.1.call-done = bf16[1024,2048]{1,0:T(8,128)(2,1)} async-done(((bf16[1024,128]{1,0:T(8,128)(2,1)}), bf16[1024,2048]{1,0:T(8,128)(2,1)}) %all-gather.5.cloned.1.call-update) | async-done | bytes 4194320 | tf_op jit(solution)/shard_map/all_gather | solution.py:68
  137.5 1.5 fusion.46
  139.2 4.0 %fusion.80 = (bf16[510,1536]{1,0:T(8,128)(2,1)}, bf16[510,1536]{1,0:T(8,128)(2,1)}) fusion(bf16[1024,2048]{1,0:T(8,128)(2,1)} %all-gather.5.cloned.1.call-done), kind=kLoop, calls=%fused_computation.108 | loop fusion | bytes 6266880 | tf_op jit(solution)/shard_map/slice | solution.py:79
  143.2 1.7 copy.44
  144.9 3.8 %slice.82 = bf16[1024,1536]{1,0:T(8,128)(2,1)} slice(bf16[1024,2048]{1,0:T(8,128)(2,1)} %all-gather.5.cloned.1.call-done), slice={[0:1024], [0:1536]} | slice | bytes 6291456 | tf_op jit(solution)/shard_map/slice | solution.py:69
  148.6 4.6 %copy.56 = bf16[1024,1536]{0,1:T(8,128)(2,1)} copy(bf16[1024,1536]{1,0:T(8,128)(2,1)} %slice.82) | data formatting | bytes 6291456 | tf_op jit(solution)/shard_map/slice | solution.py:69
  153.3 2.6 copy.48
  155.9 4.2 %bitcast_reduce_fusion = (f32[510,2,6]{0,2,1:T(8,128)S(1)}, f32[2,510,6,512]{3,1,2,0:T(8,128)S(1)}) fusion(pred[512]{0:T(512)(128)(4,1)S(1)} %get-tuple-element.29, bf16[510,2,6,128]{0,3,2,1:T(8,128)(2,1)} %bitcast.114, bf16[1,1,512,2,128]{4,3,2,1,0:T(2,128)(2,1)S(1)} %get-tuple-element.16), kind=kOutput, calls=%fused_computation.1 | convolution fusion | flops 811554816 | bytes 14387616 | tf_op jit(solution)/shard_map/qhgd,khd->qhgk/dot_general | solution.py:17
  160.1 3.6 %fusion.6 = f32[510,2,6]{0,2,1:T(8,128)S(1)} fusion(f32[2,510,6,512]{3,1,2,0:T(8,128)S(1)} %get-tuple-element.24, f32[510,2,6]{0,2,1:T(8,128)S(1)} %get-tuple-element.23, pred[512]{0:T(512)(128)(4,1)S(1)} %get-tuple-element.29), kind=kLoop, calls=%fused_computation.12 | loop fusion | flops 15661080 | bytes 12583232 | tf_op jit(solution)/shard_map/reduce_sum | solution.py:23
  163.7 4.2 %fusion.32 = f32[510,2,6,128]{3,0,2,1:T(8,128)} fusion(f32[2,510,6,512]{3,1,2,0:T(8,128)S(1)} %get-tuple-element.24, f32[510,2,6]{0,2,1:T(8,128)S(1)} %get-tuple-element.23, pred[512]{0:T(512)(128)(4,1)S(1)} %get-tuple-element.29, bf16[1,1,512,2,128]{4,3,2,1,0:T(2,128)(2,1)S(1)} %copy-done.5), kind=kOutput, calls=%fused_computation.39 | convolution fusion | flops 817827840 | bytes 15954336 | tf_op jit(solution)/shard_map/qhgk,khd->qhgd/dot_general | solution.py:24
  167.9 2.8 bitcast_reduce_fusion.1
  170.8 3.6 %fusion.4 = f32[510,2,6]{0,2,1:T(8,128)S(1)} fusion(f32[2,510,6,512]{3,1,2,0:T(8,128)S(1)} %get-tuple-element.26, f32[510,2,6]{0,2,1:T(8,128)S(1)} %get-tuple-element.25, pred[512]{0:T(512)(128)(4,1)S(1)} %get-tuple-element.30), kind=kLoop, calls=%fused_computation.10 | loop fusion | flops 15661080 | bytes 12583232 | tf_op jit(solution)/shard_map/reduce_sum | solution.py:23
  174.3 4.5 %fusion.29 = f32[510,2,6,128]{3,0,2,1:T(8,128)} fusion(f32[2,510,6,512]{3,1,2,0:T(8,128)S(1)} %get-tuple-element.26, f32[510,2,6]{0,2,1:T(8,128)S(1)} %get-tuple-element.25, pred[512]{0:T(512)(128)(4,1)S(1)} %get-tuple-element.30, bf16[1,1,512,2,128]{4,3,2,1,0:T(2,128)(2,1)S(1)} %copy-done.4), kind=kOutput, calls=%fused_computation.38 | convolution fusion | flops 817827840 | bytes 15954336 | tf_op jit(solution)/shard_map/qhgk,khd->qhgd/dot_general | solution.py:24
  180.0 1.7 copy-done.1
  182.6 17.2 %pmax.14 = f32[1024,2,6]{0,2,1:T(8,128)S(1)} all-reduce(f32[1024,2,6]{0,2,1:T(8,128)S(1)} %fusion.59), channel_id=1, replica_groups=mesh['rep'=16,'wide'=4,'narrow'=4] {'narrow'}, use_global_device_ids=true, to_apply=%region_5.6 | all-reduce | flops 12288 | bytes 98304 | tf_op jit(solution)/shard_map/pmax | solution.py:110
  199.7 15.6 %pmax.15 = f32[1024,2,6]{0,2,1:T(8,128)S(1)} all-reduce(f32[1024,2,6]{0,2,1:T(8,128)S(1)} %pmax.14), channel_id=1, replica_groups=mesh['rep'=16,'wide'=4,'narrow'=4] {'wide'}, use_global_device_ids=true, to_apply=%region_6.7 | all-reduce | flops 12288 | bytes 98304 | tf_op jit(solution)/shard_map/pmax | solution.py:110
  215.8 8.6 %fusion.13 = bf16[1024,2,6,128]{3,0,2,1:T(8,128)(2,1)S(1)} fusion(f32[4,2,6,128]{3,0,2,1:T(4,128)S(1)} %copy.54, f32[510,2,6,128]{3,0,2,1:T(8,128)} %fusion.32, f32[510,2,6,128]{3,0,2,1:T(8,128)} %fusion.29, f32[1024,2,6]{0,2,1:T(8,128)S(1)} %get-tuple-element.8, f32[1024,2,6]{0,2,1:T(8,128)S(1)} %get-tuple-element.7, ...), kind=kOutput, calls=%fused_computation.22 | convolution fusion | flops 216268800 | bytes 12877824 | tf_op jit(solution)/shard_map/rhgk,khd->rhgd/dot_general | solution.py:24
  224.3 4.1 %copy.61 = bf16[1024,2,6,128]{3,2,1,0:T(8,128)(2,1)} copy(bf16[1024,2,6,128]{3,0,2,1:T(8,128)(2,1)S(1)} %fusion.13) | data formatting | bytes 6291456 | tf_op jit(solution)/shard_map/convert.4
  228.4 7.5 %concatenate.34 = bf16[4,4,64,1536]{3,2,1,0:T(8,128)(2,1)} reshape(bf16[1024,2,6,128]{3,2,1,0:T(8,128)(2,1)} %copy.61) | data formatting | bytes 6291456 | tf_op jit(solution)/shard_map/concatenate | solution.py:113
  236.0 6.4 %concatenate.37 = bf16[4,4,64,1664]{3,2,1,0:T(8,128)(2,1)} concatenate(bf16[4,4,64,1536]{3,2,1,0:T(8,128)(2,1)} %concatenate.34, bf16[4,4,64,12]{3,2,1,0:T(8,128)(2,1)S(1)} %copy.63, bf16[4,4,64,116]{3,2,1,0:T(8,128)(2,1)S(1)} %broadcast_in_dim.104), dimensions={3} | concatenate | bytes 6815744 | tf_op jit(solution)/shard_map/concatenate | solution.py:113
  242.4 4.0 %copy.64 = bf16[4,4,64,1664]{3,2,1,0:T(8,128)(2,1)} copy(bf16[4,4,64,1664]{3,2,0,1:T(8,128)(2,1)} %bitcast.110) | data formatting | bytes 6815744 | tf_op jit(solution)/shard_map/transpose | solution.py:125
  246.5 41.3 %reduce-scatter.3.cloned.1.call-done = bf16[256,1664]{1,0:T(8,128)(2,1)} async-done(((bf16[1024,1664]{1,0:T(8,128)(2,1)}), bf16[256,1664]{1,0:T(8,128)(2,1)}) %reduce-scatter.3.cloned.1.call-update) | async-done | bytes 851984 | tf_op jit(solution)/shard_map/reduce_scatter | solution.py:128
  287.8 27.5 %reduce-scatter.5.cloned.1.call-done = bf16[64,1664]{1,0:T(8,128)(2,1)} async-done(((bf16[256,1664]{1,0:T(8,128)(2,1)}), bf16[64,1664]{1,0:T(8,128)(2,1)}) %reduce-scatter.5.cloned.1.call-update) | async-done | bytes 213008 | tf_op jit(solution)/shard_map/reduce_scatter | solution.py:129
  317.3 14.3 %all_gather.15 = bf16[256,1536]{1,0:T(8,128)(2,1)S(1)} all-gather(bf16[64,1536]{1,0:T(8,128)(2,1)S(1)} %fusion.47), channel_id=1, replica_groups=mesh['rep'=16,'wide'=4,'narrow'=4] {'narrow'}, dimensions={0}, use_global_device_ids=true | all-gather | bytes 983040 | tf_op jit(solution)/shard_map/all_gather | solution.py:134
  331.7 1.3 fusion.44
  (60 shorter events, 8.4 us)
Async XLA Ops:
  6.5 325.1 %copy-start = (bf16[1536,384]{1,0:T(8,128)(2,1)S(1)}, bf16[1536,384]{1,0:T(8,128)(2,1)}, u32[]{:S(2)}) copy-start(bf16[1536,384]{1,0:T(8,128)(2,1)} %param.11) | copy-start | bytes 3538948
  6.5 62.6 %copy-start.9 = (bf16[1536,128]{1,0:T(8,128)(2,1)S(1)}, bf16[1536,128]{1,0:T(8,128)(2,1)}, u32[]{:S(2)}) copy-start(bf16[1536,128]{1,0:T(8,128)(2,1)} %param.10) | copy-start | bytes 1179652
  6.5 62.7 %copy-start.10 = (f32[1536]{0:T(1024)S(1)}, f32[1536]{0:T(1024)}, u32[]{:S(2)}) copy-start(f32[1536]{0:T(1024)} %param.9) | copy-start | bytes 18436
  6.5 60.1 %all-gather.3.cloned.1.call-start = ((), (), s32[]{:S(2)}) async-start(), calls=%async_computation.2 | async-start | bytes 3932160 | tf_op jit(solution)/shard_map/all_gather | solution.py:65
  23.7 111.5 %all-gather.5.cloned.1.call-start = ((), (), s32[]{:S(2)}) async-start(), calls=%async_computation.3 | async-start | bytes 4456448 | tf_op jit(solution)/shard_map/all_gather | solution.py:68
  69.2 3.8 %copy-start.7 = (s32[2]{0:T(128)S(1)}, s32[2]{0:T(128)}, u32[]{:S(2)}) copy-start(s32[2]{0:T(128)} %param.14) | copy-start | bytes 28
  69.2 4.0 %copy-start.8 = (s32[4]{0:T(128)S(1)}, s32[4]{0:T(128)}, u32[]{:S(2)}) copy-start(s32[4]{0:T(128)} %param.15) | copy-start | bytes 52
  69.2 6.3 %copy-start.3 = (bf16[2,2,512,2,128]{4,3,2,1,0:T(2,128)(2,1)S(1)}, bf16[2,2,512,2,128]{4,3,2,1,0:T(2,128)(2,1)}, u32[]{:S(2)}) copy-start(bf16[2,2,512,2,128]{4,3,2,1,0:T(2,128)(2,1)} %param.12) | copy-start | bytes 3145732
  73.0 214.8 %reduce-scatter.3.cloned.1.call-start = ((), (), s32[]{:S(2)}) async-start(), calls=%async_computation.4 | async-start | bytes 4259840 | tf_op jit(solution)/shard_map/reduce_scatter | solution.py:128
  160.1 3.6 %copy-start.5 = (bf16[1,1,512,2,128]{4,3,2,1,0:T(2,128)(2,1)S(1)}, bf16[1,1,512,2,128]{4,3,2,1,0:T(2,128)(2,1)}, u32[]{:S(2)}) copy-start(bf16[1,1,512,2,128]{4,3,2,1,0:T(2,128)(2,1)} %get-tuple-element.18) | copy-start | bytes 786436
  170.7 3.6 %copy-start.4 = (bf16[1,1,512,2,128]{4,3,2,1,0:T(2,128)(2,1)S(1)}, bf16[1,1,512,2,128]{4,3,2,1,0:T(2,128)(2,1)}, u32[]{:S(2)}) copy-start(bf16[1,1,512,2,128]{4,3,2,1,0:T(2,128)(2,1)} %get-tuple-element.15) | copy-start | bytes 786436
  174.3 4.5 %copy-start.2 = (bf16[1024,1536]{0,1:T(8,128)(2,1)S(1)}, bf16[1024,1536]{0,1:T(8,128)(2,1)}, u32[]{:S(2)}) copy-start(bf16[1024,1536]{0,1:T(8,128)(2,1)} %copy.56) | copy-start | bytes 9437188
  180.0 1.7 copy-start.1
  246.4 85.3 %copy-start.6 = (bf16[256,384]{1,0:T(8,128)(2,1)S(1)}, bf16[256,384]{1,0:T(8,128)(2,1)}, u32[]{:S(2)}) copy-start(bf16[256,384]{1,0:T(8,128)(2,1)} %param.8) | copy-start | bytes 589828
  246.4 68.9 %reduce-scatter.5.cloned.1.call-start = ((), (), s32[]{:S(2)}) async-start(), calls=%async_computation.5 | async-start | bytes 1064960 | tf_op jit(solution)/shard_map/reduce_scatter | solution.py:129
Sparse Core Ops, SparseCore 0:
  23.8 42.7 all-gather.2
  73.1 62.0 all-gather.4
  246.5 41.1 reduce-scatter.2
  290.2 25.0 reduce-scatter.4

commit v3 on v2

--- a/solution.py
+++ b/solution.py
@@ -62,10 +62,19 @@
     own_pos = lax.dynamic_slice_in_dim(positions, own_start, own)
     own_seq = lax.dynamic_slice_in_dim(sequence, own_start, own)
     features = lax.all_gather(tokens, "narrow", axis=1, tiled=True)
-    everyone = lax.all_gather(features, "wide", axis=0, tiled=True)
-    normed_rows = normalize(everyone, attn_gain)
-    columns = jnp.dot(normed_rows, w_qkv, preferred_element_type=jnp.float32).astype(jnp.bfloat16)
-    qkv_all = lax.all_gather(columns, ("wide", "narrow"), axis=1, tiled=True)
+    normed_rows = normalize(features, attn_gain)
+    w_cols = lax.all_gather(w_qkv, "wide", axis=0, tiled=False)
+    part = jnp.einsum(
+        "rf,wfc->rwc", normed_rows, w_cols, preferred_element_type=jnp.float32
+    ).astype(jnp.bfloat16)
+    col_block = w_qkv.shape[1]
+    part = part.reshape(block_rows, n_wide * col_block)
+    gathered = lax.all_gather(part, ("wide", "narrow"), axis=0, tiled=False)
+    qkv_all = (
+        gathered.reshape(n_wide, n_narrow, block_rows, n_wide, col_block)
+        .transpose(0, 2, 3, 1, 4)
+        .reshape(every_rows, devices * col_block)
+    )
     query_matrix = qkv_all[:, :q_width].reshape(every_rows, heads, head_dim)
     own_qkv = lax.dynamic_slice_in_dim(qkv_all, own_start, own, 0)
     kv_width = kv_heads * head_dim

time: 341 us -> 315 us (0.924)
  waiting for transfers between devices: 166 us -> 136 us
  local copies, waits for them, and re-layouts: 49.4 us -> 58.3 us
    all_gather x2, waiting for transfers between devices: 97.5 us -> 66.8 us  [the longest x1 48.4 us: per_device(): gathered = lax.all_gather(part, ('wide', 'narrow'), axis=0, tiled=False)]
    reshape x2, local copies, waits for them, and re-layouts: 0.03 us -> 15 us  [per_device(): gathered.reshape(n_wide, n_narrow, block_rows, n_wide, col_block)]
    slice x2 -> x1, local copies, waits for them, and re-layouts: 8.41 us -> 2.29 us  [per_device(): query_matrix = qkv_all[:, :q_width].reshape(every_rows, heads, head_dim)]
    slice x3 -> x1, local copies, waits for them, and re-layouts: 8.25 us -> 2.18 us  [per_device(): block = grouped_queries[index * span:(index + 1) * span]]
    dot_general x1 -> x0, matrix products: 3.72 us -> none  [per_device(): jnp.dot(normed_rows, w_qkv, preferred_element_type=jnp.float32)]
    unnamed x22 -> x23, local copies, waits for them, and re-layouts: 1.7 us -> 5.39 us
  transfers between devices with their start and end apart: 4 -> 4, of which waited for: 4 -> 4; matrix products, arithmetic and copies ran while one was open for 2% -> 3% of each run, Pallas kernels for 0% -> 0%
where the time goes in v3:
time: 315 us; the launch traced here: 313 us
  waiting for transfers between devices  136 us (43%)
  blocking collectives  62.4 us (20%)
  local copies, waits for them, and re-layouts  58.3 us (19%)
  matrix products  31.1 us (10%)
  between operations  13.4 us (4%)
  other arithmetic  11.9 us (4%)
    all_gather x1, waiting for transfers between devices, per_device(): gathered = lax.all_gather(part, ('wide', 'narrow'), axis=0, tiled=False)  48.4 us
    reduce_scatter x1, waiting for transfers between devices, per_device(): packed = lax.psum_scatter(packed, 'narrow', scatter_dimension=0, tiled=True)  41.3 us
    pmax x2, blocking collectives, per_device(): top = lax.pmax(lax.pmax(peak, 'narrow'), 'wide')  33.1 us
    reduce_scatter x1, waiting for transfers between devices, per_device(): packed = lax.psum_scatter(packed, 'wide', scatter_dimension=0, tiled=True)  27.4 us
    dot_general x4, matrix products, partial_softmax(): jnp.einsum(form_o, weights.astype(jnp.bfloat16), values, preferred_elemen...  18.5 us
    all_gather x1, waiting for transfers between devices, per_device(): w_cols = lax.all_gather(w_qkv, 'wide', axis=0, tiled=False)  18.4 us
    reshape x2, local copies, waits for them, and re-layouts, per_device(): gathered.reshape(n_wide, n_narrow, block_rows, n_wide, col_block)  15 us
    all_gather x1, blocking collectives, per_device(): features = lax.all_gather(tokens, 'narrow', axis=1, tiled=True)  14.8 us
  transfers between devices with their start and end apart: 4, of which 4 were waited for; matrix products, arithmetic and copies ran while one was open for 3% of the time, Pallas kernels for 0%

profile of v3, /device:TPU:32, one launch (start us, length us, event | category | flops | bytes accessed | tf_op | source)
XLA Modules:
  0.0 313.5 jit_solution(4404078761352438681)
XLA Ops:
  7.3 14.8 %all_gather.15 = bf16[256,1536]{1,0:T(8,128)(2,1)S(1)} all-gather(bf16[256,384]{1,0:T(8,128)(2,1)} %param.8), channel_id=1, replica_groups=mesh['rep'=16,'wide'=4,'narrow'=4] {'narrow'}, dimensions={1}, use_global_device_ids=true | all-gather | bytes 983040 | tf_op jit(solution)/shard_map/all_gather | solution.py:64
  22.4 18.4 %all-gather.6.cloned.1.call-done = bf16[6144,128]{1,0:T(8,128)(2,1)} async-done(((bf16[1536,128]{1,0:T(8,128)(2,1)}), bf16[6144,128]{1,0:T(8,128)(2,1)}) %all-gather.6.cloned.1.call-update) | async-done | bytes 1572880 | tf_op jit(solution)/shard_map/all_gather | solution.py:66
  40.8 1.7 copy.42
  42.5 1.4 fusion.40
  47.9 2.7 fusion.76
  50.6 2.5 fusion.75
  53.1 48.4 %all-gather.4.cloned.1.call-done = bf16[16,256,512]{2,1,0:T(8,128)(2,1)} async-done(((bf16[1,256,512]{2,1,0:T(8,128)(2,1)}), bf16[16,256,512]{2,1,0:T(8,128)(2,1)}) %all-gather.4.cloned.1.call-update) | async-done | bytes 4194320 | tf_op jit(solution)/shard_map/all_gather | solution.py:72
  101.5 6.9 %reshape.212 = bf16[4,4,256,4,128]{4,3,2,1,0:T(4,128)(2,1)} reshape(bf16[16,256,512]{2,1,0:T(8,128)(2,1)} %all-gather.4.cloned.1.call-done) | data formatting | bytes 8388608 | tf_op jit(solution)/shard_map/reshape | solution.py:74
  108.4 8.1 %copy.44 = bf16[4,4,256,4,128]{2,0,4,1,3:T(4,128)(2,1)} copy(bf16[4,4,256,4,128]{4,3,2,1,0:T(4,128)(2,1)} %reshape.212) | data formatting | bytes 8388608 | tf_op jit(solution)/shard_map/reshape | solution.py:74
  116.5 3.2 %copy.91 = bf16[256,8,4,256]{3,1,2,0:T(8,128)(2,1)S(1)} copy(bf16[256,8,4,256]{3,2,1,0:T(4,128)(2,1)} %bitcast.137) | data formatting | bytes 8388608
  119.9 2.3 slice.82
  122.6 2.2 fusion.74
  125.0 1.7 fusion.78
  127.0 1.5 fusion.39
  128.7 4.2 %bitcast_reduce_fusion = (f32[510,2,6]{0,2,1:T(8,128)S(1)}, f32[2,510,6,512]{3,1,2,0:T(8,128)S(1)}) fusion(pred[512]{0:T(512)(128)(4,1)S(1)} %get-tuple-element.29, bf16[510,2,6,128]{0,3,2,1:T(8,128)(2,1)} %bitcast.142, bf16[1,1,512,2,128]{4,3,2,1,0:T(2,128)(2,1)} %get-tuple-element.16), kind=kOutput, calls=%fused_computation.1 | convolution fusion | flops 811554816 | bytes 14387616 | tf_op jit(solution)/shard_map/qhgd,khd->qhgk/dot_general | solution.py:17
  132.9 3.6 %fusion.6 = f32[510,2,6]{0,2,1:T(8,128)S(1)} fusion(f32[2,510,6,512]{3,1,2,0:T(8,128)S(1)} %get-tuple-element.24, f32[510,2,6]{0,2,1:T(8,128)S(1)} %get-tuple-element.23, pred[512]{0:T(512)(128)(4,1)S(1)} %get-tuple-element.29), kind=kLoop, calls=%fused_computation.12 | loop fusion | flops 15661080 | bytes 12583232 | tf_op jit(solution)/shard_map/reduce_sum | solution.py:23
  136.5 4.2 %fusion.25 = f32[510,2,6,128]{3,0,2,1:T(8,128)} fusion(f32[2,510,6,512]{3,1,2,0:T(8,128)S(1)} %get-tuple-element.24, f32[510,2,6]{0,2,1:T(8,128)S(1)} %get-tuple-element.23, pred[512]{0:T(512)(128)(4,1)S(1)} %get-tuple-element.29, bf16[1,1,512,2,128]{4,3,2,1,0:T(2,128)(2,1)S(1)} %copy-done.7), kind=kOutput, calls=%fused_computation.33 | convolution fusion | flops 817827840 | bytes 15954336 | tf_op jit(solution)/shard_map/qhgk,khd->qhgd/dot_general | solution.py:24
  140.8 2.8 bitcast_reduce_fusion.1
  143.6 3.6 %fusion.4 = f32[510,2,6]{0,2,1:T(8,128)S(1)} fusion(f32[2,510,6,512]{3,1,2,0:T(8,128)S(1)} %get-tuple-element.26, f32[510,2,6]{0,2,1:T(8,128)S(1)} %get-tuple-element.25, pred[512]{0:T(512)(128)(4,1)S(1)} %get-tuple-element.30), kind=kLoop, calls=%fused_computation.10 | loop fusion | flops 15661080 | bytes 12583232 | tf_op jit(solution)/shard_map/reduce_sum | solution.py:23
  147.2 4.2 %fusion.22 = f32[510,2,6,128]{3,0,2,1:T(8,128)} fusion(f32[2,510,6,512]{3,1,2,0:T(8,128)S(1)} %get-tuple-element.26, f32[510,2,6]{0,2,1:T(8,128)S(1)} %get-tuple-element.25, pred[512]{0:T(512)(128)(4,1)S(1)} %get-tuple-element.30, bf16[1,1,512,2,128]{4,3,2,1,0:T(2,128)(2,1)S(1)} %copy-done.6), kind=kOutput, calls=%fused_computation.32 | convolution fusion | flops 817827840 | bytes 15954336 | tf_op jit(solution)/shard_map/qhgk,khd->qhgd/dot_general | solution.py:24
  153.6 1.7 copy-done.3
  156.2 17.5 %pmax.14 = f32[1024,2,6]{0,2,1:T(8,128)S(1)} all-reduce(f32[1024,2,6]{0,2,1:T(8,128)S(1)} %fusion.56), channel_id=1, replica_groups=mesh['rep'=16,'wide'=4,'narrow'=4] {'narrow'}, use_global_device_ids=true, to_apply=%region_5.6 | all-reduce | flops 12288 | bytes 98304 | tf_op jit(solution)/shard_map/pmax | solution.py:119
  173.6 15.7 %pmax.15 = f32[1024,2,6]{0,2,1:T(8,128)S(1)} all-reduce(f32[1024,2,6]{0,2,1:T(8,128)S(1)} %pmax.14), channel_id=1, replica_groups=mesh['rep'=16,'wide'=4,'narrow'=4] {'wide'}, use_global_device_ids=true, to_apply=%region_6.7 | all-reduce | flops 12288 | bytes 98304 | tf_op jit(solution)/shard_map/pmax | solution.py:119
  189.8 8.5 %fusion.10 = bf16[1024,2,6,128]{3,0,2,1:T(8,128)(2,1)S(1)} fusion(f32[4,2,6,128]{3,0,2,1:T(4,128)S(1)} %copy.54, f32[510,2,6,128]{3,0,2,1:T(8,128)} %fusion.25, f32[510,2,6,128]{3,0,2,1:T(8,128)} %fusion.22, f32[1024,2,6]{0,2,1:T(8,128)S(1)} %get-tuple-element.8, f32[1024,2,6]{0,2,1:T(8,128)S(1)} %get-tuple-element.7, ...), kind=kOutput, calls=%fused_computation.17 | convolution fusion | flops 216268800 | bytes 12877824 | tf_op jit(solution)/shard_map/rhgk,khd->rhgd/dot_general | solution.py:24
  198.3 4.1 %copy.62 = bf16[1024,2,6,128]{3,2,1,0:T(8,128)(2,1)} copy(bf16[1024,2,6,128]{3,0,2,1:T(8,128)(2,1)S(1)} %fusion.10) | data formatting | bytes 6291456 | tf_op jit(solution)/shard_map/convert.4
  202.4 7.5 %concatenate.34 = bf16[4,4,64,1536]{3,2,1,0:T(8,128)(2,1)} reshape(bf16[1024,2,6,128]{3,2,1,0:T(8,128)(2,1)} %copy.62) | data formatting | bytes 6291456 | tf_op jit(solution)/shard_map/concatenate | solution.py:122
  210.0 6.4 %concatenate.37 = bf16[4,4,64,1664]{3,2,1,0:T(8,128)(2,1)} concatenate(bf16[4,4,64,1536]{3,2,1,0:T(8,128)(2,1)} %concatenate.34, bf16[4,4,64,12]{3,2,1,0:T(8,128)(2,1)S(1)} %copy.64, bf16[4,4,64,116]{3,2,1,0:T(8,128)(2,1)S(1)} %broadcast_in_dim.104), dimensions={3} | concatenate | bytes 6815744 | tf_op jit(solution)/shard_map/concatenate | solution.py:122
  216.4 4.0 %copy.65 = bf16[4,4,64,1664]{3,2,1,0:T(8,128)(2,1)} copy(bf16[4,4,64,1664]{3,2,0,1:T(8,128)(2,1)} %bitcast.138) | data formatting | bytes 6815744 | tf_op jit(solution)/shard_map/transpose | solution.py:134
  220.5 41.3 %reduce-scatter.3.cloned.1.call-done = bf16[256,1664]{1,0:T(8,128)(2,1)} async-done(((bf16[1024,1664]{1,0:T(8,128)(2,1)}), bf16[256,1664]{1,0:T(8,128)(2,1)}) %reduce-scatter.3.cloned.1.call-update) | async-done | bytes 851984 | tf_op jit(solution)/shard_map/reduce_scatter | solution.py:137
  261.8 27.4 %reduce-scatter.5.cloned.1.call-done = bf16[64,1664]{1,0:T(8,128)(2,1)} async-done(((bf16[256,1664]{1,0:T(8,128)(2,1)}), bf16[64,1664]{1,0:T(8,128)(2,1)}) %reduce-scatter.5.cloned.1.call-update) | async-done | bytes 213008 | tf_op jit(solution)/shard_map/reduce_scatter | solution.py:138
  291.3 14.4 %all_gather.19 = bf16[256,1536]{1,0:T(8,128)(2,1)S(1)} all-gather(bf16[64,1536]{1,0:T(8,128)(2,1)S(1)} %fusion.44), channel_id=1, replica_groups=mesh['rep'=16,'wide'=4,'narrow'=4] {'narrow'}, dimensions={0}, use_global_device_ids=true | all-gather | bytes 983040 | tf_op jit(solution)/shard_map/all_gather | solution.py:143
  305.7 1.3 fusion.37
  (61 shorter events, 11.9 us)
Async XLA Ops:
  6.5 299.2 %copy-start = (bf16[1536,384]{1,0:T(8,128)(2,1)S(1)}, bf16[1536,384]{1,0:T(8,128)(2,1)}, u32[]{:S(2)}) copy-start(bf16[1536,384]{1,0:T(8,128)(2,1)} %param.11) | copy-start | bytes 3538948
  6.5 34.2 %all-gather.6.cloned.1.call-start = ((), (), s32[]{:S(2)}) async-start(), calls=%async_computation.5 | async-start | bytes 1966080 | tf_op jit(solution)/shard_map/all_gather | solution.py:66
  7.3 94.2 %all-gather.4.cloned.1.call-start = ((), (), s32[]{:S(2)}) async-start(), calls=%async_computation.2 | async-start | bytes 4456448 | tf_op jit(solution)/shard_map/all_gather | solution.py:72
  40.8 4.1 %copy-start.9 = (s32[2]{0:T(128)S(1)}, s32[2]{0:T(128)}, u32[]{:S(2)}) copy-start(s32[2]{0:T(128)} %param.14) | copy-start | bytes 28
  40.8 4.3 %copy-start.10 = (s32[4]{0:T(128)S(1)}, s32[4]{0:T(128)}, u32[]{:S(2)}) copy-start(s32[4]{0:T(128)} %param.15) | copy-start | bytes 52
  43.9 6.7 %copy-start.4 = (bf16[2,4,512,2,128]{4,3,2,1,0:T(2,128)(2,1)S(1)}, bf16[2,4,512,2,128]{4,3,2,1,0:T(2,128)(2,1)}, u32[]{:S(2)}) copy-start(bf16[2,4,512,2,128]{4,3,2,1,0:T(2,128)(2,1)} %param.13) | copy-start | bytes 6291460
  44.8 217.0 %reduce-scatter.3.cloned.1.call-start = ((), (), s32[]{:S(2)}) async-start(), calls=%async_computation.3 | async-start | bytes 4259840 | tf_op jit(solution)/shard_map/reduce_scatter | solution.py:137
  119.7 3.0 copy-start.1
  132.9 3.6 %copy-start.7 = (bf16[1,1,512,2,128]{4,3,2,1,0:T(2,128)(2,1)S(1)}, bf16[1,1,512,2,128]{4,3,2,1,0:T(2,128)(2,1)}, u32[]{:S(2)}) copy-start(bf16[1,1,512,2,128]{4,3,2,1,0:T(2,128)(2,1)} %get-tuple-element.18) | copy-start | bytes 786436
  143.6 3.6 %copy-start.6 = (bf16[1,1,512,2,128]{4,3,2,1,0:T(2,128)(2,1)S(1)}, bf16[1,1,512,2,128]{4,3,2,1,0:T(2,128)(2,1)}, u32[]{:S(2)}) copy-start(bf16[1,1,512,2,128]{4,3,2,1,0:T(2,128)(2,1)} %get-tuple-element.15) | copy-start | bytes 786436
  147.2 5.2 %copy-start.2 = (bf16[1024,1536]{0,1:T(8,128)(2,1)S(1)}, bf16[1024,1536]{0,1:T(8,128)(2,1)}, u32[]{:S(2)}) copy-start(bf16[1024,1536]{0,1:T(8,128)(2,1)} %slice.82) | copy-start | bytes 9437188
  147.2 5.2 %copy-start.5 = (pred[1024,64]{0,1:T(8,128)(4,1)S(1)}, pred[1024,64]{0,1:T(8,128)(4,1)}, u32[]{:S(2)}) copy-start(pred[1024,64]{0,1:T(8,128)(4,1)} %compare_and_fusion) | copy-start | bytes 196612
  153.6 1.7 copy-start.3
  220.4 85.3 %copy-start.8 = (bf16[256,384]{1,0:T(8,128)(2,1)S(1)}, bf16[256,384]{1,0:T(8,128)(2,1)}, u32[]{:S(2)}) copy-start(bf16[256,384]{1,0:T(8,128)(2,1)} %param.8) | copy-start | bytes 589828
  220.4 68.8 %reduce-scatter.5.cloned.1.call-start = ((), (), s32[]{:S(2)}) async-start(), calls=%async_computation.4 | async-start | bytes 1064960 | tf_op jit(solution)/shard_map/reduce_scatter | solution.py:138
Sparse Core Ops, SparseCore 0:
  9.1 31.5 all-gather.5
  44.9 56.4 all-gather.3
  220.5 41.1 reduce-scatter.2
  264.2 25.0 reduce-scatter.4

commit v4 on v3

--- a/solution.py
+++ b/solution.py
@@ -135,8 +135,8 @@
         .reshape(every_rows, width)
     )
     packed = lax.psum_scatter(packed, "narrow", scatter_dimension=0, tiled=True)
-    packed = lax.psum_scatter(packed, "wide", scatter_dimension=0, tiled=True)
-    packed = packed.astype(jnp.float32)
+    packed = lax.all_to_all(packed.reshape(n_wide, own, width), "wide", 0, 0)
+    packed = jnp.sum(packed.astype(jnp.float32), 0)
     total = packed[:, q_width : q_width + heads].reshape(own, heads, 1)
     weighted = packed[:, :q_width].reshape(own, heads, head_dim)
     attended = (weighted / total).astype(jnp.bfloat16).reshape(own, q_width)

time: 315 us -> 302 us (0.959)
  waiting for transfers between devices: 136 us -> 109 us
  blocking collectives: 62.4 us -> 78.6 us
    reduce_scatter x1 -> x0, waiting for transfers between devices: 27.4 us -> none  [per_device(): packed = lax.psum_scatter(packed, 'wide', scatter_dimension=0, tiled=True)]
    all_to_all x0 -> x1, blocking collectives: none -> 17.2 us  [per_device(): packed = lax.all_to_all(packed.reshape(n_wide, own, width), 'wide', 0, 0)]
  transfers between devices with their start and end apart: 4 -> 3, of which waited for: 4 -> 3; matrix products, arithmetic and copies ran while one was open for 3% -> 3% of each run, Pallas kernels for 0% -> 0%
where the time goes in v4:
time: 302 us; the launch traced here: 301 us
  waiting for transfers between devices  109 us (36%)
  blocking collectives  78.6 us (26%)
  local copies, waits for them, and re-layouts  57.6 us (19%)
  matrix products  31.1 us (10%)
  between operations  13.4 us (4%)
  other arithmetic  11.1 us (4%)
    all_gather x1, waiting for transfers between devices, per_device(): gathered = lax.all_gather(part, ('wide', 'narrow'), axis=0, tiled=False)  48.4 us
    reduce_scatter x1, waiting for transfers between devices, per_device(): packed = lax.psum_scatter(packed, 'narrow', scatter_dimension=0, tiled=True)  41.3 us
    pmax x2, blocking collectives, per_device(): top = lax.pmax(lax.pmax(peak, 'narrow'), 'wide')  33.1 us
    dot_general x4, matrix products, partial_softmax(): jnp.einsum(form_o, weights.astype(jnp.bfloat16), values, preferred_elemen...  18.5 us
    all_gather x1, waiting for transfers between devices, per_device(): w_cols = lax.all_gather(w_qkv, 'wide', axis=0, tiled=False)  18.4 us
    all_to_all x1, blocking collectives, per_device(): packed = lax.all_to_all(packed.reshape(n_wide, own, width), 'wide', 0, 0)  17.2 us
    reshape x2, local copies, waits for them, and re-layouts, per_device(): gathered.reshape(n_wide, n_narrow, block_rows, n_wide, col_block)  15 us
    all_gather x1, blocking collectives, per_device(): features = lax.all_gather(tokens, 'narrow', axis=1, tiled=True)  14.8 us
  transfers between devices with their start and end apart: 3, of which 3 were waited for; matrix products, arithmetic and copies ran while one was open for 3% of the time, Pallas kernels for 0%

profile of v4, /device:TPU:32, one launch (start us, length us, event | category | flops | bytes accessed | tf_op | source)
XLA Modules:
  0.0 300.7 jit_solution(6452288516450540167)
XLA Ops:
  7.3 14.8 %all_gather.15 = bf16[256,1536]{1,0:T(8,128)(2,1)S(1)} all-gather(bf16[256,384]{1,0:T(8,128)(2,1)} %param.8), channel_id=1, replica_groups=mesh['rep'=16,'wide'=4,'narrow'=4] {'narrow'}, dimensions={1}, use_global_device_ids=true | all-gather | bytes 983040 | tf_op jit(solution)/shard_map/all_gather | solution.py:64
  22.4 18.4 %all-gather.6.cloned.1.call-done = bf16[6144,128]{1,0:T(8,128)(2,1)} async-done(((bf16[1536,128]{1,0:T(8,128)(2,1)}), bf16[6144,128]{1,0:T(8,128)(2,1)}) %all-gather.6.cloned.1.call-update) | async-done | bytes 1572880 | tf_op jit(solution)/shard_map/all_gather | solution.py:66
  40.8 1.7 copy.42
  42.5 1.4 fusion.40
  47.9 2.7 fusion.76
  50.6 2.5 fusion.75
  53.1 48.4 %all-gather.4.cloned.1.call-done = bf16[16,256,512]{2,1,0:T(8,128)(2,1)} async-done(((bf16[1,256,512]{2,1,0:T(8,128)(2,1)}), bf16[16,256,512]{2,1,0:T(8,128)(2,1)}) %all-gather.4.cloned.1.call-update) | async-done | bytes 4194320 | tf_op jit(solution)/shard_map/all_gather | solution.py:72
  101.5 6.9 %reshape.215 = bf16[4,4,256,4,128]{4,3,2,1,0:T(4,128)(2,1)} reshape(bf16[16,256,512]{2,1,0:T(8,128)(2,1)} %all-gather.4.cloned.1.call-done) | data formatting | bytes 8388608 | tf_op jit(solution)/shard_map/reshape | solution.py:74
  108.4 8.1 %copy.44 = bf16[4,4,256,4,128]{2,0,4,1,3:T(4,128)(2,1)} copy(bf16[4,4,256,4,128]{4,3,2,1,0:T(4,128)(2,1)} %reshape.215) | data formatting | bytes 8388608 | tf_op jit(solution)/shard_map/reshape | solution.py:74
  116.5 3.2 %copy.91 = bf16[256,8,4,256]{3,1,2,0:T(8,128)(2,1)S(1)} copy(bf16[256,8,4,256]{3,2,1,0:T(4,128)(2,1)} %bitcast.138) | data formatting | bytes 8388608
  119.9 2.3 slice.82
  122.6 2.2 fusion.74
  125.0 1.7 fusion.78
  127.0 1.5 fusion.39
  128.7 4.2 %bitcast_reduce_fusion = (f32[510,2,6]{0,2,1:T(8,128)S(1)}, f32[2,510,6,512]{3,1,2,0:T(8,128)S(1)}) fusion(pred[512]{0:T(512)(128)(4,1)S(1)} %get-tuple-element.29, bf16[510,2,6,128]{0,3,2,1:T(8,128)(2,1)} %bitcast.143, bf16[1,1,512,2,128]{4,3,2,1,0:T(2,128)(2,1)} %get-tuple-element.16), kind=kOutput, calls=%fused_computation.1 | convolution fusion | flops 811554816 | bytes 14387616 | tf_op jit(solution)/shard_map/qhgd,khd->qhgk/dot_general | solution.py:17
  132.9 3.6 %fusion.6 = f32[510,2,6]{0,2,1:T(8,128)S(1)} fusion(f32[2,510,6,512]{3,1,2,0:T(8,128)S(1)} %get-tuple-element.24, f32[510,2,6]{0,2,1:T(8,128)S(1)} %get-tuple-element.23, pred[512]{0:T(512)(128)(4,1)S(1)} %get-tuple-element.29), kind=kLoop, calls=%fused_computation.12 | loop fusion | flops 15661080 | bytes 12583232 | tf_op jit(solution)/shard_map/reduce_sum | solution.py:23
  136.5 4.2 %fusion.25 = f32[510,2,6,128]{3,0,2,1:T(8,128)} fusion(f32[2,510,6,512]{3,1,2,0:T(8,128)S(1)} %get-tuple-element.24, f32[510,2,6]{0,2,1:T(8,128)S(1)} %get-tuple-element.23, pred[512]{0:T(512)(128)(4,1)S(1)} %get-tuple-element.29, bf16[1,1,512,2,128]{4,3,2,1,0:T(2,128)(2,1)S(1)} %copy-done.7), kind=kOutput, calls=%fused_computation.33 | convolution fusion | flops 817827840 | bytes 15954336 | tf_op jit(solution)/shard_map/qhgk,khd->qhgd/dot_general | solution.py:24
  140.8 2.8 bitcast_reduce_fusion.1
  143.6 3.6 %fusion.4 = f32[510,2,6]{0,2,1:T(8,128)S(1)} fusion(f32[2,510,6,512]{3,1,2,0:T(8,128)S(1)} %get-tuple-element.26, f32[510,2,6]{0,2,1:T(8,128)S(1)} %get-tuple-element.25, pred[512]{0:T(512)(128)(4,1)S(1)} %get-tuple-element.30), kind=kLoop, calls=%fused_computation.10 | loop fusion | flops 15661080 | bytes 12583232 | tf_op jit(solution)/shard_map/reduce_sum | solution.py:23
  147.2 4.2 %fusion.22 = f32[510,2,6,128]{3,0,2,1:T(8,128)} fusion(f32[2,510,6,512]{3,1,2,0:T(8,128)S(1)} %get-tuple-element.26, f32[510,2,6]{0,2,1:T(8,128)S(1)} %get-tuple-element.25, pred[512]{0:T(512)(128)(4,1)S(1)} %get-tuple-element.30, bf16[1,1,512,2,128]{4,3,2,1,0:T(2,128)(2,1)S(1)} %copy-done.6), kind=kOutput, calls=%fused_computation.32 | convolution fusion | flops 817827840 | bytes 15954336 | tf_op jit(solution)/shard_map/qhgk,khd->qhgd/dot_general | solution.py:24
  153.6 1.7 copy-done.3
  156.2 17.5 %pmax.14 = f32[1024,2,6]{0,2,1:T(8,128)S(1)} all-reduce(f32[1024,2,6]{0,2,1:T(8,128)S(1)} %fusion.56), channel_id=1, replica_groups=mesh['rep'=16,'wide'=4,'narrow'=4] {'narrow'}, use_global_device_ids=true, to_apply=%region_5.6 | all-reduce | flops 12288 | bytes 98304 | tf_op jit(solution)/shard_map/pmax | solution.py:119
  173.6 15.7 %pmax.15 = f32[1024,2,6]{0,2,1:T(8,128)S(1)} all-reduce(f32[1024,2,6]{0,2,1:T(8,128)S(1)} %pmax.14), channel_id=1, replica_groups=mesh['rep'=16,'wide'=4,'narrow'=4] {'wide'}, use_global_device_ids=true, to_apply=%region_6.7 | all-reduce | flops 12288 | bytes 98304 | tf_op jit(solution)/shard_map/pmax | solution.py:119
  189.8 8.5 %fusion.10 = bf16[1024,2,6,128]{3,0,2,1:T(8,128)(2,1)S(1)} fusion(f32[4,2,6,128]{3,0,2,1:T(4,128)S(1)} %copy.54, f32[510,2,6,128]{3,0,2,1:T(8,128)} %fusion.25, f32[510,2,6,128]{3,0,2,1:T(8,128)} %fusion.22, f32[1024,2,6]{0,2,1:T(8,128)S(1)} %get-tuple-element.8, f32[1024,2,6]{0,2,1:T(8,128)S(1)} %get-tuple-element.7, ...), kind=kOutput, calls=%fused_computation.17 | convolution fusion | flops 216268800 | bytes 12877824 | tf_op jit(solution)/shard_map/rhgk,khd->rhgd/dot_general | solution.py:24
  198.3 4.1 %copy.62 = bf16[1024,2,6,128]{3,2,1,0:T(8,128)(2,1)} copy(bf16[1024,2,6,128]{3,0,2,1:T(8,128)(2,1)S(1)} %fusion.10) | data formatting | bytes 6291456 | tf_op jit(solution)/shard_map/convert.4
  202.4 7.5 %concatenate.34 = bf16[4,4,64,1536]{3,2,1,0:T(8,128)(2,1)} reshape(bf16[1024,2,6,128]{3,2,1,0:T(8,128)(2,1)} %copy.62) | data formatting | bytes 6291456 | tf_op jit(solution)/shard_map/concatenate | solution.py:122
  210.0 6.4 %concatenate.37 = bf16[4,4,64,1664]{3,2,1,0:T(8,128)(2,1)} concatenate(bf16[4,4,64,1536]{3,2,1,0:T(8,128)(2,1)} %concatenate.34, bf16[4,4,64,12]{3,2,1,0:T(8,128)(2,1)S(1)} %copy.64, bf16[4,4,64,116]{3,2,1,0:T(8,128)(2,1)S(1)} %broadcast_in_dim.104), dimensions={3} | concatenate | bytes 6815744 | tf_op jit(solution)/shard_map/concatenate | solution.py:122
  216.4 4.0 %copy.65 = bf16[4,4,64,1664]{3,2,1,0:T(8,128)(2,1)} copy(bf16[4,4,64,1664]{3,2,0,1:T(8,128)(2,1)} %bitcast.139) | data formatting | bytes 6815744 | tf_op jit(solution)/shard_map/transpose | solution.py:134
  220.4 41.3 %reduce-scatter.2.cloned.1.call-done = bf16[256,1664]{1,0:T(8,128)(2,1)} async-done(((bf16[1024,1664]{1,0:T(8,128)(2,1)}), bf16[256,1664]{1,0:T(8,128)(2,1)}) %reduce-scatter.2.cloned.1.call-update) | async-done | bytes 851984 | tf_op jit(solution)/shard_map/reduce_scatter | solution.py:137
  261.8 17.2 %all_to_all.5 = bf16[4,64,1664]{2,1,0:T(8,128)(2,1)S(1)} all-to-all(bf16[4,64,1664]{2,1,0:T(8,128)(2,1)} %bitcast.149), channel_id=1, replica_groups=mesh['rep'=16,'wide'=4,'narrow'=4] {'wide'}, dimensions={0} | all-to-all | bytes 1703936 | tf_op jit(solution)/shard_map/all_to_all | solution.py:138
  279.4 13.5 %all_gather.19 = bf16[256,1536]{1,0:T(8,128)(2,1)S(1)} all-gather(bf16[64,1536]{1,0:T(8,128)(2,1)S(1)} %fusion.44), channel_id=1, replica_groups=mesh['rep'=16,'wide'=4,'narrow'=4] {'narrow'}, dimensions={0}, use_global_device_ids=true | all-gather | bytes 983040 | tf_op jit(solution)/shard_map/all_gather | solution.py:143
  293.0 1.3 fusion.37
  (59 shorter events, 10.3 us)
Async XLA Ops:
  6.5 286.4 %copy-start = (bf16[1536,384]{1,0:T(8,128)(2,1)S(1)}, bf16[1536,384]{1,0:T(8,128)(2,1)}, u32[]{:S(2)}) copy-start(bf16[1536,384]{1,0:T(8,128)(2,1)} %param.11) | copy-start | bytes 3538948
  6.5 34.2 %all-gather.6.cloned.1.call-start = ((), (), s32[]{:S(2)}) async-start(), calls=%async_computation.4 | async-start | bytes 1966080 | tf_op jit(solution)/shard_map/all_gather | solution.py:66
  7.3 94.2 %all-gather.4.cloned.1.call-start = ((), (), s32[]{:S(2)}) async-start(), calls=%async_computation.2 | async-start | bytes 4456448 | tf_op jit(solution)/shard_map/all_gather | solution.py:72
  42.5 2.4 copy-start.9
  42.5 2.5 copy-start.10
  43.9 6.7 %copy-start.4 = (bf16[2,4,512,2,128]{4,3,2,1,0:T(2,128)(2,1)S(1)}, bf16[2,4,512,2,128]{4,3,2,1,0:T(2,128)(2,1)}, u32[]{:S(2)}) copy-start(bf16[2,4,512,2,128]{4,3,2,1,0:T(2,128)(2,1)} %param.13) | copy-start | bytes 6291460
  44.8 217.0 %reduce-scatter.2.cloned.1.call-start = ((), (), s32[]{:S(2)}) async-start(), calls=%async_computation.3 | async-start | bytes 4259840 | tf_op jit(solution)/shard_map/reduce_scatter | solution.py:137
  119.7 3.0 copy-start.1
  132.9 3.6 %copy-start.7 = (bf16[1,1,512,2,128]{4,3,2,1,0:T(2,128)(2,1)S(1)}, bf16[1,1,512,2,128]{4,3,2,1,0:T(2,128)(2,1)}, u32[]{:S(2)}) copy-start(bf16[1,1,512,2,128]{4,3,2,1,0:T(2,128)(2,1)} %get-tuple-element.18) | copy-start | bytes 786436
  143.6 3.6 %copy-start.6 = (bf16[1,1,512,2,128]{4,3,2,1,0:T(2,128)(2,1)S(1)}, bf16[1,1,512,2,128]{4,3,2,1,0:T(2,128)(2,1)}, u32[]{:S(2)}) copy-start(bf16[1,1,512,2,128]{4,3,2,1,0:T(2,128)(2,1)} %get-tuple-element.15) | copy-start | bytes 786436
  147.2 5.2 %copy-start.2 = (bf16[1024,1536]{0,1:T(8,128)(2,1)S(1)}, bf16[1024,1536]{0,1:T(8,128)(2,1)}, u32[]{:S(2)}) copy-start(bf16[1024,1536]{0,1:T(8,128)(2,1)} %slice.82) | copy-start | bytes 9437188
  147.2 5.2 %copy-start.5 = (pred[1024,64]{0,1:T(8,128)(4,1)S(1)}, pred[1024,64]{0,1:T(8,128)(4,1)}, u32[]{:S(2)}) copy-start(pred[1024,64]{0,1:T(8,128)(4,1)} %compare_and_fusion) | copy-start | bytes 196612
  153.6 1.7 copy-start.3
  220.4 72.6 %copy-start.8 = (bf16[256,384]{1,0:T(8,128)(2,1)S(1)}, bf16[256,384]{1,0:T(8,128)(2,1)}, u32[]{:S(2)}) copy-start(bf16[256,384]{1,0:T(8,128)(2,1)} %param.8) | copy-start | bytes 589828
Sparse Core Ops, SparseCore 0:
  9.1 31.5 all-gather.5
  44.9 56.4 all-gather.3
  220.5 41.1 reduce-scatter.1

commit v5 on v4

--- a/solution.py
+++ b/solution.py
@@ -116,14 +116,24 @@
         grouped_queries, own_keys, own_values, allowed, "rhgd,khd->rhgk", "rhgk,khd->rhgd"
     )
     peak, total, weighted = join_parts(cached, fresh)
-    top = lax.pmax(lax.pmax(peak, "narrow"), "wide")
-    scale = jnp.exp(peak - top)
+    top = lax.pmax(peak, "narrow")
+    hi = lax.reduce_precision(top, exponent_bits=8, mantissa_bits=7)
+    lo = lax.reduce_precision(top - hi, exponent_bits=8, mantissa_bits=7)
+    shift = hi + lo
+    scale = jnp.exp(jnp.minimum(peak - shift, 80.0))
+    first = lax.axis_index("narrow") == 0
+
+    def kept(a):
+        return jnp.where(first, a, jnp.zeros_like(a)).reshape(every_rows, heads)
+
     lanes = 128
     packed = jnp.concatenate(
         [
             (weighted * scale[..., None]).reshape(every_rows, q_width),
             (total * scale).reshape(every_rows, heads),
-            jnp.zeros((every_rows, lanes - heads), jnp.float32),
+            kept(hi),
+            kept(lo),
+            jnp.zeros((every_rows, lanes - 3 * heads), jnp.float32),
         ],
         1,
     )
@@ -136,9 +146,16 @@
     )
     packed = lax.psum_scatter(packed, "narrow", scatter_dimension=0, tiled=True)
     packed = lax.all_to_all(packed.reshape(n_wide, own, width), "wide", 0, 0)
-    packed = jnp.sum(packed.astype(jnp.float32), 0)
-    total = packed[:, q_width : q_width + heads].reshape(own, heads, 1)
-    weighted = packed[:, :q_width].reshape(own, heads, head_dim)
+    packed = packed.astype(jnp.float32)
+    part_shift = (
+        packed[:, :, q_width + heads : q_width + 2 * heads]
+        + packed[:, :, q_width + 2 * heads : q_width + 3 * heads]
+    )
+    part_scale = jnp.exp(part_shift - jnp.max(part_shift, 0)[None])
+    total = jnp.sum(packed[:, :, q_width : q_width + heads] * part_scale, 0)
+    total = total.reshape(own, heads, 1)
+    weighted = packed[:, :, :q_width].reshape(n_wide, own, heads, head_dim)
+    weighted = jnp.sum(weighted * part_scale[..., None], 0)
     attended = (weighted / total).astype(jnp.bfloat16).reshape(own, q_width)
     mine_rows = lax.all_gather(attended, "narrow", axis=0, tiled=True)
     mixed = tokens.astype(jnp.float32) + jnp.dot(

time: 302 us -> 294 us (0.974)
  blocking collectives: 78.6 us -> 63 us
  local copies, waits for them, and re-layouts: 57.6 us -> 62.8 us
    pmax x2 -> x1, blocking collectives: 33.1 us -> 17.5 us  [per_device(): top = lax.pmax(peak, 'narrow')]
    mul x0 -> x2, local copies, waits for them, and re-layouts: none -> 4.55 us  [per_device(): weighted = jnp.sum(weighted * part_scale[..., None], 0)]
    concatenate x4 -> x8, local copies, waits for them, and re-layouts: 14.2 us -> 14.9 us  [per_device(): jnp.concatenate([(weighted * scale[..., None]).reshape(every_rows, q_widt...]
where the time goes in v5:
time: 294 us; the launch traced here: 292 us
  waiting for transfers between devices  109 us (37%)
  blocking collectives  63 us (21%)
  local copies, waits for them, and re-layouts  62.8 us (21%)
  matrix products  31.1 us (11%)
  between operations  13.4 us (5%)
  other arithmetic  13 us (4%)
    all_gather x1, waiting for transfers between devices, per_device(): gathered = lax.all_gather(part, ('wide', 'narrow'), axis=0, tiled=False)  48.4 us
    reduce_scatter x1, waiting for transfers between devices, per_device(): packed = lax.psum_scatter(packed, 'narrow', scatter_dimension=0, tiled=True)  41.4 us
    dot_general x4, matrix products, partial_softmax(): jnp.einsum(form_o, weights.astype(jnp.bfloat16), values, preferred_elemen...  18.5 us
    all_gather x1, waiting for transfers between devices, per_device(): w_cols = lax.all_gather(w_qkv, 'wide', axis=0, tiled=False)  18.4 us
    pmax x1, blocking collectives, per_device(): top = lax.pmax(peak, 'narrow')  17.5 us
    all_to_all x1, blocking collectives, per_device(): packed = lax.all_to_all(packed.reshape(n_wide, own, width), 'wide', 0, 0)  17.2 us
    reshape x2, local copies, waits for them, and re-layouts, per_device(): gathered.reshape(n_wide, n_narrow, block_rows, n_wide, col_block)  15 us
    concatenate x8, local copies, waits for them, and re-layouts, per_device(): jnp.concatenate([(weighted * scale[..., None]).reshape(every_rows, q_widt...  14.9 us
  transfers between devices with their start and end apart: 3, of which 3 were waited for; matrix products, arithmetic and copies ran while one was open for 3% of the time, Pallas kernels for 0%

profile of v5, /device:TPU:32, one launch (start us, length us, event | category | flops | bytes accessed | tf_op | source)
XLA Modules:
  0.0 292.2 jit_solution(13812464199082671373)
XLA Ops:
  7.3 14.8 %all_gather.15 = bf16[256,1536]{1,0:T(8,128)(2,1)S(1)} all-gather(bf16[256,384]{1,0:T(8,128)(2,1)} %param.8), channel_id=1, replica_groups=mesh['rep'=16,'wide'=4,'narrow'=4] {'narrow'}, dimensions={1}, use_global_device_ids=true | all-gather | bytes 983040 | tf_op jit(solution)/shard_map/all_gather | solution.py:64
  22.4 18.4 %all-gather.6.cloned.1.call-done = bf16[6144,128]{1,0:T(8,128)(2,1)} async-done(((bf16[1536,128]{1,0:T(8,128)(2,1)}), bf16[6144,128]{1,0:T(8,128)(2,1)}) %all-gather.6.cloned.1.call-update) | async-done | bytes 1572880 | tf_op jit(solution)/shard_map/all_gather | solution.py:66
  40.8 1.7 copy.46
  47.9 2.7 fusion.87
  50.6 2.5 fusion.86
  53.1 48.4 %all-gather.4.cloned.1.call-done = bf16[16,256,512]{2,1,0:T(8,128)(2,1)} async-done(((bf16[1,256,512]{2,1,0:T(8,128)(2,1)}), bf16[16,256,512]{2,1,0:T(8,128)(2,1)}) %all-gather.4.cloned.1.call-update) | async-done | bytes 4194320 | tf_op jit(solution)/shard_map/all_gather | solution.py:72
  101.5 6.9 %reshape.229 = bf16[4,4,256,4,128]{4,3,2,1,0:T(4,128)(2,1)} reshape(bf16[16,256,512]{2,1,0:T(8,128)(2,1)} %all-gather.4.cloned.1.call-done) | data formatting | bytes 8388608 | tf_op jit(solution)/shard_map/reshape | solution.py:74
  108.4 8.1 %copy.48 = bf16[4,4,256,4,128]{2,0,4,1,3:T(4,128)(2,1)} copy(bf16[4,4,256,4,128]{4,3,2,1,0:T(4,128)(2,1)} %reshape.229) | data formatting | bytes 8388608 | tf_op jit(solution)/shard_map/reshape | solution.py:74
  116.5 3.2 %copy.97 = bf16[256,8,4,256]{3,1,2,0:T(8,128)(2,1)S(1)} copy(bf16[256,8,4,256]{3,2,1,0:T(4,128)(2,1)} %bitcast.142) | data formatting | bytes 8388608
  119.9 2.3 slice.90
  122.6 2.2 fusion.85
  125.0 1.7 fusion.89
  127.0 1.5 fusion.40
  128.7 4.2 %bitcast_reduce_fusion = (f32[510,2,6]{0,2,1:T(8,128)S(1)}, f32[2,510,6,512]{3,1,2,0:T(8,128)S(1)}) fusion(pred[512]{0:T(512)(128)(4,1)S(1)} %get-tuple-element.37, bf16[510,2,6,128]{0,3,2,1:T(8,128)(2,1)} %bitcast.147, bf16[1,1,512,2,128]{4,3,2,1,0:T(2,128)(2,1)} %get-tuple-element.18), kind=kOutput, calls=%fused_computation.1 | convolution fusion | flops 811554816 | bytes 14387616 | tf_op jit(solution)/shard_map/qhgd,khd->qhgk/dot_general | solution.py:17
  132.9 3.6 %fusion.6 = f32[510,2,6]{0,2,1:T(8,128)S(1)} fusion(f32[2,510,6,512]{3,1,2,0:T(8,128)S(1)} %get-tuple-element.32, f32[510,2,6]{0,2,1:T(8,128)S(1)} %get-tuple-element.31, pred[512]{0:T(512)(128)(4,1)S(1)} %get-tuple-element.37), kind=kLoop, calls=%fused_computation.12 | loop fusion | flops 15661080 | bytes 12583232 | tf_op jit(solution)/shard_map/reduce_sum | solution.py:23
  136.5 4.2 %fusion.25 = f32[510,2,6,128]{3,0,2,1:T(8,128)} fusion(f32[2,510,6,512]{3,1,2,0:T(8,128)S(1)} %get-tuple-element.32, f32[510,2,6]{0,2,1:T(8,128)S(1)} %get-tuple-element.31, pred[512]{0:T(512)(128)(4,1)S(1)} %get-tuple-element.37, bf16[1,1,512,2,128]{4,3,2,1,0:T(2,128)(2,1)S(1)} %copy-done.7), kind=kOutput, calls=%fused_computation.33 | convolution fusion | flops 817827840 | bytes 15954336 | tf_op jit(solution)/shard_map/qhgk,khd->qhgd/dot_general | solution.py:24
  140.8 2.8 bitcast_reduce_fusion.1
  143.6 3.6 %fusion.4 = f32[510,2,6]{0,2,1:T(8,128)S(1)} fusion(f32[2,510,6,512]{3,1,2,0:T(8,128)S(1)} %get-tuple-element.34, f32[510,2,6]{0,2,1:T(8,128)S(1)} %get-tuple-element.33, pred[512]{0:T(512)(128)(4,1)S(1)} %get-tuple-element.38), kind=kLoop, calls=%fused_computation.10 | loop fusion | flops 15661080 | bytes 12583232 | tf_op jit(solution)/shard_map/reduce_sum | solution.py:23
  147.2 4.2 %fusion.22 = f32[510,2,6,128]{3,0,2,1:T(8,128)} fusion(f32[2,510,6,512]{3,1,2,0:T(8,128)S(1)} %get-tuple-element.34, f32[510,2,6]{0,2,1:T(8,128)S(1)} %get-tuple-element.33, pred[512]{0:T(512)(128)(4,1)S(1)} %get-tuple-element.38, bf16[1,1,512,2,128]{4,3,2,1,0:T(2,128)(2,1)S(1)} %copy-done.6), kind=kOutput, calls=%fused_computation.32 | convolution fusion | flops 817827840 | bytes 15954336 | tf_op jit(solution)/shard_map/qhgk,khd->qhgd/dot_general | solution.py:24
  153.6 1.7 copy-done.3
  156.2 17.5 %pmax.7 = f32[1024,2,6]{0,2,1:T(8,128)S(1)} all-reduce(f32[1024,2,6]{0,2,1:T(8,128)S(1)} %fusion.66), channel_id=1, replica_groups=mesh['rep'=16,'wide'=4,'narrow'=4] {'narrow'}, use_global_device_ids=true, to_apply=%region_5.6 | all-reduce | flops 12288 | bytes 98304 | tf_op jit(solution)/shard_map/pmax | solution.py:119
  174.7 8.5 %fusion.10 = bf16[1024,2,6,128]{3,0,2,1:T(8,128)(2,1)S(1)} fusion(f32[4,2,6,128]{3,0,2,1:T(4,128)S(1)} %copy.58, f32[510,2,6,128]{3,0,2,1:T(8,128)} %fusion.25, f32[510,2,6,128]{3,0,2,1:T(8,128)} %fusion.22, f32[1024,2,6]{0,2,1:T(8,128)S(1)} %get-tuple-element.24, f32[1024,2,6]{0,2,1:T(8,128)S(1)} %get-tuple-element.25, ...), kind=kOutput, calls=%fused_computation.17 | convolution fusion | flops 216268800 | bytes 12877824 | tf_op jit(solution)/shard_map/rhgk,khd->rhgd/dot_general | solution.py:24
  183.3 4.1 %copy.66 = bf16[1024,2,6,128]{3,2,1,0:T(8,128)(2,1)} copy(bf16[1024,2,6,128]{3,0,2,1:T(8,128)(2,1)S(1)} %fusion.10) | data formatting | bytes 6291456 | tf_op jit(solution)/shard_map/convert.8
  187.4 7.5 %concatenate.38 = bf16[4,4,64,1536]{3,2,1,0:T(8,128)(2,1)} reshape(bf16[1024,2,6,128]{3,2,1,0:T(8,128)(2,1)} %copy.66) | data formatting | bytes 6291456 | tf_op jit(solution)/shard_map/concatenate | solution.py:130
  195.0 6.4 %concatenate.43 = bf16[4,4,64,1664]{3,2,1,0:T(8,128)(2,1)} concatenate(bf16[4,4,64,1536]{3,2,1,0:T(8,128)(2,1)} %concatenate.38, bf16[4,4,64,12]{3,2,1,0:T(8,128)(2,1)S(1)} %copy.68, bf16[4,4,64,12]{3,2,1,0:T(8,128)(2,1)S(1)} %copy.69, bf16[4,4,64,12]{3,2,1,0:T(8,128)(2,1)S(1)} %copy.70, bf16[4,4,64,92]{3,2,1,0:T(8,128)(2,1)S(1)} %broadcast_in_dim.106), dimensions={3} | concatenate | bytes 6815744 | tf_op jit(solution)/shard_map/concatenate | solution.py:130
  201.4 4.0 %copy.71 = bf16[4,4,64,1664]{3,2,1,0:T(8,128)(2,1)} copy(bf16[4,4,64,1664]{3,2,0,1:T(8,128)(2,1)} %bitcast.144) | data formatting | bytes 6815744 | tf_op jit(solution)/shard_map/transpose | solution.py:144
  205.4 41.4 %reduce-scatter.2.cloned.1.call-done = bf16[256,1664]{1,0:T(8,128)(2,1)} async-done(((bf16[1024,1664]{1,0:T(8,128)(2,1)}), bf16[256,1664]{1,0:T(8,128)(2,1)}) %reduce-scatter.2.cloned.1.call-update) | async-done | bytes 851984 | tf_op jit(solution)/shard_map/reduce_scatter | solution.py:147
  246.8 17.2 %all_to_all.5 = bf16[4,64,1664]{2,1,0:T(8,128)(2,1)S(1)} all-to-all(bf16[4,64,1664]{2,1,0:T(8,128)(2,1)} %bitcast.153), channel_id=1, replica_groups=mesh['rep'=16,'wide'=4,'narrow'=4] {'wide'}, dimensions={0} | all-to-all | bytes 1703936 | tf_op jit(solution)/shard_map/all_to_all | solution.py:148
  264.4 2.0 mul.122
  266.3 2.6 mul.123
  268.9 1.7 fusion.32
  271.0 13.5 %all_gather.19 = bf16[256,1536]{1,0:T(8,128)(2,1)S(1)} all-gather(bf16[64,1536]{1,0:T(8,128)(2,1)S(1)} %fusion.45), channel_id=1, replica_groups=mesh['rep'=16,'wide'=4,'narrow'=4] {'narrow'}, dimensions={0}, use_global_device_ids=true | all-gather | bytes 983040 | tf_op jit(solution)/shard_map/all_gather | solution.py:160
  (66 shorter events, 13.8 us)
Async XLA Ops:
  6.5 277.9 %copy-start = (bf16[1536,384]{1,0:T(8,128)(2,1)S(1)}, bf16[1536,384]{1,0:T(8,128)(2,1)}, u32[]{:S(2)}) copy-start(bf16[1536,384]{1,0:T(8,128)(2,1)} %param.11) | copy-start | bytes 3538948
  6.5 34.2 %all-gather.6.cloned.1.call-start = ((), (), s32[]{:S(2)}) async-start(), calls=%async_computation.4 | async-start | bytes 1966080 | tf_op jit(solution)/shard_map/all_gather | solution.py:66
  7.3 94.2 %all-gather.4.cloned.1.call-start = ((), (), s32[]{:S(2)}) async-start(), calls=%async_computation.2 | async-start | bytes 4456448 | tf_op jit(solution)/shard_map/all_gather | solution.py:72
  42.5 2.4 copy-start.9
  42.5 2.5 copy-start.10
  43.9 6.7 %copy-start.4 = (bf16[2,4,512,2,128]{4,3,2,1,0:T(2,128)(2,1)S(1)}, bf16[2,4,512,2,128]{4,3,2,1,0:T(2,128)(2,1)}, u32[]{:S(2)}) copy-start(bf16[2,4,512,2,128]{4,3,2,1,0:T(2,128)(2,1)} %param.13) | copy-start | bytes 6291460
  44.8 202.0 %reduce-scatter.2.cloned.1.call-start = ((), (), s32[]{:S(2)}) async-start(), calls=%async_computation.3 | async-start | bytes 4259840 | tf_op jit(solution)/shard_map/reduce_scatter | solution.py:147
  119.7 3.0 %copy-start.1 = (bf16[256,8,4,256]{3,1,2,0:T(8,128)(2,1)}, bf16[256,8,4,256]{3,1,2,0:T(8,128)(2,1)S(1)}, u32[]{:S(2)}) copy-start(bf16[256,8,4,256]{3,1,2,0:T(8,128)(2,1)S(1)} %copy.97) | copy-start | bytes 12582916
  132.9 3.6 %copy-start.7 = (bf16[1,1,512,2,128]{4,3,2,1,0:T(2,128)(2,1)S(1)}, bf16[1,1,512,2,128]{4,3,2,1,0:T(2,128)(2,1)}, u32[]{:S(2)}) copy-start(bf16[1,1,512,2,128]{4,3,2,1,0:T(2,128)(2,1)} %get-tuple-element.20) | copy-start | bytes 786436
  143.6 3.6 %copy-start.6 = (bf16[1,1,512,2,128]{4,3,2,1,0:T(2,128)(2,1)S(1)}, bf16[1,1,512,2,128]{4,3,2,1,0:T(2,128)(2,1)}, u32[]{:S(2)}) copy-start(bf16[1,1,512,2,128]{4,3,2,1,0:T(2,128)(2,1)} %get-tuple-element.17) | copy-start | bytes 786436
  147.2 5.2 %copy-start.2 = (bf16[1024,1536]{0,1:T(8,128)(2,1)S(1)}, bf16[1024,1536]{0,1:T(8,128)(2,1)}, u32[]{:S(2)}) copy-start(bf16[1024,1536]{0,1:T(8,128)(2,1)} %slice.90) | copy-start | bytes 9437188
  147.2 5.2 %copy-start.5 = (pred[1024,64]{0,1:T(8,128)(4,1)S(1)}, pred[1024,64]{0,1:T(8,128)(4,1)}, u32[]{:S(2)}) copy-start(pred[1024,64]{0,1:T(8,128)(4,1)} %compare_and_fusion) | copy-start | bytes 196612
  153.6 1.7 copy-start.3
  268.9 15.5 %copy-start.8 = (bf16[256,384]{1,0:T(8,128)(2,1)S(1)}, bf16[256,384]{1,0:T(8,128)(2,1)}, u32[]{:S(2)}) copy-start(bf16[256,384]{1,0:T(8,128)(2,1)} %param.8) | copy-start | bytes 589828
Sparse Core Ops, SparseCore 0:
  9.1 31.5 all-gather.5
  44.9 56.4 all-gather.3
  205.6 41.1 reduce-scatter.1

commit v6 on v5

--- a/solution.py
+++ b/solution.py
@@ -13,27 +13,20 @@
     return (full * lax.rsqrt(meansq + EPS) * gain).astype(jnp.bfloat16)
 
 
-def partial_softmax(grouped_queries, keys, values, allowed, form_s, form_o):
+def masked_scores(grouped_queries, keys, allowed, form_s):
     scores = jnp.einsum(
         form_s, grouped_queries, keys, preferred_element_type=jnp.float32
     ) * grouped_queries.shape[-1] ** (-0.5)
-    masked = jnp.where(allowed, scores, NEG)
-    peak = jnp.max(masked, -1)
-    weights = jnp.where(allowed, jnp.exp(masked - peak[..., None]), 0.0)
+    return jnp.where(allowed, scores, NEG)
+
+
+def weigh(masked, allowed, shift, values, form_o):
+    weights = jnp.where(allowed, jnp.exp(jnp.minimum(masked - shift[..., None], 80.0)), 0.0)
     total = jnp.sum(weights, -1)
     weighted = jnp.einsum(
         form_o, weights.astype(jnp.bfloat16), values, preferred_element_type=jnp.float32
     )
-    return (peak, total, weighted)
-
-
-def join_parts(first, second):
-    peak = jnp.maximum(first[0], second[0])
-    scale_a = jnp.exp(first[0] - peak)
-    scale_b = jnp.exp(second[0] - peak)
-    total = first[1] * scale_a + second[1] * scale_b
-    weighted = first[2] * scale_a[..., None] + second[2] * scale_b[..., None]
-    return (peak, total, weighted)
+    return total, weighted
 
 
 def per_device(tokens, attn_gain, w_qkv, w_out, prefix_cache, decode_cache, offsets, lengths):
@@ -85,42 +78,42 @@
     cache_pos = joined * shard + jnp.arange(shard, dtype=jnp.int32)
     pieces = []
     for index in range(n_prefix):
-        block = grouped_queries[index * span : (index + 1) * span]
+        rows = slice(index * span, (index + 1) * span)
         allowed = (cache_pos < offsets[index])[None, None, None, :]
         pieces.append(
-            partial_softmax(
-                block,
-                prefix_cache[0, index],
+            (
+                rows,
+                masked_scores(grouped_queries[rows], prefix_cache[0, index], allowed, "qhgd,khd->qhgk"),
+                allowed,
                 prefix_cache[1, index],
-                allowed,
-                "qhgd,khd->qhgk",
                 "qhgk,khd->qhgd",
             )
         )
+    rows = slice(n_prefix * span, every_rows)
     allowed = (cache_pos[None, :] < lengths[:, None])[:, None, None, :]
     pieces.append(
-        partial_softmax(
-            grouped_queries[n_prefix * span :],
-            decode_cache[0],
+        (
+            rows,
+            masked_scores(grouped_queries[rows], decode_cache[0], allowed, "nhgd,nkhd->nhgk"),
+            allowed,
             decode_cache[1],
-            allowed,
-            "nhgd,nkhd->nhgk",
             "nhgk,nkhd->nhgd",
         )
     )
-    cached = tuple((jnp.concatenate([piece[slot] for piece in pieces], 0) for slot in range(3)))
     allowed = ((sequence[:, None] == own_seq[None, :]) & (own_pos[None, :] <= positions[:, None]))[
         :, None, None, :
     ]
-    fresh = partial_softmax(
-        grouped_queries, own_keys, own_values, allowed, "rhgd,khd->rhgk", "rhgk,khd->rhgd"
-    )
-    peak, total, weighted = join_parts(cached, fresh)
+    fresh = masked_scores(grouped_queries, own_keys, allowed, "rhgd,khd->rhgk")
+    peak = jnp.concatenate([jnp.max(piece[1], -1) for piece in pieces], 0)
+    peak = jnp.maximum(peak, jnp.max(fresh, -1))
     top = lax.pmax(peak, "narrow")
     hi = lax.reduce_precision(top, exponent_bits=8, mantissa_bits=7)
     lo = lax.reduce_precision(top - hi, exponent_bits=8, mantissa_bits=7)
     shift = hi + lo
-    scale = jnp.exp(jnp.minimum(peak - shift, 80.0))
+    total, weighted = weigh(fresh, allowed, shift, own_values, "rhgk,khd->rhgd")
+    cached = [weigh(m, ok, shift[rows], v, form) for rows, m, ok, v, form in pieces]
+    total = total + jnp.concatenate([piece[0] for piece in cached], 0)
+    weighted = weighted + jnp.concatenate([piece[1] for piece in cached], 0)
     first = lax.axis_index("narrow") == 0
 
     def kept(a):
@@ -129,8 +122,8 @@
     lanes = 128
     packed = jnp.concatenate(
         [
-            (weighted * scale[..., None]).reshape(every_rows, q_width),
-            (total * scale).reshape(every_rows, heads),
+            weighted.reshape(every_rows, q_width),
+            total.reshape(every_rows, heads),
             kept(hi),
             kept(lo),
             jnp.zeros((every_rows, lanes - 3 * heads), jnp.float32),

time: 294 us -> 322 us (1.095)
  matrix products: 31.1 us -> 46.1 us
  other arithmetic: 13 us -> 22.4 us
  local copies, waits for them, and re-layouts: 62.8 us -> 67 us
    dot_general x8, matrix products: 28.4 us -> 43.4 us  [the longest x4 21.8 us: weigh(): jnp.einsum(form_o, weights.astype(jnp.bfloat16), values, preferred_elemen...]
    reduce_sum x4, other arithmetic: 8.16 us -> 17.5 us  [weigh(): total = jnp.sum(weights, -1)]
    concatenate x8 -> x11, local copies, waits for them, and re-layouts: 14.9 us -> 15 us  [the longest x6 14.6 us: per_device(): jnp.concatenate([weighted.reshape(every_rows, q_width), total.reshape(eve...]
where the time goes in v6:
time: 322 us; the launch traced here: 321 us
  waiting for transfers between devices  109 us (34%)
  local copies, waits for them, and re-layouts  67 us (21%)
  blocking collectives  62.9 us (20%)
  matrix products  46.1 us (14%)
  other arithmetic  22.4 us (7%)
  between operations  13.4 us (4%)
    all_gather x1, waiting for transfers between devices, per_device(): gathered = lax.all_gather(part, ('wide', 'narrow'), axis=0, tiled=False)  48.2 us
    reduce_scatter x1, waiting for transfers between devices, per_device(): packed = lax.psum_scatter(packed, 'narrow', scatter_dimension=0, tiled=True)  41.4 us
    dot_general x4, matrix products, weigh(): jnp.einsum(form_o, weights.astype(jnp.bfloat16), values, preferred_elemen...  21.8 us
    dot_general x4, matrix products, masked_scores(): jnp.einsum(form_s, grouped_queries, keys, preferred_element_type=jnp.floa...  21.6 us
    all_gather x1, waiting for transfers between devices, per_device(): w_cols = lax.all_gather(w_qkv, 'wide', axis=0, tiled=False)  18.4 us
    pmax x1, blocking collectives, per_device(): top = lax.pmax(peak, 'narrow')  17.5 us
    reduce_sum x4, other arithmetic, weigh(): total = jnp.sum(weights, -1)  17.5 us
    all_to_all x1, blocking collectives, per_device(): packed = lax.all_to_all(packed.reshape(n_wide, own, width), 'wide', 0, 0)  17.2 us
  transfers between devices with their start and end apart: 3, of which 3 were waited for; matrix products, arithmetic and copies ran while one was open for 3% of the time, Pallas kernels for 0%

profile of v6, /device:TPU:32, one launch (start us, length us, event | category | flops | bytes accessed | tf_op | source)
XLA Modules:
  0.0 320.7 jit_solution(5814297536260967705)
XLA Ops:
  7.3 14.8 %all_gather.15 = bf16[256,1536]{1,0:T(8,128)(2,1)S(1)} all-gather(bf16[256,384]{1,0:T(8,128)(2,1)} %param.8), channel_id=1, replica_groups=mesh['rep'=16,'wide'=4,'narrow'=4] {'narrow'}, dimensions={1}, use_global_device_ids=true | all-gather | bytes 983040 | tf_op jit(solution)/shard_map/all_gather | solution.py:57
  22.4 18.4 %all-gather.6.cloned.1.call-done = bf16[6144,128]{1,0:T(8,128)(2,1)} async-done(((bf16[1536,128]{1,0:T(8,128)(2,1)}), bf16[6144,128]{1,0:T(8,128)(2,1)}) %all-gather.6.cloned.1.call-update) | async-done | bytes 1572880 | tf_op jit(solution)/shard_map/all_gather | solution.py:59
  40.8 1.7 copy.48
  47.9 2.7 fusion.85
  50.6 2.6 fusion.84
  53.2 48.2 %all-gather.4.cloned.1.call-done = bf16[16,256,512]{2,1,0:T(8,128)(2,1)} async-done(((bf16[1,256,512]{2,1,0:T(8,128)(2,1)}), bf16[16,256,512]{2,1,0:T(8,128)(2,1)}) %all-gather.4.cloned.1.call-update) | async-done | bytes 4194320 | tf_op jit(solution)/shard_map/all_gather | solution.py:65
  101.5 6.9 %reshape.172 = bf16[4,4,256,4,128]{4,3,2,1,0:T(4,128)(2,1)} reshape(bf16[16,256,512]{2,1,0:T(8,128)(2,1)} %all-gather.4.cloned.1.call-done) | data formatting | bytes 8388608 | tf_op jit(solution)/shard_map/reshape | solution.py:67
  108.4 8.1 %copy.50 = bf16[4,4,256,4,128]{2,0,4,1,3:T(4,128)(2,1)} copy(bf16[4,4,256,4,128]{4,3,2,1,0:T(4,128)(2,1)} %reshape.172) | data formatting | bytes 8388608 | tf_op jit(solution)/shard_map/reshape | solution.py:67
  116.5 3.2 %copy.103 = bf16[256,8,4,256]{3,1,2,0:T(8,128)(2,1)S(1)} copy(bf16[256,8,4,256]{3,2,1,0:T(4,128)(2,1)} %bitcast.149) | data formatting | bytes 8388608
  119.9 2.3 slice.99
  122.6 2.2 fusion.83
  125.0 2.3 fusion.88
  129.0 4.9 %fusion.19 = (f32[1024,2,6]{0,2,1:T(8,128)S(1)}, f32[2,64,1024,6]{2,1,3,0:T(8,128)}) fusion(pred[1024,64]{0,1:T(8,128)(4,1)S(1)} %copy-done.6, bf16[64,2,128,1]{0,2,3,1:T(8,128)(2,1)S(1)} %bitcast.163, bf16[1024,2,6,128]{0,3,2,1:T(8,128)(2,1)} %bitcast.152), kind=kOutput, calls=%fused_computation.26 | convolution fusion | flops 203673600 | bytes 6438912 | tf_op jit(solution)/shard_map/rhgd,khd->rhgk/dot_general | solution.py:17
  133.9 7.3 %bitcast_reduce_fusion = (f32[510,2,6]{0,2,1:T(8,128)S(1)}, f32[2,510,6,512]{3,1,2,0:T(8,128)}) fusion(pred[512]{0:T(512)(128)(4,1)S(1)} %get-tuple-element.34, bf16[510,2,6,128]{0,3,2,1:T(8,128)(2,1)S(1)} %bitcast.154, bf16[1,1,512,2,128]{4,3,2,1,0:T(2,128)(2,1)S(1)} %copy-done.5), kind=kOutput, calls=%fused_computation.1 | convolution fusion | flops 811554816 | bytes 14387616 | tf_op jit(solution)/shard_map/qhgd,khd->qhgk/dot_general | solution.py:17
  141.2 7.2 %bitcast_reduce_fusion.1 = (f32[510,2,6]{0,2,1:T(8,128)S(1)}, f32[2,510,6,512]{3,1,2,0:T(8,128)}) fusion(pred[512]{0:T(512)(128)(4,1)S(1)} %get-tuple-element.35, bf16[510,2,6,128]{0,3,2,1:T(8,128)(2,1)S(1)} %bitcast.153, bf16[1,1,512,2,128]{4,3,2,1,0:T(2,128)(2,1)S(1)} %get-tuple-element.15), kind=kOutput, calls=%fused_computation.6 | convolution fusion | flops 811554816 | bytes 14387616 | tf_op jit(solution)/shard_map/qhgd,khd->qhgk/dot_general | solution.py:17
  148.5 17.5 %pmax.7 = f32[1024,2,6]{0,2,1:T(8,128)S(1)} all-reduce(f32[1024,2,6]{0,2,1:T(8,128)S(1)} %maximum_maximum_fusion), channel_id=1, replica_groups=mesh['rep'=16,'wide'=4,'narrow'=4] {'narrow'}, use_global_device_ids=true, to_apply=%region_5.6 | all-reduce | flops 12288 | bytes 98304 | tf_op jit(solution)/shard_map/pmax | solution.py:109
  168.3 2.9 fusion.20
  171.3 7.4 %fusion.6 = f32[510,2,6]{0,2,1:T(8,128)S(1)} fusion(f32[2,510,6,512]{3,1,2,0:T(8,128)} %get-tuple-element.31, f32[510,2,6]{0,2,1:T(8,128)S(1)} %get-tuple-element.20, pred[512]{0:T(512)(128)(4,1)S(1)} %get-tuple-element.35), kind=kLoop, calls=%fused_computation.12 | loop fusion | flops 18794520 | bytes 12583232 | tf_op jit(solution)/shard_map/reduce_sum | solution.py:25
  179.6 5.2 %fusion.22 = f32[510,2,6,128]{0,3,2,1:T(8,128)} fusion(f32[2,510,6,512]{3,1,2,0:T(8,128)S(1)} %copy-done.1, f32[510,2,6]{0,2,1:T(8,128)S(1)} %get-tuple-element.20, pred[512]{0:T(512)(128)(4,1)S(1)} %get-tuple-element.35, bf16[1,1,512,2,128]{4,3,2,1,0:T(2,128)(2,1)S(1)} %copy-done.9), kind=kOutput, calls=%fused_computation.31 | convolution fusion | flops 820961280 | bytes 15954336 | tf_op jit(solution)/shard_map/qhgk,khd->qhgd/dot_general | solution.py:26
  184.8 7.0 %fusion.8 = f32[510,2,6]{0,2,1:T(8,128)S(1)} fusion(f32[2,510,6,512]{3,1,2,0:T(8,128)} %get-tuple-element.29, f32[510,2,6]{0,2,1:T(8,128)S(1)} %get-tuple-element.21, pred[512]{0:T(512)(128)(4,1)S(1)} %get-tuple-element.34), kind=kLoop, calls=%fused_computation.14 | loop fusion | flops 18794520 | bytes 12583232 | tf_op jit(solution)/shard_map/reduce_sum | solution.py:25
  191.8 7.7 %fusion.25 = f32[510,2,6,128]{0,3,2,1:T(8,128)} fusion(f32[2,510,6,512]{3,1,2,0:T(8,128)} %get-tuple-element.29, f32[510,2,6]{0,2,1:T(8,128)S(1)} %get-tuple-element.21, pred[512]{0:T(512)(128)(4,1)S(1)} %get-tuple-element.34, bf16[1,1,512,2,128]{4,3,2,1,0:T(2,128)(2,1)S(1)} %copy-done.8), kind=kOutput, calls=%fused_computation.32 | convolution fusion | flops 820961280 | bytes 15954336 | tf_op jit(solution)/shard_map/qhgk,khd->qhgd/dot_general | solution.py:26
  201.7 7.4 %fusion.10 = bf16[1024,2,6,128]{0,3,2,1:T(8,128)(2,1)} fusion(f32[4,2,6,128]{0,3,2,1:T(8,128)} %copy.69, f32[510,2,6,128]{0,3,2,1:T(8,128)} %fusion.25, f32[510,2,6,128]{0,3,2,1:T(8,128)} %fusion.22, bf16[64,2,128,1]{0,2,3,1:T(8,128)(2,1)S(1)} %bitcast.164, f32[2,64,1024,6]{2,1,3,0:T(8,128)} %get-tuple-element.25, f32[1024,2,6]{0,2,1:T(8,128)S(1)} %get-tuple-element.19, ...), kind=kOutput, calls=%fused_computation.17 | convolution fusion | flops 212336640 | bytes 12730368 | tf_op jit(solution)/shard_map/rhgk,khd->rhgd/dot_general | solution.py:26
  209.2 6.6 %copy.70 = bf16[1024,2,6,128]{3,2,1,0:T(8,128)(2,1)} copy(bf16[1024,2,6,128]{0,3,2,1:T(8,128)(2,1)} %fusion.10) | data formatting | bytes 6291456 | tf_op jit(solution)/shard_map/convert.7
  215.7 7.5 %concatenate.35 = bf16[4,4,64,1536]{3,2,1,0:T(8,128)(2,1)} reshape(bf16[1024,2,6,128]{3,2,1,0:T(8,128)(2,1)} %copy.70) | data formatting | bytes 6291456 | tf_op jit(solution)/shard_map/concatenate | solution.py:123
  223.4 6.4 %concatenate.43 = bf16[4,4,64,1664]{3,2,1,0:T(8,128)(2,1)} concatenate(bf16[4,4,64,1536]{3,2,1,0:T(8,128)(2,1)} %concatenate.35, bf16[4,4,64,12]{3,2,1,0:T(8,128)(2,1)S(1)} %add_convert_fusion, bf16[4,4,64,12]{3,2,1,0:T(8,128)(2,1)S(1)} %copy.74, bf16[4,4,64,12]{3,2,1,0:T(8,128)(2,1)S(1)} %copy.75, bf16[4,4,64,92]{3,2,1,0:T(8,128)(2,1)S(1)} %broadcast_in_dim.103), dimensions={3} | concatenate | bytes 6815744 | tf_op jit(solution)/shard_map/concatenate | solution.py:123
  229.8 4.0 %copy.76 = bf16[4,4,64,1664]{3,2,1,0:T(8,128)(2,1)} copy(bf16[4,4,64,1664]{3,2,0,1:T(8,128)(2,1)} %bitcast.151) | data formatting | bytes 6815744 | tf_op jit(solution)/shard_map/transpose | solution.py:137
  233.9 41.4 %reduce-scatter.2.cloned.1.call-done = bf16[256,1664]{1,0:T(8,128)(2,1)} async-done(((bf16[1024,1664]{1,0:T(8,128)(2,1)}), bf16[256,1664]{1,0:T(8,128)(2,1)}) %reduce-scatter.2.cloned.1.call-update) | async-done | bytes 851984 | tf_op jit(solution)/shard_map/reduce_scatter | solution.py:140
  275.2 17.2 %all_to_all.5 = bf16[4,64,1664]{2,1,0:T(8,128)(2,1)S(1)} all-to-all(bf16[4,64,1664]{2,1,0:T(8,128)(2,1)} %bitcast.161), channel_id=1, replica_groups=mesh['rep'=16,'wide'=4,'narrow'=4] {'wide'}, dimensions={0} | all-to-all | bytes 1703936 | tf_op jit(solution)/shard_map/all_to_all | solution.py:141
  292.8 2.0 mul.80
  294.8 2.6 mul.81
  297.4 1.7 fusion.32
  299.4 13.5 %all_gather.19 = bf16[256,1536]{1,0:T(8,128)(2,1)S(1)} all-gather(bf16[64,1536]{1,0:T(8,128)(2,1)S(1)} %fusion.46), channel_id=1, replica_groups=mesh['rep'=16,'wide'=4,'narrow'=4] {'narrow'}, dimensions={0}, use_global_device_ids=true | all-gather | bytes 983040 | tf_op jit(solution)/shard_map/all_gather | solution.py:153
  (81 shorter events, 16.7 us)
Async XLA Ops:
  6.5 306.3 %copy-start = (bf16[1536,384]{1,0:T(8,128)(2,1)S(1)}, bf16[1536,384]{1,0:T(8,128)(2,1)}, u32[]{:S(2)}) copy-start(bf16[1536,384]{1,0:T(8,128)(2,1)} %param.11) | copy-start | bytes 3538948
  6.5 34.2 %all-gather.6.cloned.1.call-start = ((), (), s32[]{:S(2)}) async-start(), calls=%async_computation.4 | async-start | bytes 1966080 | tf_op jit(solution)/shard_map/all_gather | solution.py:59
  7.3 94.2 %all-gather.4.cloned.1.call-start = ((), (), s32[]{:S(2)}) async-start(), calls=%async_computation.2 | async-start | bytes 4456448 | tf_op jit(solution)/shard_map/all_gather | solution.py:65
  42.5 2.4 copy-start.12
  42.5 2.5 copy-start.13
  43.9 6.7 %copy-start.4 = (bf16[2,4,512,2,128]{4,3,2,1,0:T(2,128)(2,1)S(1)}, bf16[2,4,512,2,128]{4,3,2,1,0:T(2,128)(2,1)}, u32[]{:S(2)}) copy-start(bf16[2,4,512,2,128]{4,3,2,1,0:T(2,128)(2,1)} %param.13) | copy-start | bytes 6291460
  44.8 230.4 %reduce-scatter.2.cloned.1.call-start = ((), (), s32[]{:S(2)}) async-start(), calls=%async_computation.3 | async-start | bytes 4259840 | tf_op jit(solution)/shard_map/reduce_scatter | solution.py:140
  119.7 3.0 copy-start.2
  122.6 6.4 %copy-start.6 = (pred[1024,64]{0,1:T(8,128)(4,1)S(1)}, pred[1024,64]{0,1:T(8,128)(4,1)}, u32[]{:S(2)}) copy-start(pred[1024,64]{0,1:T(8,128)(4,1)} %compare_and_fusion) | copy-start | bytes 196612
  129.0 4.9 %copy-start.3 = (bf16[510,1536]{0,1:T(8,128)(2,1)S(1)}, bf16[510,1536]{0,1:T(8,128)(2,1)}, u32[]{:S(2)}) copy-start(bf16[510,1536]{0,1:T(8,128)(2,1)} %get-tuple-element.10) | copy-start | bytes 4700164
  129.0 4.9 %copy-start.5 = (bf16[1,1,512,2,128]{4,3,2,1,0:T(2,128)(2,1)S(1)}, bf16[1,1,512,2,128]{4,3,2,1,0:T(2,128)(2,1)}, u32[]{:S(2)}) copy-start(bf16[1,1,512,2,128]{4,3,2,1,0:T(2,128)(2,1)} %get-tuple-element.14) | copy-start | bytes 786436
  141.2 25.0 %copy-start.7 = (f32[4,2,6,512]{3,2,1,0:T(8,128)S(1)}, f32[4,2,6,512]{3,2,1,0:T(8,128)}, u32[]{:S(2)}) copy-start(f32[4,2,6,512]{3,2,1,0:T(8,128)} %get-tuple-element.27) | copy-start | bytes 294916
  168.3 10.4 %copy-start.9 = (bf16[1,1,512,2,128]{4,3,2,1,0:T(2,128)(2,1)S(1)}, bf16[1,1,512,2,128]{4,3,2,1,0:T(2,128)(2,1)}, u32[]{:S(2)}) copy-start(bf16[1,1,512,2,128]{4,3,2,1,0:T(2,128)(2,1)} %get-tuple-element.13) | copy-start | bytes 786436
  171.3 8.3 %copy-start.1 = (f32[2,510,6,512]{3,1,2,0:T(8,128)S(1)}, f32[2,510,6,512]{3,1,2,0:T(8,128)}, u32[]{:S(2)}) copy-start(f32[2,510,6,512]{3,1,2,0:T(8,128)} %get-tuple-element.31) | copy-start | bytes 37601284
  184.8 7.0 %copy-start.8 = (bf16[1,1,512,2,128]{4,3,2,1,0:T(2,128)(2,1)S(1)}, bf16[1,1,512,2,128]{4,3,2,1,0:T(2,128)(2,1)}, u32[]{:S(2)}) copy-start(bf16[1,1,512,2,128]{4,3,2,1,0:T(2,128)(2,1)} %get-tuple-element.16) | copy-start | bytes 786436
  191.8 9.9 %copy-start.11 = (bf16[64,256]{0,1:T(8,128)(2,1)S(1)}, bf16[64,256]{0,1:T(8,128)(2,1)}, u32[]{:S(2)}) copy-start(bf16[64,256]{0,1:T(8,128)(2,1)} %get-tuple-element.7) | copy-start | bytes 98308
  297.4 15.5 %copy-start.10 = (bf16[256,384]{1,0:T(8,128)(2,1)S(1)}, bf16[256,384]{1,0:T(8,128)(2,1)}, u32[]{:S(2)}) copy-start(bf16[256,384]{1,0:T(8,128)(2,1)} %param.8) | copy-start | bytes 589828
Sparse Core Ops, SparseCore 0:
  9.1 31.5 all-gather.5
  44.9 56.4 all-gather.3
  234.0 41.1 reduce-scatter.1

commit v7 on v5

--- a/solution.py
+++ b/solution.py
@@ -68,18 +68,17 @@
         "rf,wfc->rwc", normed_rows, w_cols, preferred_element_type=jnp.float32
     ).astype(jnp.bfloat16)
     col_block = w_qkv.shape[1]
-    part = part.reshape(block_rows, n_wide * col_block)
-    gathered = lax.all_gather(part, ("wide", "narrow"), axis=0, tiled=False)
-    qkv_all = (
-        gathered.reshape(n_wide, n_narrow, block_rows, n_wide, col_block)
+    q_blocks = q_width // (n_narrow * col_block)
+    gathered = lax.all_gather(part[:, :q_blocks], ("wide", "narrow"), axis=0, tiled=False)
+    query_matrix = (
+        gathered.reshape(n_wide, n_narrow, block_rows, q_blocks, col_block)
         .transpose(0, 2, 3, 1, 4)
-        .reshape(every_rows, devices * col_block)
+        .reshape(every_rows, heads, head_dim)
     )
-    query_matrix = qkv_all[:, :q_width].reshape(every_rows, heads, head_dim)
-    own_qkv = lax.dynamic_slice_in_dim(qkv_all, own_start, own, 0)
-    kv_width = kv_heads * head_dim
-    own_keys = own_qkv[:, q_width : q_width + kv_width].reshape(own, kv_heads, head_dim)
-    own_values = own_qkv[:, q_width + kv_width :].reshape(own, kv_heads, head_dim)
+    fresh_kv = part[:, q_blocks:].reshape(n_narrow, own, col_block)
+    fresh_kv = lax.all_to_all(fresh_kv, "narrow", 0, 0)
+    own_keys = fresh_kv[:kv_heads].transpose(1, 0, 2)
+    own_values = fresh_kv[kv_heads:].transpose(1, 0, 2)
     grouped_queries = query_matrix.reshape(every_rows, kv_heads, group, head_dim)
     shard = prefix_cache.shape[2]
     cache_pos = joined * shard + jnp.arange(shard, dtype=jnp.int32)

time: 294 us -> 262 us (0.89)
  local copies, waits for them, and re-layouts: 62.8 us -> 40.3 us
  waiting for transfers between devices: 109 us -> 101 us
  starting transfers between devices: 0.08 us -> 4.33 us
  matrix products: 31.1 us -> 28 us
    reshape x2 -> x0, local copies, waits for them, and re-layouts: 15 us -> none  [per_device(): gathered.reshape(n_wide, n_narrow, block_rows, n_wide, col_block)]
    all_gather x1, waiting for transfers between devices: 48.4 us -> 40 us  [per_device(): lax.all_gather(part[:, :q_blocks], ('wide', 'narrow'), axis=0, tiled=False)]
    all_to_all x0 -> x1, starting transfers between devices: none -> 4.28 us  [per_device(): fresh_kv = lax.all_to_all(fresh_kv, 'narrow', 0, 0)]
    slice x3 -> x2, local copies, waits for them, and re-layouts: 5.46 us -> 1.31 us  [the longest x1 0.69 us: per_device(): part[:, :q_blocks]]
    unnamed x23 -> x16, local copies, waits for them, and re-layouts: 5.4 us -> 1.72 us
  transfers between devices with their start and end apart: 3 -> 4, of which waited for: 3 -> 3; matrix products, arithmetic and copies ran while one was open for 3% -> 12% of each run, Pallas kernels for 0% -> 0%
where the time goes in v7:
time: 262 us; the launch traced here: 261 us
  waiting for transfers between devices  101 us (39%)
  blocking collectives  62 us (24%)
  local copies, waits for them, and re-layouts  40.3 us (15%)
  matrix products  28 us (11%)
  between operations  13.3 us (5%)
  other arithmetic  12.3 us (5%)
  starting transfers between devices  4.33 us (2%)
    reduce_scatter x1, waiting for transfers between devices, per_device(): packed = lax.psum_scatter(packed, 'narrow', scatter_dimension=0, tiled=True)  41.7 us
    all_gather x1, waiting for transfers between devices, per_device(): lax.all_gather(part[:, :q_blocks], ('wide', 'narrow'), axis=0, tiled=False)  40 us
    all_gather x1, waiting for transfers between devices, per_device(): w_cols = lax.all_gather(w_qkv, 'wide', axis=0, tiled=False)  18.4 us
    dot_general x4, matrix products, partial_softmax(): jnp.einsum(form_o, weights.astype(jnp.bfloat16), values, preferred_elemen...  17.3 us
    all_to_all x1, blocking collectives, per_device(): packed = lax.all_to_all(packed.reshape(n_wide, own, width), 'wide', 0, 0)  17.2 us
    pmax x1, blocking collectives, per_device(): top = lax.pmax(peak, 'narrow')  16.5 us
    concatenate x8, local copies, waits for them, and re-layouts, per_device(): jnp.concatenate([(weighted * scale[..., None]).reshape(every_rows, q_widt...  14.9 us
    all_gather x1, blocking collectives, per_device(): features = lax.all_gather(tokens, 'narrow', axis=1, tiled=True)  14.8 us
  transfers between devices with their start and end apart: 4, of which 3 were waited for; matrix products, arithmetic and copies ran while one was open for 12% of the time, Pallas kernels for 0%

profile of v7, /device:TPU:32, one launch (start us, length us, event | category | flops | bytes accessed | tf_op | source)
XLA Modules:
  0.0 261.0 jit_solution(17190418783668780346)
XLA Ops:
  6.5 0.7 all-gather.5.cloned.1.call-update
  7.3 14.8 %all_gather.18 = bf16[256,1536]{1,0:T(8,128)(2,1)S(1)} all-gather(bf16[256,384]{1,0:T(8,128)(2,1)} %param.8), channel_id=1, replica_groups=mesh['rep'=16,'wide'=4,'narrow'=4] {'narrow'}, dimensions={1}, use_global_device_ids=true | all-gather | bytes 983040 | tf_op jit(solution)/shard_map/all_gather | solution.py:64
  22.4 18.4 %all-gather.5.cloned.1.call-done = bf16[6144,128]{1,0:T(8,128)(2,1)} async-done(((bf16[1536,128]{1,0:T(8,128)(2,1)}), bf16[6144,128]{1,0:T(8,128)(2,1)}) %all-gather.5.cloned.1.call-update) | async-done | bytes 1572880 | tf_op jit(solution)/shard_map/all_gather | solution.py:66
  40.8 2.0 convolution_convert_fusion
  44.5 1.2 fusion.75
  45.9 2.6 %fusion.89 = (bf16[1,1,512,2,128]{4,3,2,1,0:T(2,128)(2,1)S(1)}, bf16[1,1,512,2,128]{4,3,2,1,0:T(2,128)(2,1)}, bf16[1,1,512,2,128]{4,3,2,1,0:T(2,128)(2,1)S(1)}, bf16[1,1,512,2,128]{4,3,2,1,0:T(2,128)(2,1)S(1)}) fusion(bf16[2,2,512,2,128]{4,3,2,1,0:T(2,128)(2,1)} %param.12), kind=kLoop, calls=%fused_computation.127 | loop fusion | bytes 2097152 | tf_op jit(solution)/shard_map/slice | solution.py:93
  48.5 3.4 %fusion.88 = (bf16[1,4,512,2,128]{4,3,2,1,0:T(2,128)(2,1)S(1)}, bf16[1,4,512,2,128]{4,3,2,1,0:T(2,128)(2,1)}) fusion(bf16[2,4,512,2,128]{4,3,2,1,0:T(2,128)(2,1)} %param.13), kind=kLoop, calls=%fused_computation.126 | loop fusion | bytes 4194304 | tf_op jit(solution)/shard_map/slice | solution.py:103
  52.6 4.3 %all-to-all-start = ((bf16[4,64,128]{2,1,0:T(8,128)(2,1)}), bf16[4,64,128]{2,1,0:T(8,128)(2,1)S(1)}, u32[]{:S(2)}, u32[]{:S(2)}) async-start(bf16[4,64,128]{2,1,0:T(8,128)(2,1)} %bitcast.25), calls=%async_computation | async-start | bytes 131072 | tf_op jit(solution)/shard_map/all_to_all | solution.py:79
  56.9 40.0 %all-gather.7.cloned.1.call-done = bf16[4096,3,128]{2,0,1:T(8,128)(2,1)} async-done(((bf16[256,3,128]{2,0,1:T(8,128)(2,1)}), bf16[4096,3,128]{2,0,1:T(8,128)(2,1)}) %all-gather.7.cloned.1.call-update) | async-done | bytes 3145744 | tf_op jit(solution)/shard_map/all_gather | solution.py:72
  96.9 2.3 copy.39
  99.2 1.9 bitcast_reduce_fusion
  101.1 3.6 %fusion.6 = f32[510,2,6]{0,2,1:T(8,128)S(1)} fusion(f32[2,510,6,512]{3,1,2,0:T(8,128)S(1)} %get-tuple-element.28, f32[510,2,6]{0,2,1:T(8,128)S(1)} %get-tuple-element.27, pred[512]{0:T(512)(128)(4,1)S(1)} %get-tuple-element.33), kind=kLoop, calls=%fused_computation.12 | loop fusion | flops 15661080 | bytes 12583232 | tf_op jit(solution)/shard_map/reduce_sum | solution.py:23
  104.7 4.2 %fusion.25 = f32[510,2,6,128]{3,0,2,1:T(8,128)} fusion(f32[2,510,6,512]{3,1,2,0:T(8,128)S(1)} %get-tuple-element.28, f32[510,2,6]{0,2,1:T(8,128)S(1)} %get-tuple-element.27, pred[512]{0:T(512)(128)(4,1)S(1)} %get-tuple-element.33, bf16[1,1,512,2,128]{4,3,2,1,0:T(2,128)(2,1)S(1)} %get-tuple-element.16), kind=kOutput, calls=%fused_computation.33 | convolution fusion | flops 817827840 | bytes 15954336 | tf_op jit(solution)/shard_map/qhgk,khd->qhgd/dot_general | solution.py:24
  108.9 1.9 bitcast_reduce_fusion.1
  110.8 3.6 %fusion.4 = f32[510,2,6]{0,2,1:T(8,128)S(1)} fusion(f32[2,510,6,512]{3,1,2,0:T(8,128)S(1)} %get-tuple-element.30, f32[510,2,6]{0,2,1:T(8,128)S(1)} %get-tuple-element.29, pred[512]{0:T(512)(128)(4,1)S(1)} %get-tuple-element.34), kind=kLoop, calls=%fused_computation.10 | loop fusion | flops 15661080 | bytes 12583232 | tf_op jit(solution)/shard_map/reduce_sum | solution.py:23
  114.3 4.3 %fusion.22 = f32[510,2,6,128]{3,0,2,1:T(8,128)} fusion(f32[2,510,6,512]{3,1,2,0:T(8,128)S(1)} %get-tuple-element.30, f32[510,2,6]{0,2,1:T(8,128)S(1)} %get-tuple-element.29, pred[512]{0:T(512)(128)(4,1)S(1)} %get-tuple-element.34, bf16[1,1,512,2,128]{4,3,2,1,0:T(2,128)(2,1)S(1)} %get-tuple-element.13), kind=kOutput, calls=%fused_computation.32 | convolution fusion | flops 817827840 | bytes 15954336 | tf_op jit(solution)/shard_map/qhgk,khd->qhgd/dot_general | solution.py:24
  119.8 3.1 %fusion.19 = (f32[1024,2,6]{0,2,1:T(8,128)S(1)}, f32[2,64,1024,6]{2,1,3,0:T(8,128)S(1)}) fusion(pred[1024,64]{0,1:T(8,128)(4,1)S(1)} %compare_and_fusion, bf16[1024,2,6,128]{3,0,2,1:T(8,128)(2,1)} %bitcast.135, bf16[4,64,128]{2,1,0:T(8,128)(2,1)S(1)} %all-to-all-done), kind=kOutput, calls=%fused_computation.27 | convolution fusion | flops 203673600 | bytes 6438912 | tf_op jit(solution)/shard_map/rhgd,khd->rhgk/dot_general | solution.py:17
  122.9 1.7 copy-done.2
  124.6 0.8 fusion.20
  125.6 16.5 %pmax.7 = f32[1024,2,6]{0,2,1:T(8,128)S(1)} all-reduce(f32[1024,2,6]{0,2,1:T(8,128)S(1)} %fusion.68), channel_id=1, replica_groups=mesh['rep'=16,'wide'=4,'narrow'=4] {'narrow'}, use_global_device_ids=true, to_apply=%region_5.6 | all-reduce | flops 12288 | bytes 98304 | tf_op jit(solution)/shard_map/pmax | solution.py:118
  143.1 8.5 %fusion.10 = bf16[1024,2,6,128]{3,0,2,1:T(8,128)(2,1)S(1)} fusion(f32[4,2,6,128]{3,0,2,1:T(4,128)S(1)} %copy.47, f32[510,2,6,128]{3,0,2,1:T(8,128)} %fusion.25, f32[510,2,6,128]{3,0,2,1:T(8,128)} %fusion.22, f32[1024,2,6]{0,2,1:T(8,128)S(1)} %get-tuple-element.20, f32[1024,2,6]{0,2,1:T(8,128)S(1)} %get-tuple-element.21, ...), kind=kOutput, calls=%fused_computation.17 | convolution fusion | flops 216268800 | bytes 12943360 | tf_op jit(solution)/shard_map/rhgk,khd->rhgd/dot_general | solution.py:24
  151.7 4.1 %copy.50 = bf16[1024,2,6,128]{3,2,1,0:T(8,128)(2,1)} copy(bf16[1024,2,6,128]{3,0,2,1:T(8,128)(2,1)S(1)} %fusion.10) | data formatting | bytes 6291456 | tf_op jit(solution)/shard_map/convert.8
  155.8 7.5 %concatenate.38 = bf16[4,4,64,1536]{3,2,1,0:T(8,128)(2,1)} reshape(bf16[1024,2,6,128]{3,2,1,0:T(8,128)(2,1)} %copy.50) | data formatting | bytes 6291456 | tf_op jit(solution)/shard_map/concatenate | solution.py:129
  163.4 6.4 %concatenate.43 = bf16[4,4,64,1664]{3,2,1,0:T(8,128)(2,1)} concatenate(bf16[4,4,64,1536]{3,2,1,0:T(8,128)(2,1)} %concatenate.38, bf16[4,4,64,12]{3,2,1,0:T(8,128)(2,1)S(1)} %copy.52, bf16[4,4,64,12]{3,2,1,0:T(8,128)(2,1)S(1)} %copy.53, bf16[4,4,64,12]{3,2,1,0:T(8,128)(2,1)S(1)} %copy.54, bf16[4,4,64,92]{3,2,1,0:T(8,128)(2,1)S(1)} %broadcast_in_dim.106), dimensions={3} | concatenate | bytes 6815744 | tf_op jit(solution)/shard_map/concatenate | solution.py:129
  169.8 4.0 %copy.55 = bf16[4,4,64,1664]{3,2,1,0:T(8,128)(2,1)} copy(bf16[4,4,64,1664]{3,2,0,1:T(8,128)(2,1)} %bitcast.137) | data formatting | bytes 6815744 | tf_op jit(solution)/shard_map/transpose | solution.py:143
  173.8 41.7 %reduce-scatter.2.cloned.1.call-done = bf16[256,1664]{1,0:T(8,128)(2,1)} async-done(((bf16[1024,1664]{1,0:T(8,128)(2,1)}), bf16[256,1664]{1,0:T(8,128)(2,1)}) %reduce-scatter.2.cloned.1.call-update) | async-done | bytes 851984 | tf_op jit(solution)/shard_map/reduce_scatter | solution.py:146
  215.6 17.2 %all_to_all.10 = bf16[4,64,1664]{2,1,0:T(8,128)(2,1)S(1)} all-to-all(bf16[4,64,1664]{2,1,0:T(8,128)(2,1)} %bitcast.140), channel_id=1, replica_groups=mesh['rep'=16,'wide'=4,'narrow'=4] {'wide'}, dimensions={0} | all-to-all | bytes 1703936 | tf_op jit(solution)/shard_map/all_to_all | solution.py:147
  233.2 2.0 mul.122
  235.1 2.6 mul.123
  237.7 1.7 fusion.32
  239.7 13.5 %all_gather.23 = bf16[256,1536]{1,0:T(8,128)(2,1)S(1)} all-gather(bf16[64,1536]{1,0:T(8,128)(2,1)S(1)} %fusion.49), channel_id=1, replica_groups=mesh['rep'=16,'wide'=4,'narrow'=4] {'narrow'}, dimensions={0}, use_global_device_ids=true | all-gather | bytes 983040 | tf_op jit(solution)/shard_map/all_gather | solution.py:159
  253.2 1.3 fusion.42
  (55 shorter events, 6.0 us)
Async XLA Ops:
  6.5 246.7 %copy-start = (bf16[1536,384]{1,0:T(8,128)(2,1)S(1)}, bf16[1536,384]{1,0:T(8,128)(2,1)}, u32[]{:S(2)}) copy-start(bf16[1536,384]{1,0:T(8,128)(2,1)} %param.11) | copy-start | bytes 3538948
  6.5 37.0 %copy-start.6 = (s32[2]{0:T(128)S(1)}, s32[2]{0:T(128)}, u32[]{:S(2)}) copy-start(s32[2]{0:T(128)} %param.14) | copy-start | bytes 28
  6.5 37.2 %copy-start.7 = (s32[4]{0:T(128)S(1)}, s32[4]{0:T(128)}, u32[]{:S(2)}) copy-start(s32[4]{0:T(128)} %param.15) | copy-start | bytes 52
  6.5 34.2 %all-gather.5.cloned.1.call-start = ((), (), s32[]{:S(2)}) async-start(), calls=%async_computation.4 | async-start | bytes 1966080 | tf_op jit(solution)/shard_map/all_gather | solution.py:66
  7.3 89.6 %all-gather.7.cloned.1.call-start = ((), (), s32[]{:S(2)}) async-start(), calls=%async_computation.5 | async-start | bytes 3342336 | tf_op jit(solution)/shard_map/all_gather | solution.py:72
  52.6 67.2 %all-to-all-start = ((bf16[4,64,128]{2,1,0:T(8,128)(2,1)}), bf16[4,64,128]{2,1,0:T(8,128)(2,1)S(1)}, u32[]{:S(2)}, u32[]{:S(2)}) async-start(bf16[4,64,128]{2,1,0:T(8,128)(2,1)} %bitcast.25), calls=%async_computation | async-start | bytes 131072 | tf_op jit(solution)/shard_map/all_to_all | solution.py:79
  56.9 158.7 %reduce-scatter.2.cloned.1.call-start = ((), (), s32[]{:S(2)}) async-start(), calls=%async_computation.3 | async-start | bytes 4259840 | tf_op jit(solution)/shard_map/reduce_scatter | solution.py:146
  96.9 2.3 copy-start.4
  99.2 9.7 %copy-start.1 = (bf16[4,256,3,4,128]{4,1,0,3,2:T(8,128)(2,1)}, bf16[4,256,3,4,128]{4,1,0,3,2:T(8,128)(2,1)S(1)}, u32[]{:S(2)}) copy-start(bf16[4,256,3,4,128]{4,1,0,3,2:T(8,128)(2,1)S(1)} %copy.39) | copy-start | bytes 9437188
  114.3 4.7 %copy-start.3 = (bf16[1,4,512,2,128]{4,3,2,1,0:T(2,128)(2,1)S(1)}, bf16[1,4,512,2,128]{4,3,2,1,0:T(2,128)(2,1)}, u32[]{:S(2)}) copy-start(bf16[1,4,512,2,128]{4,3,2,1,0:T(2,128)(2,1)} %get-tuple-element.12) | copy-start | bytes 3145732
  122.9 1.7 copy-start.2
  237.7 15.5 %copy-start.5 = (bf16[256,384]{1,0:T(8,128)(2,1)S(1)}, bf16[256,384]{1,0:T(8,128)(2,1)}, u32[]{:S(2)}) copy-start(bf16[256,384]{1,0:T(8,128)(2,1)} %param.8) | copy-start | bytes 589828
Sparse Core Ops, SparseCore 0:
  9.1 31.5 all-gather.4
  43.6 53.1 all-gather.6
  174.0 41.5 reduce-scatter.1

commit v8 on v7

--- a/solution.py
+++ b/solution.py
@@ -32,8 +32,12 @@
     scale_a = jnp.exp(first[0] - peak)
     scale_b = jnp.exp(second[0] - peak)
     total = first[1] * scale_a + second[1] * scale_b
-    weighted = first[2] * scale_a[..., None] + second[2] * scale_b[..., None]
+    weighted = first[2] * heads_major(scale_a) + second[2] * heads_major(scale_b)
     return (peak, total, weighted)
+
+
+def heads_major(scale):
+    return scale.transpose(1, 2, 0)[..., None]
 
 
 def per_device(tokens, attn_gain, w_qkv, w_out, prefix_cache, decode_cache, offsets, lengths):
@@ -93,7 +97,7 @@
                 prefix_cache[1, index],
                 allowed,
                 "qhgd,khd->qhgk",
-                "qhgk,khd->qhgd",
+                "qhgk,khd->hgqd",
             )
         )
     allowed = (cache_pos[None, :] < lengths[:, None])[:, None, None, :]
@@ -104,15 +108,15 @@
             decode_cache[1],
             allowed,
             "nhgd,nkhd->nhgk",
-            "nhgk,nkhd->nhgd",
+            "nhgk,nkhd->hgnd",
         )
     )
-    cached = tuple((jnp.concatenate([piece[slot] for piece in pieces], 0) for slot in range(3)))
+    cached = tuple((jnp.concatenate([piece[slot] for piece in pieces], 2 * (slot // 2)) for slot in range(3)))
     allowed = ((sequence[:, None] == own_seq[None, :]) & (own_pos[None, :] <= positions[:, None]))[
         :, None, None, :
     ]
     fresh = partial_softmax(
-        grouped_queries, own_keys, own_values, allowed, "rhgd,khd->rhgk", "rhgk,khd->rhgd"
+        grouped_queries, own_keys, own_values, allowed, "rhgd,khd->rhgk", "rhgk,khd->hgrd"
     )
     peak, total, weighted = join_parts(cached, fresh)
     top = lax.pmax(peak, "narrow")
@@ -126,9 +130,8 @@
         return jnp.where(first, a, jnp.zeros_like(a)).reshape(every_rows, heads)
 
     lanes = 128
-    packed = jnp.concatenate(
+    extra = jnp.concatenate(
         [
-            (weighted * scale[..., None]).reshape(every_rows, q_width),
             (total * scale).reshape(every_rows, heads),
             kept(hi),
             kept(lo),
@@ -136,26 +139,24 @@
         ],
         1,
     )
-    width = packed.shape[1]
+    scaled = (weighted * heads_major(scale)).reshape(heads, every_rows, head_dim)
+    packed = jnp.concatenate([scaled, extra[None]], 0).astype(jnp.bfloat16)
+    slots = packed.shape[0]
     packed = (
-        packed.astype(jnp.bfloat16)
-        .reshape(n_wide, n_narrow, own, width)
-        .transpose(1, 0, 2, 3)
-        .reshape(every_rows, width)
+        packed.reshape(slots, n_wide, n_narrow, own, head_dim)
+        .transpose(0, 2, 1, 3, 4)
+        .reshape(slots, every_rows, head_dim)
     )
-    packed = lax.psum_scatter(packed, "narrow", scatter_dimension=0, tiled=True)
-    packed = lax.all_to_all(packed.reshape(n_wide, own, width), "wide", 0, 0)
+    packed = lax.psum_scatter(packed, "narrow", scatter_dimension=1, tiled=True)
+    packed = lax.all_to_all(packed.reshape(slots, n_wide, own, head_dim), "wide", 1, 1)
     packed = packed.astype(jnp.float32)
-    part_shift = (
-        packed[:, :, q_width + heads : q_width + 2 * heads]
-        + packed[:, :, q_width + 2 * heads : q_width + 3 * heads]
-    )
+    extra = packed[heads]
+    part_shift = extra[..., heads : 2 * heads] + extra[..., 2 * heads : 3 * heads]
     part_scale = jnp.exp(part_shift - jnp.max(part_shift, 0)[None])
-    total = jnp.sum(packed[:, :, q_width : q_width + heads] * part_scale, 0)
-    total = total.reshape(own, heads, 1)
-    weighted = packed[:, :, :q_width].reshape(n_wide, own, heads, head_dim)
-    weighted = jnp.sum(weighted * part_scale[..., None], 0)
-    attended = (weighted / total).astype(jnp.bfloat16).reshape(own, q_width)
+    total = jnp.sum(extra[..., :heads] * part_scale, 0)
+    weighted = jnp.sum(packed[:heads] * part_scale.transpose(2, 0, 1)[..., None], 1)
+    attended = weighted / total.T[..., None]
+    attended = attended.astype(jnp.bfloat16).transpose(1, 0, 2).reshape(own, q_width)
     mine_rows = lax.all_gather(attended, "narrow", axis=0, tiled=True)
     mixed = tokens.astype(jnp.float32) + jnp.dot(
         mine_rows, w_out, preferred_element_type=jnp.float32

time: 262 us -> 238 us (0.908)
  local copies, waits for them, and re-layouts: 40.3 us -> 12.4 us
  other arithmetic: 12.3 us -> 15.4 us
    concatenate x8 -> x7, local copies, waits for them, and re-layouts: 14.9 us -> 1.05 us  [per_device(): jnp.concatenate([(total * scale).reshape(every_rows, heads), kept(hi), ke...]
    mul x2 -> x0, local copies, waits for them, and re-layouts: 4.55 us -> none  [per_device(): weighted = jnp.sum(weighted * part_scale[..., None], 0)]
    another operation x1 -> x0, local copies, waits for them, and re-layouts: 4.09 us -> none
    transpose x1, local copies, waits for them, and re-layouts: 4.02 us -> 0.1 us  [per_device(): part_scale.transpose(2, 0, 1)[..., None]]
    concatenate x0 -> x1, other arithmetic: none -> 3.26 us  [per_device(): packed = jnp.concatenate([scaled, extra[None]], 0).astype(jnp.bfloat16)]
    reduce_sum x4 -> x3, other arithmetic: 8.15 us -> 7.97 us  [partial_softmax(): total = jnp.sum(weights, -1)]
  transfers between devices with their start and end apart: 4 -> 4, of which waited for: 3 -> 3; matrix products, arithmetic and copies ran while one was open for 12% -> 9% of each run, Pallas kernels for 0% -> 0%
where the time goes in v8:
time: 238 us; the launch traced here: 237 us
  waiting for transfers between devices  102 us (43%)
  blocking collectives  61.7 us (26%)
  matrix products  28.1 us (12%)
  other arithmetic  15.4 us (6%)
  between operations  13.4 us (6%)
  local copies, waits for them, and re-layouts  12.4 us (5%)
  starting transfers between devices  4.37 us (2%)
    reduce_scatter x1, waiting for transfers between devices, per_device(): packed = lax.psum_scatter(packed, 'narrow', scatter_dimension=1, tiled=True)  41.7 us
    all_gather x1, waiting for transfers between devices, per_device(): lax.all_gather(part[:, :q_blocks], ('wide', 'narrow'), axis=0, tiled=False)  41 us
    all_gather x1, waiting for transfers between devices, per_device(): w_cols = lax.all_gather(w_qkv, 'wide', axis=0, tiled=False)  18.4 us
    dot_general x4, matrix products, partial_softmax(): jnp.einsum(form_o, weights.astype(jnp.bfloat16), values, preferred_elemen...  17.4 us
    all_to_all x1, blocking collectives, per_device(): lax.all_to_all(packed.reshape(slots, n_wide, own, head_dim), 'wide', 1, 1)  17 us
    pmax x1, blocking collectives, per_device(): top = lax.pmax(peak, 'narrow')  16.5 us
    all_gather x1, blocking collectives, per_device(): features = lax.all_gather(tokens, 'narrow', axis=1, tiled=True)  14.8 us
    all_gather x1, blocking collectives, per_device(): mine_rows = lax.all_gather(attended, 'narrow', axis=0, tiled=True)  13.5 us
  transfers between devices with their start and end apart: 4, of which 3 were waited for; matrix products, arithmetic and copies ran while one was open for 9% of the time, Pallas kernels for 0%

profile of v8, /device:TPU:32, one launch (start us, length us, event | category | flops | bytes accessed | tf_op | source)
XLA Modules:
  0.0 237.3 jit_solution(5814794510141817188)
XLA Ops:
  6.6 0.7 all-gather.5.cloned.1.call-update
  7.3 14.8 %all_gather.18 = bf16[256,1536]{1,0:T(8,128)(2,1)S(1)} all-gather(bf16[256,384]{1,0:T(8,128)(2,1)} %param.8), channel_id=1, replica_groups=mesh['rep'=16,'wide'=4,'narrow'=4] {'narrow'}, dimensions={1}, use_global_device_ids=true | all-gather | bytes 983040 | tf_op jit(solution)/shard_map/all_gather | solution.py:68
  22.4 18.4 %all-gather.5.cloned.1.call-done = bf16[6144,128]{1,0:T(8,128)(2,1)} async-done(((bf16[1536,128]{1,0:T(8,128)(2,1)}), bf16[6144,128]{1,0:T(8,128)(2,1)}) %all-gather.5.cloned.1.call-update) | async-done | bytes 1572880 | tf_op jit(solution)/shard_map/all_gather | solution.py:70
  40.8 2.0 convolution_convert_fusion
  42.8 0.7 copy-done.7
  43.5 0.7 slice.80
  44.7 0.7 fusion.93
  45.4 1.3 fusion.76
  46.7 0.7 compare_and_fusion
  47.5 1.5 fusion.92
  49.0 1.5 fusion.91
  50.5 1.5 slice.84
  52.0 4.3 %all-to-all-start = ((bf16[4,64,128]{2,1,0:T(8,128)(2,1)}), bf16[4,64,128]{2,1,0:T(8,128)(2,1)}, u32[]{:S(2)}, u32[]{:S(2)}) async-start(bf16[4,64,128]{2,1,0:T(8,128)(2,1)} %bitcast.160), calls=%async_computation | async-start | bytes 131072 | tf_op jit(solution)/shard_map/all_to_all | solution.py:83
  56.3 41.0 %all-gather.7.cloned.1.call-done = bf16[4096,3,128]{2,0,1:T(8,128)(2,1)} async-done(((bf16[256,3,128]{2,0,1:T(8,128)(2,1)}), bf16[4096,3,128]{2,0,1:T(8,128)(2,1)}) %all-gather.7.cloned.1.call-update) | async-done | bytes 3145744 | tf_op jit(solution)/shard_map/all_gather | solution.py:76
  97.3 2.3 copy.85
  100.4 1.9 bitcast_reduce_fusion
  102.3 3.6 %fusion.6 = f32[510,2,6]{0,2,1:T(8,128)S(1)} fusion(f32[2,510,6,512]{3,1,2,0:T(8,128)S(1)} %get-tuple-element.27, f32[510,2,6]{0,2,1:T(8,128)S(1)} %get-tuple-element.26, pred[512]{0:T(512)(128)(4,1)S(1)} %get-tuple-element.32), kind=kLoop, calls=%fused_computation.12 | loop fusion | flops 15661080 | bytes 12583232 | tf_op jit(solution)/shard_map/reduce_sum | solution.py:23
  105.9 4.2 %fusion.25 = f32[2,6,510,128]{3,2,1,0:T(8,128)} fusion(f32[2,510,6,512]{3,1,2,0:T(8,128)S(1)} %get-tuple-element.27, f32[510,2,6]{0,2,1:T(8,128)S(1)} %get-tuple-element.26, pred[512]{0:T(512)(128)(4,1)S(1)} %get-tuple-element.32, bf16[1,1,512,2,128]{4,3,2,1,0:T(2,128)(2,1)S(1)} %copy-done.9), kind=kOutput, calls=%fused_computation.34 | convolution fusion | flops 817827840 | bytes 15954336 | tf_op jit(solution)/shard_map/qhgk,khd->hgqd/dot_general | solution.py:24
  110.4 3.3 %fusion.19 = (f32[1024,2,6]{0,2,1:T(8,128)S(1)}, f32[2,64,1024,6]{2,1,3,0:T(8,128)S(1)}) fusion(pred[1024,64]{0,1:T(8,128)(4,1)S(1)} %copy-done.5, bf16[1024,2,6,128]{3,0,2,1:T(8,128)(2,1)} %bitcast.154, bf16[4,64,128]{2,1,0:T(8,128)(2,1)} %all-to-all-done), kind=kOutput, calls=%fused_computation.28 | convolution fusion | flops 203673600 | bytes 6438912 | tf_op jit(solution)/shard_map/rhgd,khd->rhgk/dot_general | solution.py:17
  113.7 0.8 fusion.20
  114.5 0.8 copy-done.3
  115.4 1.9 bitcast_reduce_fusion.1
  117.4 3.6 %fusion.4 = f32[510,2,6]{0,2,1:T(8,128)S(1)} fusion(f32[2,510,6,512]{3,1,2,0:T(8,128)S(1)} %get-tuple-element.29, f32[510,2,6]{0,2,1:T(8,128)S(1)} %get-tuple-element.28, pred[512]{0:T(512)(128)(4,1)S(1)} %get-tuple-element.33), kind=kLoop, calls=%fused_computation.10 | loop fusion | flops 15661080 | bytes 12583232 | tf_op jit(solution)/shard_map/reduce_sum | solution.py:23
  121.0 4.2 %fusion.22 = f32[2,6,510,128]{3,2,1,0:T(8,128)} fusion(f32[2,510,6,512]{3,1,2,0:T(8,128)S(1)} %get-tuple-element.29, f32[510,2,6]{0,2,1:T(8,128)S(1)} %get-tuple-element.28, pred[512]{0:T(512)(128)(4,1)S(1)} %get-tuple-element.33, bf16[1,1,512,2,128]{4,3,2,1,0:T(2,128)(2,1)S(1)} %copy-done.8), kind=kOutput, calls=%fused_computation.33 | convolution fusion | flops 817827840 | bytes 15954336 | tf_op jit(solution)/shard_map/qhgk,khd->hgqd/dot_general | solution.py:24
  125.2 16.5 %pmax.7 = f32[1024,2,6]{0,2,1:T(8,128)S(1)} all-reduce(f32[1024,2,6]{0,2,1:T(8,128)S(1)} %get-tuple-element.6), channel_id=1, replica_groups=mesh['rep'=16,'wide'=4,'narrow'=4] {'narrow'}, use_global_device_ids=true, to_apply=%region_5.6 | all-reduce | flops 12288 | bytes 98304 | tf_op jit(solution)/shard_map/pmax | solution.py:122
  142.8 8.7 %fusion.10 = bf16[2,6,1024,128]{3,2,1,0:T(8,128)(2,1)S(1)} fusion(f32[2,6,4,128]{3,2,1,0:T(4,128)S(1)} %bitcast.161, f32[2,6,510,128]{3,2,1,0:T(8,128)} %fusion.25, f32[2,6,510,128]{3,2,1,0:T(8,128)} %fusion.22, f32[2,6,1024]{2,1,0:T(8,128)S(1)} %get-tuple-element.19, f32[2,6,1024]{2,1,0:T(8,128)S(1)} %get-tuple-element.17, ...), kind=kOutput, calls=%fused_computation.17 | convolution fusion | flops 216268800 | bytes 12902400 | tf_op jit(solution)/shard_map/rhgk,khd->hgrd/dot_general | solution.py:24
  151.4 3.3 %maximum_maximum_fusion = bf16[13,4,4,64,128]{4,3,1,2,0:T(8,128)(2,1)} fusion(bf16[1,4,4,64,12]{4,3,1,2,0:T(8,128)(2,1)S(1)} %copy.104, bf16[1,4,4,64,12]{4,3,1,2,0:T(8,128)(2,1)S(1)} %copy.103, bf16[1,4,4,64,12]{4,3,1,2,0:T(8,128)(2,1)S(1)} %copy.102, bf16[13,128]{1,0:T(8,128)(2,1)S(1)} %pad.4.clone, bf16[12,4,4,64,128]{4,3,2,1,0:T(8,128)(2,1)S(1)} %bitcast.158), kind=kLoop, calls=%fused_computation.25 | loop fusion | flops 17039360 | bytes 6630656 | tf_op jit(solution)/shard_map/concatenate | solution.py:143
  154.7 41.7 %reduce-scatter.2.cloned.1.call-done = bf16[13,256,128]{2,1,0:T(8,128)(2,1)} async-done(((bf16[13,1024,128]{2,1,0:T(8,128)(2,1)}), bf16[13,256,128]{2,1,0:T(8,128)(2,1)}) %reduce-scatter.2.cloned.1.call-update) | async-done | bytes 851984 | tf_op jit(solution)/shard_map/reduce_scatter | solution.py:150
  196.4 1.2 copy.106
  197.7 17.0 %all_to_all.10 = bf16[13,4,64,128]{3,2,0,1:T(8,128)(2,1)S(1)} all-to-all(bf16[13,4,64,128]{3,2,0,1:T(8,128)(2,1)S(1)} %copy.106), channel_id=1, replica_groups=mesh['rep'=16,'wide'=4,'narrow'=4] {'wide'}, dimensions={1} | all-to-all | bytes 1703936 | tf_op jit(solution)/shard_map/all_to_all | solution.py:151
  216.0 13.5 %all_gather.23 = bf16[256,1536]{1,0:T(8,128)(2,1)S(1)} all-gather(bf16[64,1536]{1,0:T(8,128)(2,1)S(1)} %copy_bitcast_fusion.12), channel_id=1, replica_groups=mesh['rep'=16,'wide'=4,'narrow'=4] {'narrow'}, dimensions={0}, use_global_device_ids=true | all-gather | bytes 983040 | tf_op jit(solution)/shard_map/all_gather | solution.py:160
  229.5 1.3 fusion.42
  (65 shorter events, 4.4 us)
Async XLA Ops:
  6.5 222.9 %copy-start = (bf16[1536,384]{1,0:T(8,128)(2,1)S(1)}, bf16[1536,384]{1,0:T(8,128)(2,1)}, u32[]{:S(2)}) copy-start(bf16[1536,384]{1,0:T(8,128)(2,1)} %param.11) | copy-start | bytes 3538948
  6.5 37.7 %copy-start.12 = (s32[2]{0:T(128)S(1)}, s32[2]{0:T(128)}, u32[]{:S(2)}) copy-start(s32[2]{0:T(128)} %param.14) | copy-start | bytes 28
  6.5 37.9 %copy-start.13 = (s32[4]{0:T(128)S(1)}, s32[4]{0:T(128)}, u32[]{:S(2)}) copy-start(s32[4]{0:T(128)} %param.15) | copy-start | bytes 52
  6.5 40.9 %copy-start.6 = (bf16[2,2,512,2,128]{4,3,2,1,0:T(2,128)(2,1)S(1)}, bf16[2,2,512,2,128]{4,3,2,1,0:T(2,128)(2,1)}, u32[]{:S(2)}) copy-start(bf16[2,2,512,2,128]{4,3,2,1,0:T(2,128)(2,1)} %param.12) | copy-start | bytes 3145732
  6.5 34.2 %all-gather.5.cloned.1.call-start = ((), (), s32[]{:S(2)}) async-start(), calls=%async_computation.4 | async-start | bytes 1966080 | tf_op jit(solution)/shard_map/all_gather | solution.py:70
  7.3 90.0 %all-gather.7.cloned.1.call-start = ((), (), s32[]{:S(2)}) async-start(), calls=%async_computation.5 | async-start | bytes 3342336 | tf_op jit(solution)/shard_map/all_gather | solution.py:76
  42.8 0.7 copy-start.7
  44.4 4.6 %copy-start.4 = (bf16[2,4,512,2,128]{4,3,2,1,0:T(2,128)(2,1)S(1)}, bf16[2,4,512,2,128]{4,3,2,1,0:T(2,128)(2,1)}, u32[]{:S(2)}) copy-start(bf16[2,4,512,2,128]{4,3,2,1,0:T(2,128)(2,1)} %param.13) | copy-start | bytes 6291460
  52.0 58.4 %all-to-all-start = ((bf16[4,64,128]{2,1,0:T(8,128)(2,1)}), bf16[4,64,128]{2,1,0:T(8,128)(2,1)}, u32[]{:S(2)}, u32[]{:S(2)}) async-start(bf16[4,64,128]{2,1,0:T(8,128)(2,1)} %bitcast.160), calls=%async_computation | async-start | bytes 131072 | tf_op jit(solution)/shard_map/all_to_all | solution.py:83
  56.3 140.2 %reduce-scatter.2.cloned.1.call-start = ((), (), s32[]{:S(2)}) async-start(), calls=%async_computation.3 | async-start | bytes 4259840 | tf_op jit(solution)/shard_map/reduce_scatter | solution.py:150
  97.3 3.1 %copy-start.10 = (bf16[1,1,512,2,128]{4,3,2,1,0:T(2,128)(2,1)S(1)}, bf16[1,1,512,2,128]{4,3,2,1,0:T(2,128)(2,1)}, u32[]{:S(2)}) copy-start(bf16[1,1,512,2,128]{4,3,2,1,0:T(2,128)(2,1)} %get-tuple-element.10) | copy-start | bytes 786436
  99.6 2.7 %copy-start.1 = (bf16[4,256,3,4,128]{4,1,0,3,2:T(8,128)(2,1)}, bf16[4,256,3,4,128]{4,1,0,3,2:T(8,128)(2,1)S(1)}, u32[]{:S(2)}) copy-start(bf16[4,256,3,4,128]{4,1,0,3,2:T(8,128)(2,1)S(1)} %copy.85) | copy-start | bytes 9437188
  102.3 3.6 %copy-start.9 = (bf16[1,1,512,2,128]{4,3,2,1,0:T(2,128)(2,1)S(1)}, bf16[1,1,512,2,128]{4,3,2,1,0:T(2,128)(2,1)}, u32[]{:S(2)}) copy-start(bf16[1,1,512,2,128]{4,3,2,1,0:T(2,128)(2,1)} %get-tuple-element.12) | copy-start | bytes 786436
  105.9 4.5 %copy-start.5 = (pred[1024,64]{0,1:T(8,128)(4,1)S(1)}, pred[1024,64]{0,1:T(8,128)(4,1)}, u32[]{:S(2)}) copy-start(pred[1024,64]{0,1:T(8,128)(4,1)} %compare_and_fusion) | copy-start | bytes 196612
  110.4 5.0 %copy-start.2 = (bf16[4,256,3,4,128]{4,1,0,3,2:T(8,128)(2,1)S(1)}, bf16[4,256,3,4,128]{4,1,0,3,2:T(8,128)(2,1)}, u32[]{:S(2)}) copy-start(bf16[4,256,3,4,128]{4,1,0,3,2:T(8,128)(2,1)} %copy-done.1) | copy-start | bytes 9437188
  113.7 1.7 copy-start.3
  117.4 3.6 %copy-start.8 = (bf16[1,1,512,2,128]{4,3,2,1,0:T(2,128)(2,1)S(1)}, bf16[1,1,512,2,128]{4,3,2,1,0:T(2,128)(2,1)}, u32[]{:S(2)}) copy-start(bf16[1,1,512,2,128]{4,3,2,1,0:T(2,128)(2,1)} %get-tuple-element.9) | copy-start | bytes 786436
  214.6 14.8 %copy-start.11 = (bf16[256,384]{1,0:T(8,128)(2,1)S(1)}, bf16[256,384]{1,0:T(8,128)(2,1)}, u32[]{:S(2)}) copy-start(bf16[256,384]{1,0:T(8,128)(2,1)} %param.8) | copy-start | bytes 589828
Sparse Core Ops, SparseCore 0:
  9.2 31.5 all-gather.4
  44.4 52.8 all-gather.6
  154.8 41.5 reduce-scatter.1

commit v9 on v8

--- a/solution.py
+++ b/solution.py
@@ -118,12 +118,14 @@
     fresh = partial_softmax(
         grouped_queries, own_keys, own_values, allowed, "rhgd,khd->rhgk", "rhgk,khd->hgrd"
     )
-    peak, total, weighted = join_parts(cached, fresh)
-    top = lax.pmax(peak, "narrow")
+    top = lax.pmax(jnp.maximum(cached[0], fresh[0]), "narrow")
     hi = lax.reduce_precision(top, exponent_bits=8, mantissa_bits=7)
     lo = lax.reduce_precision(top - hi, exponent_bits=8, mantissa_bits=7)
     shift = hi + lo
-    scale = jnp.exp(jnp.minimum(peak - shift, 80.0))
+    scale_a = jnp.exp(jnp.minimum(cached[0] - shift, 80.0))
+    scale_b = jnp.exp(jnp.minimum(fresh[0] - shift, 80.0))
+    total = cached[1] * scale_a + fresh[1] * scale_b
+    weighted = cached[2] * heads_major(scale_a) + fresh[2] * heads_major(scale_b)
     first = lax.axis_index("narrow") == 0
 
     def kept(a):
@@ -132,14 +134,14 @@
     lanes = 128
     extra = jnp.concatenate(
         [
-            (total * scale).reshape(every_rows, heads),
+            total.reshape(every_rows, heads),
             kept(hi),
             kept(lo),
             jnp.zeros((every_rows, lanes - 3 * heads), jnp.float32),
         ],
         1,
     )
-    scaled = (weighted * heads_major(scale)).reshape(heads, every_rows, head_dim)
+    scaled = weighted.reshape(heads, every_rows, head_dim)
     packed = jnp.concatenate([scaled, extra[None]], 0).astype(jnp.bfloat16)
     slots = packed.shape[0]
     packed = (

time: 238 us -> 239 us (level)
  local copies, waits for them, and re-layouts: 12.4 us -> 14.9 us
where the time goes in v9:
time: 239 us; the launch traced here: 238 us
  waiting for transfers between devices  101 us (42%)
  blocking collectives  61.7 us (26%)
  matrix products  27.3 us (11%)
  other arithmetic  15.4 us (6%)
  local copies, waits for them, and re-layouts  14.9 us (6%)
  between operations  13.4 us (6%)
  starting transfers between devices  4.36 us (2%)
    reduce_scatter x1, waiting for transfers between devices, per_device(): packed = lax.psum_scatter(packed, 'narrow', scatter_dimension=1, tiled=True)  41.7 us
    all_gather x1, waiting for transfers between devices, per_device(): lax.all_gather(part[:, :q_blocks], ('wide', 'narrow'), axis=0, tiled=False)  40.2 us
    all_gather x1, waiting for transfers between devices, per_device(): w_cols = lax.all_gather(w_qkv, 'wide', axis=0, tiled=False)  18.4 us
    all_to_all x1, blocking collectives, per_device(): lax.all_to_all(packed.reshape(slots, n_wide, own, head_dim), 'wide', 1, 1)  17 us
    dot_general x4, matrix products, partial_softmax(): jnp.einsum(form_o, weights.astype(jnp.bfloat16), values, preferred_elemen...  16.8 us
    pmax x1, blocking collectives, per_device(): top = lax.pmax(jnp.maximum(cached[0], fresh[0]), 'narrow')  16.5 us
    all_gather x1, blocking collectives, per_device(): features = lax.all_gather(tokens, 'narrow', axis=1, tiled=True)  14.8 us
    all_gather x1, blocking collectives, per_device(): mine_rows = lax.all_gather(attended, 'narrow', axis=0, tiled=True)  13.5 us
  transfers between devices with their start and end apart: 4, of which 3 were waited for; matrix products, arithmetic and copies ran while one was open for 9% of the time, Pallas kernels for 0%

profile of v9, /device:TPU:32, one launch (start us, length us, event | category | flops | bytes accessed | tf_op | source)
XLA Modules:
  0.0 238.2 jit_solution(10492842360361214254)
XLA Ops:
  6.6 0.7 all-gather.5.cloned.1.call-update
  7.3 14.8 %all_gather.18 = bf16[256,1536]{1,0:T(8,128)(2,1)S(1)} all-gather(bf16[256,384]{1,0:T(8,128)(2,1)} %param.8), channel_id=1, replica_groups=mesh['rep'=16,'wide'=4,'narrow'=4] {'narrow'}, dimensions={1}, use_global_device_ids=true | all-gather | bytes 983040 | tf_op jit(solution)/shard_map/all_gather | solution.py:68
  22.4 18.4 %all-gather.5.cloned.1.call-done = bf16[6144,128]{1,0:T(8,128)(2,1)} async-done(((bf16[1536,128]{1,0:T(8,128)(2,1)}), bf16[6144,128]{1,0:T(8,128)(2,1)}) %all-gather.5.cloned.1.call-update) | async-done | bytes 1572880 | tf_op jit(solution)/shard_map/all_gather | solution.py:70
  40.8 2.0 convolution_convert_fusion
  42.8 0.7 copy-done.6
  43.5 0.7 slice.80
  45.4 1.3 fusion.70
  46.7 0.7 compare_and_fusion
  47.5 1.5 fusion.85
  49.0 2.7 %fusion.84 = (bf16[1,4,512,2,128]{4,3,2,1,0:T(2,128)(2,1)S(1)}, bf16[1,4,512,2,128]{4,3,2,1,0:T(2,128)(2,1)S(1)}) fusion(bf16[2,4,512,2,128]{4,3,2,1,0:T(2,128)(2,1)} %param.13), kind=kLoop, calls=%fused_computation.128 | loop fusion | bytes 4194304 | tf_op jit(solution)/shard_map/slice | solution.py:108
  51.7 1.5 slice.84
  53.2 4.3 %all-to-all-start = ((bf16[4,64,128]{2,1,0:T(8,128)(2,1)}), bf16[4,64,128]{2,1,0:T(8,128)(2,1)}, u32[]{:S(2)}, u32[]{:S(2)}) async-start(bf16[4,64,128]{2,1,0:T(8,128)(2,1)} %bitcast.158), calls=%async_computation | async-start | bytes 131072 | tf_op jit(solution)/shard_map/all_to_all | solution.py:83
  57.5 40.2 %all-gather.7.cloned.1.call-done = bf16[4096,3,128]{2,0,1:T(8,128)(2,1)} async-done(((bf16[256,3,128]{2,0,1:T(8,128)(2,1)}), bf16[4096,3,128]{2,0,1:T(8,128)(2,1)}) %all-gather.7.cloned.1.call-update) | async-done | bytes 3145744 | tf_op jit(solution)/shard_map/all_gather | solution.py:76
  97.6 2.3 copy.85
  100.7 1.9 bitcast_reduce_fusion
  102.6 3.6 %fusion.6 = f32[510,2,6]{0,2,1:T(8,128)S(1)} fusion(f32[2,510,6,512]{3,1,2,0:T(8,128)S(1)} %get-tuple-element.25, f32[510,2,6]{0,2,1:T(8,128)S(1)} %get-tuple-element.24, pred[512]{0:T(512)(128)(4,1)S(1)} %get-tuple-element.30), kind=kLoop, calls=%fused_computation.12 | loop fusion | flops 15661080 | bytes 12583232 | tf_op jit(solution)/shard_map/reduce_sum | solution.py:23
  106.2 4.2 %fusion.24 = f32[2,6,510,128]{3,2,1,0:T(8,128)} fusion(f32[2,510,6,512]{3,1,2,0:T(8,128)S(1)} %get-tuple-element.25, f32[510,2,6]{0,2,1:T(8,128)S(1)} %get-tuple-element.24, pred[512]{0:T(512)(128)(4,1)S(1)} %get-tuple-element.30, bf16[1,1,512,2,128]{4,3,2,1,0:T(2,128)(2,1)S(1)} %copy-done.8), kind=kOutput, calls=%fused_computation.33 | convolution fusion | flops 817827840 | bytes 15954336 | tf_op jit(solution)/shard_map/qhgk,khd->hgqd/dot_general | solution.py:24
  110.7 3.1 %fusion.18 = (f32[1024,2,6]{0,2,1:T(8,128)S(1)}, f32[2,64,1024,6]{2,1,3,0:T(8,128)S(1)}) fusion(pred[1024,64]{0,1:T(8,128)(4,1)S(1)} %copy-done.4, bf16[1024,2,6,128]{3,0,2,1:T(8,128)(2,1)} %bitcast.152, bf16[4,64,128]{2,1,0:T(8,128)(2,1)} %all-to-all-done), kind=kOutput, calls=%fused_computation.27 | convolution fusion | flops 203673600 | bytes 6438912 | tf_op jit(solution)/shard_map/rhgd,khd->rhgk/dot_general | solution.py:17
  113.9 0.8 fusion.19
  114.7 0.8 copy-done.3
  115.6 1.3 copy-done.2
  116.9 1.9 bitcast_reduce_fusion.1
  118.9 3.6 %fusion.4 = f32[510,2,6]{0,2,1:T(8,128)S(1)} fusion(f32[2,510,6,512]{3,1,2,0:T(8,128)S(1)} %get-tuple-element.27, f32[510,2,6]{0,2,1:T(8,128)S(1)} %get-tuple-element.26, pred[512]{0:T(512)(128)(4,1)S(1)} %get-tuple-element.31), kind=kLoop, calls=%fused_computation.10 | loop fusion | flops 15661080 | bytes 12583232 | tf_op jit(solution)/shard_map/reduce_sum | solution.py:23
  122.5 4.3 %fusion.21 = f32[2,6,510,128]{3,2,1,0:T(8,128)} fusion(f32[2,510,6,512]{3,1,2,0:T(8,128)S(1)} %get-tuple-element.27, f32[510,2,6]{0,2,1:T(8,128)S(1)} %get-tuple-element.26, pred[512]{0:T(512)(128)(4,1)S(1)} %get-tuple-element.31, bf16[1,1,512,2,128]{4,3,2,1,0:T(2,128)(2,1)S(1)} %copy-done.7), kind=kOutput, calls=%fused_computation.32 | convolution fusion | flops 817827840 | bytes 15954336 | tf_op jit(solution)/shard_map/qhgk,khd->hgqd/dot_general | solution.py:24
  126.8 16.5 %pmax.7 = f32[1024,2,6]{0,2,1:T(8,128)S(1)} all-reduce(f32[1024,2,6]{0,2,1:T(8,128)S(1)} %fusion.62), channel_id=1, replica_groups=mesh['rep'=16,'wide'=4,'narrow'=4] {'narrow'}, use_global_device_ids=true, to_apply=%region_5.6 | all-reduce | flops 12288 | bytes 98304 | tf_op jit(solution)/shard_map/pmax | solution.py:121
  144.3 8.0 %fusion.9 = bf16[2,6,1024,128]{3,2,1,0:T(8,128)(2,1)S(1)} fusion(f32[2,6,4,128]{3,2,1,0:T(4,128)S(1)} %bitcast.159, f32[2,6,510,128]{3,2,1,0:T(8,128)} %fusion.24, f32[2,6,510,128]{3,2,1,0:T(8,128)} %fusion.21, f32[2,6,1024]{2,1,0:T(8,128)S(1)} %get-tuple-element.17, f32[2,6,1024]{2,1,0:T(8,128)S(1)} %get-tuple-element.15, ...), kind=kOutput, calls=%fused_computation.16 | convolution fusion | flops 214695936 | bytes 12853248 | tf_op jit(solution)/shard_map/rhgk,khd->hgrd/dot_general | solution.py:24
  152.3 3.3 %maximum_maximum_fusion = bf16[13,4,4,64,128]{4,3,1,2,0:T(8,128)(2,1)} fusion(bf16[1,4,4,64,12]{4,3,1,2,0:T(8,128)(2,1)S(1)} %copy.104, bf16[1,4,4,64,12]{4,3,1,2,0:T(8,128)(2,1)S(1)} %copy.103, bf16[1,4,4,64,12]{4,3,1,2,0:T(8,128)(2,1)S(1)} %copy.102, bf16[13,128]{1,0:T(8,128)(2,1)S(1)} %pad.4.clone, bf16[12,4,4,64,128]{4,3,2,1,0:T(8,128)(2,1)S(1)} %bitcast.156), kind=kLoop, calls=%fused_computation.24 | loop fusion | flops 17039360 | bytes 6630656 | tf_op jit(solution)/shard_map/concatenate | solution.py:145
  155.6 41.7 %reduce-scatter.2.cloned.1.call-done = bf16[13,256,128]{2,1,0:T(8,128)(2,1)} async-done(((bf16[13,1024,128]{2,1,0:T(8,128)(2,1)}), bf16[13,256,128]{2,1,0:T(8,128)(2,1)}) %reduce-scatter.2.cloned.1.call-update) | async-done | bytes 851984 | tf_op jit(solution)/shard_map/reduce_scatter | solution.py:152
  197.3 1.2 copy.106
  198.6 17.0 %all_to_all.10 = bf16[13,4,64,128]{3,2,0,1:T(8,128)(2,1)S(1)} all-to-all(bf16[13,4,64,128]{3,2,0,1:T(8,128)(2,1)S(1)} %copy.106), channel_id=1, replica_groups=mesh['rep'=16,'wide'=4,'narrow'=4] {'wide'}, dimensions={1} | all-to-all | bytes 1703936 | tf_op jit(solution)/shard_map/all_to_all | solution.py:153
  216.9 13.5 %all_gather.23 = bf16[256,1536]{1,0:T(8,128)(2,1)S(1)} all-gather(bf16[64,1536]{1,0:T(8,128)(2,1)S(1)} %copy_bitcast_fusion.12), channel_id=1, replica_groups=mesh['rep'=16,'wide'=4,'narrow'=4] {'narrow'}, dimensions={0}, use_global_device_ids=true | all-gather | bytes 983040 | tf_op jit(solution)/shard_map/all_gather | solution.py:162
  230.4 1.3 fusion.41
  (63 shorter events, 5.1 us)
Async XLA Ops:
  6.5 223.8 %copy-start = (bf16[1536,384]{1,0:T(8,128)(2,1)S(1)}, bf16[1536,384]{1,0:T(8,128)(2,1)}, u32[]{:S(2)}) copy-start(bf16[1536,384]{1,0:T(8,128)(2,1)} %param.11) | copy-start | bytes 3538948
  6.5 37.7 %copy-start.11 = (s32[2]{0:T(128)S(1)}, s32[2]{0:T(128)}, u32[]{:S(2)}) copy-start(s32[2]{0:T(128)} %param.14) | copy-start | bytes 28
  6.5 37.9 %copy-start.12 = (s32[4]{0:T(128)S(1)}, s32[4]{0:T(128)}, u32[]{:S(2)}) copy-start(s32[4]{0:T(128)} %param.15) | copy-start | bytes 52
  6.5 40.9 %copy-start.5 = (bf16[2,2,512,2,128]{4,3,2,1,0:T(2,128)(2,1)S(1)}, bf16[2,2,512,2,128]{4,3,2,1,0:T(2,128)(2,1)}, u32[]{:S(2)}) copy-start(bf16[2,2,512,2,128]{4,3,2,1,0:T(2,128)(2,1)} %param.12) | copy-start | bytes 3145732
  6.5 34.2 %all-gather.5.cloned.1.call-start = ((), (), s32[]{:S(2)}) async-start(), calls=%async_computation.4 | async-start | bytes 1966080 | tf_op jit(solution)/shard_map/all_gather | solution.py:70
  7.3 90.4 %all-gather.7.cloned.1.call-start = ((), (), s32[]{:S(2)}) async-start(), calls=%async_computation.5 | async-start | bytes 3342336 | tf_op jit(solution)/shard_map/all_gather | solution.py:76
  42.8 0.7 copy-start.6
  53.2 57.5 %all-to-all-start = ((bf16[4,64,128]{2,1,0:T(8,128)(2,1)}), bf16[4,64,128]{2,1,0:T(8,128)(2,1)}, u32[]{:S(2)}, u32[]{:S(2)}) async-start(bf16[4,64,128]{2,1,0:T(8,128)(2,1)} %bitcast.158), calls=%async_computation | async-start | bytes 131072 | tf_op jit(solution)/shard_map/all_to_all | solution.py:83
  57.5 139.9 %reduce-scatter.2.cloned.1.call-start = ((), (), s32[]{:S(2)}) async-start(), calls=%async_computation.3 | async-start | bytes 4259840 | tf_op jit(solution)/shard_map/reduce_scatter | solution.py:152
  97.6 3.1 %copy-start.9 = (bf16[1,1,512,2,128]{4,3,2,1,0:T(2,128)(2,1)S(1)}, bf16[1,1,512,2,128]{4,3,2,1,0:T(2,128)(2,1)}, u32[]{:S(2)}) copy-start(bf16[1,1,512,2,128]{4,3,2,1,0:T(2,128)(2,1)} %get-tuple-element.8) | copy-start | bytes 786436
  99.9 2.7 %copy-start.1 = (bf16[4,256,3,4,128]{4,1,0,3,2:T(8,128)(2,1)}, bf16[4,256,3,4,128]{4,1,0,3,2:T(8,128)(2,1)S(1)}, u32[]{:S(2)}) copy-start(bf16[4,256,3,4,128]{4,1,0,3,2:T(8,128)(2,1)S(1)} %copy.85) | copy-start | bytes 9437188
  102.6 3.6 %copy-start.8 = (bf16[1,1,512,2,128]{4,3,2,1,0:T(2,128)(2,1)S(1)}, bf16[1,1,512,2,128]{4,3,2,1,0:T(2,128)(2,1)}, u32[]{:S(2)}) copy-start(bf16[1,1,512,2,128]{4,3,2,1,0:T(2,128)(2,1)} %get-tuple-element.10) | copy-start | bytes 786436
  106.2 4.5 %copy-start.4 = (pred[1024,64]{0,1:T(8,128)(4,1)S(1)}, pred[1024,64]{0,1:T(8,128)(4,1)}, u32[]{:S(2)}) copy-start(pred[1024,64]{0,1:T(8,128)(4,1)} %compare_and_fusion) | copy-start | bytes 196612
  113.9 1.7 copy-start.3
  113.9 3.0 %copy-start.2 = (bf16[4,256,3,4,128]{4,1,0,3,2:T(8,128)(2,1)S(1)}, bf16[4,256,3,4,128]{4,1,0,3,2:T(8,128)(2,1)}, u32[]{:S(2)}) copy-start(bf16[4,256,3,4,128]{4,1,0,3,2:T(8,128)(2,1)} %copy-done.1) | copy-start | bytes 9437188
  118.9 3.6 %copy-start.7 = (bf16[1,1,512,2,128]{4,3,2,1,0:T(2,128)(2,1)S(1)}, bf16[1,1,512,2,128]{4,3,2,1,0:T(2,128)(2,1)}, u32[]{:S(2)}) copy-start(bf16[1,1,512,2,128]{4,3,2,1,0:T(2,128)(2,1)} %get-tuple-element.7) | copy-start | bytes 786436
  215.5 14.9 %copy-start.10 = (bf16[256,384]{1,0:T(8,128)(2,1)S(1)}, bf16[256,384]{1,0:T(8,128)(2,1)}, u32[]{:S(2)}) copy-start(bf16[256,384]{1,0:T(8,128)(2,1)} %param.8) | copy-start | bytes 589828
Sparse Core Ops, SparseCore 0:
  9.2 31.5 all-gather.4
  44.4 53.2 all-gather.6
  155.7 41.5 reduce-scatter.1

commit v10 on v8

--- a/solution.py
+++ b/solution.py
@@ -119,35 +119,35 @@
         grouped_queries, own_keys, own_values, allowed, "rhgd,khd->rhgk", "rhgk,khd->hgrd"
     )
     peak, total, weighted = join_parts(cached, fresh)
-    top = lax.pmax(peak, "narrow")
-    hi = lax.reduce_precision(top, exponent_bits=8, mantissa_bits=7)
-    lo = lax.reduce_precision(top - hi, exponent_bits=8, mantissa_bits=7)
-    shift = hi + lo
-    scale = jnp.exp(jnp.minimum(peak - shift, 80.0))
-    first = lax.axis_index("narrow") == 0
+    hi = lax.reduce_precision(peak, exponent_bits=8, mantissa_bits=7)
+    lo = lax.reduce_precision(peak - hi, exponent_bits=8, mantissa_bits=7)
+    scale = jnp.exp(jnp.minimum(peak - (hi + lo), 80.0))
+    lanes = 128
 
-    def kept(a):
-        return jnp.where(first, a, jnp.zeros_like(a)).reshape(every_rows, heads)
+    def slot(total, hi, lo):
+        rows = total.shape[0]
+        flat = lambda a: a.reshape(rows, heads)
+        pad = jnp.zeros((rows, lanes - 3 * heads), jnp.float32)
+        return jnp.concatenate([flat(total), flat(hi), flat(lo), pad], 1)
 
-    lanes = 128
-    extra = jnp.concatenate(
-        [
-            (total * scale).reshape(every_rows, heads),
-            kept(hi),
-            kept(lo),
-            jnp.zeros((every_rows, lanes - 3 * heads), jnp.float32),
-        ],
-        1,
-    )
     scaled = (weighted * heads_major(scale)).reshape(heads, every_rows, head_dim)
-    packed = jnp.concatenate([scaled, extra[None]], 0).astype(jnp.bfloat16)
+    packed = jnp.concatenate([scaled, slot(total * scale, hi, lo)[None]], 0).astype(jnp.bfloat16)
     slots = packed.shape[0]
     packed = (
         packed.reshape(slots, n_wide, n_narrow, own, head_dim)
         .transpose(0, 2, 1, 3, 4)
-        .reshape(slots, every_rows, head_dim)
+        .reshape(slots, n_narrow, block_rows, head_dim)
     )
-    packed = lax.psum_scatter(packed, "narrow", scatter_dimension=1, tiled=True)
+    packed = lax.all_to_all(packed, "narrow", 1, 1).astype(jnp.float32)
+    extra = packed[heads]
+    part_shift = extra[..., heads : 2 * heads] + extra[..., 2 * heads : 3 * heads]
+    top = jnp.max(part_shift, 0)
+    hi = lax.reduce_precision(top, exponent_bits=8, mantissa_bits=7)
+    lo = lax.reduce_precision(top - hi, exponent_bits=8, mantissa_bits=7)
+    part_scale = jnp.exp(jnp.minimum(part_shift - (hi + lo)[None], 80.0))
+    total = jnp.sum(extra[..., :heads] * part_scale, 0)
+    weighted = jnp.sum(packed[:heads] * part_scale.transpose(2, 0, 1)[..., None], 1)
+    packed = jnp.concatenate([weighted, slot(total, hi, lo)[None]], 0).astype(jnp.bfloat16)
     packed = lax.all_to_all(packed.reshape(slots, n_wide, own, head_dim), "wide", 1, 1)
     packed = packed.astype(jnp.float32)
     extra = packed[heads]

time: 238 us -> 256 us (1.076)
  waiting for transfers between devices: 102 us -> 59.3 us
  blocking collectives: 61.7 us -> 85.7 us
  matrix products: 28.1 us -> 44.4 us
  other arithmetic: 15.4 us -> 29.6 us
  local copies, waits for them, and re-layouts: 12.4 us -> 18.1 us
    all_to_all x0 -> x1, blocking collectives: none -> 43.1 us  [per_device(): packed = lax.all_to_all(packed, 'narrow', 1, 1).astype(jnp.float32)]
    reduce_scatter x1 -> x0, waiting for transfers between devices: 41.7 us -> none  [per_device(): packed = lax.psum_scatter(packed, 'narrow', scatter_dimension=1, tiled=True)]
    pmax x1 -> x0, blocking collectives: 16.5 us -> none  [per_device(): top = lax.pmax(peak, 'narrow')]
    dot_general x4, matrix products: 7.44 us -> 20.8 us  [partial_softmax(): jnp.einsum(form_s, grouped_queries, keys, preferred_element_type=jnp.floa...]
    reduce_sum x3, other arithmetic: 7.97 us -> 16.7 us  [partial_softmax(): total = jnp.sum(weights, -1)]
    unnamed x28 -> x26, local copies, waits for them, and re-layouts: 1.6 us -> 6.37 us
    reduce_sum x1 -> x2, other arithmetic: 0.48 us -> 5.1 us  [per_device(): jnp.sum(packed[:heads] * part_scale.transpose(2, 0, 1)[..., None], 1)]
    dot_general x4, matrix products: 17.4 us -> 20.3 us  [partial_softmax(): jnp.einsum(form_o, weights.astype(jnp.bfloat16), values, preferred_elemen...]
  transfers between devices with their start and end apart: 4 -> 3, of which waited for: 3 -> 2; matrix products, arithmetic and copies ran while one was open for 9% -> 5% of each run, Pallas kernels for 0% -> 0%
where the time goes in v10:
time: 256 us; the launch traced here: 255 us
  blocking collectives  85.7 us (33%)
  waiting for transfers between devices  59.3 us (23%)
  matrix products  44.4 us (17%)
  other arithmetic  29.6 us (12%)
  local copies, waits for them, and re-layouts  18.1 us (7%)
  between operations  13.8 us (5%)
  starting transfers between devices  4.36 us (2%)
    all_to_all x1, blocking collectives, per_device(): packed = lax.all_to_all(packed, 'narrow', 1, 1).astype(jnp.float32)  43.1 us
    all_gather x1, waiting for transfers between devices, per_device(): lax.all_gather(part[:, :q_blocks], ('wide', 'narrow'), axis=0, tiled=False)  40.2 us
    dot_general x4, matrix products, partial_softmax(): jnp.einsum(form_s, grouped_queries, keys, preferred_element_type=jnp.floa...  20.8 us
    dot_general x4, matrix products, partial_softmax(): jnp.einsum(form_o, weights.astype(jnp.bfloat16), values, preferred_elemen...  20.3 us
    all_gather x1, waiting for transfers between devices, per_device(): w_cols = lax.all_gather(w_qkv, 'wide', axis=0, tiled=False)  18.4 us
    reduce_sum x3, other arithmetic, partial_softmax(): total = jnp.sum(weights, -1)  16.7 us
    all_gather x1, blocking collectives, per_device(): features = lax.all_gather(tokens, 'narrow', axis=1, tiled=True)  14.8 us
    all_to_all x1, blocking collectives, per_device(): lax.all_to_all(packed.reshape(slots, n_wide, own, head_dim), 'wide', 1, 1)  14.5 us
  transfers between devices with their start and end apart: 3, of which 2 were waited for; matrix products, arithmetic and copies ran while one was open for 5% of the time, Pallas kernels for 0%

profile of v10, /device:TPU:32, one launch (start us, length us, event | category | flops | bytes accessed | tf_op | source)
XLA Modules:
  0.0 255.2 jit_solution(11178427617587871949)
XLA Ops:
  7.3 14.8 %all_gather.18 = bf16[256,1536]{1,0:T(8,128)(2,1)S(1)} all-gather(bf16[256,384]{1,0:T(8,128)(2,1)} %param.8), channel_id=1, replica_groups=mesh['rep'=16,'wide'=4,'narrow'=4] {'narrow'}, dimensions={1}, use_global_device_ids=true | all-gather | bytes 983040 | tf_op jit(solution)/shard_map/all_gather | solution.py:68
  22.4 18.4 %all-gather.5.cloned.1.call-done = bf16[6144,128]{1,0:T(8,128)(2,1)} async-done(((bf16[1536,128]{1,0:T(8,128)(2,1)}), bf16[6144,128]{1,0:T(8,128)(2,1)}) %all-gather.5.cloned.1.call-update) | async-done | bytes 1572880 | tf_op jit(solution)/shard_map/all_gather | solution.py:70
  40.8 2.0 convolution_convert_fusion
  42.8 0.7 copy-done.6
  43.5 0.7 slice.100
  45.4 1.3 fusion.81
  46.7 0.7 compare_and_fusion
  47.5 1.5 fusion.96
  49.0 2.7 %fusion.95 = (bf16[1,4,512,2,128]{4,3,2,1,0:T(2,128)(2,1)S(1)}, bf16[1,4,512,2,128]{4,3,2,1,0:T(2,128)(2,1)S(1)}) fusion(bf16[2,4,512,2,128]{4,3,2,1,0:T(2,128)(2,1)} %param.13), kind=kLoop, calls=%fused_computation.152 | loop fusion | bytes 4194304 | tf_op jit(solution)/shard_map/slice | solution.py:108
  51.7 1.5 slice.104
  53.2 4.3 %all-to-all-start = ((bf16[4,64,128]{2,1,0:T(8,128)(2,1)}), bf16[4,64,128]{2,1,0:T(8,128)(2,1)}, u32[]{:S(2)}, u32[]{:S(2)}) async-start(bf16[4,64,128]{2,1,0:T(8,128)(2,1)} %bitcast.182), calls=%async_computation | async-start | bytes 131072 | tf_op jit(solution)/shard_map/all_to_all | solution.py:83
  57.5 40.2 %all-gather.7.cloned.1.call-done = bf16[4096,3,128]{2,0,1:T(8,128)(2,1)} async-done(((bf16[256,3,128]{2,0,1:T(8,128)(2,1)}), bf16[4096,3,128]{2,0,1:T(8,128)(2,1)}) %all-gather.7.cloned.1.call-update) | async-done | bytes 3145744 | tf_op jit(solution)/shard_map/all_gather | solution.py:76
  97.6 2.2 copy.168
  99.9 1.7 copy-done.2
  102.4 4.9 %fusion.20 = (f32[1024,2,6]{0,2,1:T(8,128)S(1)}, f32[2,64,1024,6]{2,1,3,0:T(8,128)}) fusion(pred[1024,64]{0,1:T(8,128)(4,1)} %compare_and_fusion, bf16[1024,2,6,128]{3,0,2,1:T(8,128)(2,1)} %bitcast.173, bf16[4,64,128]{2,1,0:T(8,128)(2,1)} %all-to-all-done), kind=kOutput, calls=%fused_computation.30 | convolution fusion | flops 203673600 | bytes 6438912 | tf_op jit(solution)/shard_map/rhgd,khd->rhgk/dot_general | solution.py:17
  107.5 7.7 %bitcast_reduce_fusion = (f32[510,2,6]{0,2,1:T(8,128)S(1)}, f32[2,510,6,512]{3,1,2,0:T(8,128)}) fusion(pred[512]{0:T(512)(128)(4,1)S(1)} %get-tuple-element.35, bf16[1,1,512,2,128]{4,3,2,1,0:T(2,128)(2,1)S(1)} %copy-done.9, bf16[1024,2,6,128]{3,0,2,1:T(8,128)(2,1)} %bitcast.174), kind=kOutput, calls=%fused_computation.1 | convolution fusion | flops 811554816 | bytes 14393760 | tf_op jit(solution)/shard_map/qhgd,khd->qhgk/dot_general | solution.py:17
  115.2 7.8 %bitcast_reduce_fusion.1 = (f32[510,2,6]{0,2,1:T(8,128)S(1)}, f32[2,510,6,512]{3,1,2,0:T(8,128)}) fusion(pred[512]{0:T(512)(128)(4,1)S(1)} %get-tuple-element.36, bf16[1,1,512,2,128]{4,3,2,1,0:T(2,128)(2,1)S(1)} %get-tuple-element.9, bf16[1024,2,6,128]{3,0,2,1:T(8,128)(2,1)} %bitcast.175), kind=kOutput, calls=%fused_computation.5 | convolution fusion | flops 811554816 | bytes 14393760 | tf_op jit(solution)/shard_map/qhgd,khd->qhgk/dot_general | solution.py:17
  123.4 2.8 %fusion.21 = f32[1024,2,6]{0,2,1:T(8,128)S(1)} fusion(f32[2,64,1024,6]{2,1,3,0:T(8,128)} %get-tuple-element.28, f32[1024,2,6]{0,2,1:T(8,128)S(1)} %get-tuple-element.27, pred[1024,64]{0,1:T(8,128)(4,1)S(1)} %copy-done.4), kind=kLoop, calls=%fused_computation.31 | loop fusion | flops 3919872 | bytes 3309568 | tf_op jit(solution)/shard_map/reduce_sum | solution.py:23
  126.3 7.1 %fusion.6 = f32[510,2,6]{0,2,1:T(8,128)S(1)} fusion(f32[2,510,6,512]{3,1,2,0:T(8,128)} %get-tuple-element.30, f32[510,2,6]{0,2,1:T(8,128)S(1)} %get-tuple-element.29, pred[512]{0:T(512)(128)(4,1)S(1)} %get-tuple-element.35), kind=kLoop, calls=%fused_computation.12 | loop fusion | flops 15661080 | bytes 12583232 | tf_op jit(solution)/shard_map/reduce_sum | solution.py:23
  133.4 1.1 copy-done.3
  134.5 4.2 %fusion.26 = f32[2,6,510,128]{3,2,1,0:T(8,128)} fusion(f32[2,510,6,512]{3,1,2,0:T(8,128)S(1)} %copy-done.3, f32[510,2,6]{0,2,1:T(8,128)S(1)} %get-tuple-element.29, pred[512]{0:T(512)(128)(4,1)S(1)} %get-tuple-element.35, bf16[1,1,512,2,128]{4,3,2,1,0:T(2,128)(2,1)S(1)} %copy-done.8), kind=kOutput, calls=%fused_computation.36 | convolution fusion | flops 817827840 | bytes 15954336 | tf_op jit(solution)/shard_map/qhgk,khd->hgqd/dot_general | solution.py:24
  138.7 6.8 %fusion.4 = f32[510,2,6]{0,2,1:T(8,128)S(1)} fusion(f32[2,510,6,512]{3,1,2,0:T(8,128)} %get-tuple-element.32, f32[510,2,6]{0,2,1:T(8,128)S(1)} %get-tuple-element.31, pred[512]{0:T(512)(128)(4,1)S(1)} %get-tuple-element.36), kind=kLoop, calls=%fused_computation.10 | loop fusion | flops 15661080 | bytes 12583232 | tf_op jit(solution)/shard_map/reduce_sum | solution.py:23
  145.5 7.2 %fusion.23 = f32[2,6,510,128]{3,2,1,0:T(8,128)} fusion(f32[2,510,6,512]{3,1,2,0:T(8,128)} %get-tuple-element.32, f32[510,2,6]{0,2,1:T(8,128)S(1)} %get-tuple-element.31, pred[512]{0:T(512)(128)(4,1)S(1)} %get-tuple-element.36, bf16[1,1,512,2,128]{4,3,2,1,0:T(2,128)(2,1)S(1)} %copy-done.7), kind=kOutput, calls=%fused_computation.35 | convolution fusion | flops 817827840 | bytes 15954336 | tf_op jit(solution)/shard_map/qhgk,khd->hgqd/dot_general | solution.py:24
  154.0 8.7 %fusion.11 = bf16[2,6,1024,128]{3,2,1,0:T(8,128)(2,1)S(1)} fusion(f32[2,6,4,128]{3,2,1,0:T(4,128)S(1)} %bitcast.183, f32[2,6,510,128]{3,2,1,0:T(8,128)} %fusion.26, f32[2,6,510,128]{3,2,1,0:T(8,128)} %fusion.23, f32[2,6,1024]{2,1,0:T(8,128)S(1)} %get-tuple-element.21, f32[2,6,1024]{2,1,0:T(8,128)S(1)} %get-tuple-element.22, ...), kind=kOutput, calls=%fused_computation.19 | convolution fusion | flops 216268800 | bytes 12902400 | tf_op jit(solution)/shard_map/rhgk,khd->hgrd/dot_general | solution.py:24
  162.6 2.1 maximum_maximum_fusion
  165.1 43.1 %all_to_all.15 = bf16[13,4,256,128]{3,2,0,1:T(8,128)(2,1)S(1)} all-to-all(bf16[13,4,256,128]{3,2,0,1:T(8,128)(2,1)S(1)} %copy.190), channel_id=1, replica_groups=mesh['rep'=16,'wide'=4,'narrow'=4] {'narrow'}, dimensions={1} | all-to-all | bytes 6815744 | tf_op jit(solution)/shard_map/all_to_all | solution.py:141
  208.2 0.8 convert_element_type.49
  209.0 2.8 %copy-done.1 = f32[13,4,256,128]{3,2,0,1:T(8,128)} copy-done((f32[13,4,256,128]{3,2,0,1:T(8,128)}, f32[13,4,256,128]{3,2,0,1:T(8,128)S(1)}, u32[]{:S(2)}) %copy-start.1) | copy-done | bytes 6815768
  212.9 4.6 %fusion.8 = bf16[12,256,128]{2,1,0:T(8,128)(2,1)S(1)} fusion(f32[13,4,256,128]{3,2,0,1:T(8,128)} %copy-done.1, f32[12,4,256]{2,0,1:T(8,128)S(1)} %copy.194), kind=kLoop, calls=%fused_computation.15 | loop fusion | flops 2752512 | bytes 7127040 | tf_op jit(solution)/shard_map/reduce_sum | solution.py:149
  217.9 14.5 %all_to_all.16 = bf16[13,4,64,128]{3,2,0,1:T(8,128)(2,1)S(1)} all-to-all(bf16[13,4,64,128]{3,2,0,1:T(8,128)(2,1)S(1)} %copy.195), channel_id=1, replica_groups=mesh['rep'=16,'wide'=4,'narrow'=4] {'wide'}, dimensions={1} | all-to-all | bytes 1703936 | tf_op jit(solution)/shard_map/all_to_all | solution.py:151
  233.8 13.3 %all_gather.23 = bf16[256,1536]{1,0:T(8,128)(2,1)S(1)} all-gather(bf16[64,1536]{1,0:T(8,128)(2,1)S(1)} %copy_bitcast_fusion.12), channel_id=1, replica_groups=mesh['rep'=16,'wide'=4,'narrow'=4] {'narrow'}, dimensions={0}, use_global_device_ids=true | all-gather | bytes 983040 | tf_op jit(solution)/shard_map/all_gather | solution.py:160
  247.1 1.3 fusion.43
  (81 shorter events, 8.0 us)
Async XLA Ops:
  6.5 240.6 %copy-start = (bf16[1536,384]{1,0:T(8,128)(2,1)S(1)}, bf16[1536,384]{1,0:T(8,128)(2,1)}, u32[]{:S(2)}) copy-start(bf16[1536,384]{1,0:T(8,128)(2,1)} %param.11) | copy-start | bytes 3538948
  6.5 37.7 %copy-start.11 = (s32[2]{0:T(128)S(1)}, s32[2]{0:T(128)}, u32[]{:S(2)}) copy-start(s32[2]{0:T(128)} %param.14) | copy-start | bytes 28
  6.5 37.9 %copy-start.12 = (s32[4]{0:T(128)S(1)}, s32[4]{0:T(128)}, u32[]{:S(2)}) copy-start(s32[4]{0:T(128)} %param.15) | copy-start | bytes 52
  6.5 40.9 %copy-start.5 = (bf16[2,2,512,2,128]{4,3,2,1,0:T(2,128)(2,1)S(1)}, bf16[2,2,512,2,128]{4,3,2,1,0:T(2,128)(2,1)}, u32[]{:S(2)}) copy-start(bf16[2,2,512,2,128]{4,3,2,1,0:T(2,128)(2,1)} %param.12) | copy-start | bytes 3145732
  6.5 34.2 %all-gather.5.cloned.1.call-start = ((), (), s32[]{:S(2)}) async-start(), calls=%async_computation.3 | async-start | bytes 1966080 | tf_op jit(solution)/shard_map/all_gather | solution.py:70
  7.3 90.4 %all-gather.7.cloned.1.call-start = ((), (), s32[]{:S(2)}) async-start(), calls=%async_computation.4 | async-start | bytes 3342336 | tf_op jit(solution)/shard_map/all_gather | solution.py:76
  42.8 0.7 copy-start.6
  53.2 49.3 %all-to-all-start = ((bf16[4,64,128]{2,1,0:T(8,128)(2,1)}), bf16[4,64,128]{2,1,0:T(8,128)(2,1)}, u32[]{:S(2)}, u32[]{:S(2)}) async-start(bf16[4,64,128]{2,1,0:T(8,128)(2,1)} %bitcast.182), calls=%async_computation | async-start | bytes 131072 | tf_op jit(solution)/shard_map/all_to_all | solution.py:83
  99.9 1.8 copy-start.2
  102.4 5.0 %copy-start.9 = (bf16[1,1,512,2,128]{4,3,2,1,0:T(2,128)(2,1)S(1)}, bf16[1,1,512,2,128]{4,3,2,1,0:T(2,128)(2,1)}, u32[]{:S(2)}) copy-start(bf16[1,1,512,2,128]{4,3,2,1,0:T(2,128)(2,1)} %get-tuple-element.8) | copy-start | bytes 786436
  115.2 8.2 %copy-start.4 = (pred[1024,64]{0,1:T(8,128)(4,1)S(1)}, pred[1024,64]{0,1:T(8,128)(4,1)}, u32[]{:S(2)}) copy-start(pred[1024,64]{0,1:T(8,128)(4,1)} %compare_and_fusion) | copy-start | bytes 196612
  123.4 10.0 %copy-start.8 = (bf16[1,1,512,2,128]{4,3,2,1,0:T(2,128)(2,1)S(1)}, bf16[1,1,512,2,128]{4,3,2,1,0:T(2,128)(2,1)}, u32[]{:S(2)}) copy-start(bf16[1,1,512,2,128]{4,3,2,1,0:T(2,128)(2,1)} %get-tuple-element.10) | copy-start | bytes 786436
  126.3 8.2 %copy-start.3 = (f32[2,510,6,512]{3,1,2,0:T(8,128)S(1)}, f32[2,510,6,512]{3,1,2,0:T(8,128)}, u32[]{:S(2)}) copy-start(f32[2,510,6,512]{3,1,2,0:T(8,128)} %get-tuple-element.30) | copy-start | bytes 37601284
  138.7 6.8 %copy-start.7 = (bf16[1,1,512,2,128]{4,3,2,1,0:T(2,128)(2,1)S(1)}, bf16[1,1,512,2,128]{4,3,2,1,0:T(2,128)(2,1)}, u32[]{:S(2)}) copy-start(bf16[1,1,512,2,128]{4,3,2,1,0:T(2,128)(2,1)} %get-tuple-element.7) | copy-start | bytes 786436
  209.0 2.8 %copy-start.1 = (f32[13,4,256,128]{3,2,0,1:T(8,128)}, f32[13,4,256,128]{3,2,0,1:T(8,128)S(1)}, u32[]{:S(2)}) copy-start(f32[13,4,256,128]{3,2,0,1:T(8,128)S(1)} %convert_element_type.49) | copy-start | bytes 20447236
  232.5 14.7 %copy-start.10 = (bf16[256,384]{1,0:T(8,128)(2,1)S(1)}, bf16[256,384]{1,0:T(8,128)(2,1)}, u32[]{:S(2)}) copy-start(bf16[256,384]{1,0:T(8,128)(2,1)} %param.8) | copy-start | bytes 589828
Sparse Core Ops, SparseCore 0:
  9.2 31.5 all-gather.4
  44.4 53.2 all-gather.6
